TPU v7x, 256 devices: a whole 4x4x8 slice. The times are simulated.
256 devices in a mesh: chan: 64 (over z, y_hi, x), seg: 4 (over y_lo, core).
Axes of the slice: x: 4, y: 4 (y_hi: 2, y_lo: 2; y = y_hi * 2 + y_lo), z: 8, core: 2. Of those that a mesh axis runs over, the one named last changes fastest.
Arguments:
- spectra: bfloat16 [32, 128, 2, 8192], P(None, 'seg', None, 'chan'), may hold values from -6 to 6
- plan: int32 [4, 64], replicated, may hold values from 0 to 63, as said below
- assignment: int32 [8192], P('chan'), may hold values from 0 to 8191, as said below
Outputs:
- cross_spectra: float32 [4, 32, 2, 8192, 128], P(None, 'seg', None, 'chan')
Inputs may be any that keep to these rules, and one draw needn't show every extreme that they name: Each row is a pairing of the blocks: plan[r, plan[r, b]] = b and plan[r, b] != b; no two blocks are paired in two different rounds. `assignment`: entries b * 128 to (b + 1) * 128 - 1 are a permutation of that same range of channels.
All inputs are finite; a program needn't handle non-finite values.
Results may differ from a plain program's by a relative error of at most 0.0003.
Values may be sent and summed in bfloat16 or wider, within the bound.
No kernel may reach another device: no remote copies, remote signals or barrier semaphores. Data moves between devices by JAX's collectives and lax.ppermute only.
A program may use at most 128 MiB of HBM per device.

v0:
```python
import math

import jax
import jax.numpy as jnp
from jax import lax
from jax.sharding import PartitionSpec as P


def cross_block(own_rows, other_rows, chan_width):
    product = jnp.einsum("fwa,fwb->fab", own_rows, other_rows, preferred_element_type=jnp.float32)
    real_part = product[:, :chan_width, :chan_width] + product[:, chan_width:, chan_width:]
    imag_part = product[:, chan_width:, :chan_width] - product[:, :chan_width, chan_width:]
    return jnp.stack([real_part, imag_part], axis=1)


def on_device(spectra, plan, assignment):
    chan_width = spectra.shape[3]
    scale = 1.0 / math.sqrt(spectra.shape[1] * lax.axis_size("seg"))
    local_slots = assignment - lax.axis_index("chan") * chan_width
    ordered = jnp.take(spectra, local_slots, axis=3)
    bin_count = ordered.shape[0]
    win_count = ordered.shape[1]
    group_count = lax.axis_size("chan")
    piece_rows = bin_count * win_count // group_count
    own_rows = ordered.reshape(bin_count, win_count, 2 * chan_width)
    pieces = ordered.reshape(group_count, piece_rows, 2 * chan_width)
    held = lax.all_to_all(pieces, "chan", split_axis=0, concat_axis=0, tiled=True)
    results = []
    for round_index in range(plan.shape[0]):
        outgoing = jnp.take(held, plan[round_index], axis=0)
        arrived = lax.all_to_all(outgoing, "chan", split_axis=0, concat_axis=0, tiled=True)
        other_rows = arrived.reshape(bin_count, win_count, 2 * chan_width)
        block_result = cross_block(own_rows, other_rows, chan_width) * scale
        results.append(block_result)
    stacked = jnp.stack(results)
    return lax.psum_scatter(stacked, "seg", scatter_dimension=1, tiled=True)


def solution(mesh):
    in_specs = (P(None, "seg", None, "chan"), P(), P("chan"))
    out_specs = P(None, "seg", None, "chan", None)
    return jax.shard_map(
        on_device, mesh=mesh, in_specs=in_specs, out_specs=out_specs, check_vma=False
    )
```

profile of v0, /device:TPU:2, one launch (start us, length us, event | category | flops | bytes accessed | tf_op | source)
XLA Modules:
  0.0 335.1 jit_solution(12101090352674338851)
XLA Ops:
  6.5 0.7 compare_and_fusion.4
  7.2 0.0 copy-start.5
  7.2 3.5 %copy.11 = bf16[32,32,2,128]{1,0,2,3:T(8,128)(2,1)S(1)} copy(bf16[32,32,2,128]{3,2,1,0:T(2,128)(2,1)} %param.5) | data formatting | bytes 1048576 | tf_op args[0]
  10.7 2.1 gather_fusion
  12.8 3.5 %copy.12 = bf16[32,32,2,128]{3,2,1,0:T(2,128)(2,1)S(1)} copy(bf16[32,32,2,128]{1,0,2,3:T(8,128)(2,1)} %bitcast.58) | data formatting | bytes 1048576 | tf_op jit(solution)/shard_map/jit(_take)/gather | solution.py:20
  16.3 0.3 gather.13
  16.7 0.8 broadcast_select_fusion.4
  17.5 14.6 %all-to-all-start = ((bf16[64,16,256]{2,1,0:T(8,128)(2,1)}), bf16[64,16,256]{2,1,0:T(8,128)(2,1)S(1)}, u32[]{:S(2)}, u32[]{:S(2)}) async-start(bf16[64,16,256]{2,1,0:T(8,128)(2,1)} %broadcast_select_fusion.4), calls=%async_computation | async-start | bytes 1048576 | tf_op jit(solution)/shard_map/all_to_all | solution.py:27
  32.2 0.0 copy-done.5
  32.2 17.6 %all-to-all-done = bf16[64,16,256]{2,1,0:T(8,128)(2,1)S(1)} async-done(((bf16[64,16,256]{2,1,0:T(8,128)(2,1)}), bf16[64,16,256]{2,1,0:T(8,128)(2,1)S(1)}, u32[]{:S(2)}, u32[]{:S(2)}) %all-to-all-start) | async-done | bytes 524320 | tf_op jit(solution)/shard_map/all_to_all | solution.py:27
  49.9 0.6 gather_fusion.2
  50.5 0.9 broadcast_select_fusion.2
  51.4 7.3 %all-to-all-start.2 = ((bf16[64,16,256]{2,1,0:T(8,128)(2,1)}), bf16[64,16,256]{2,1,0:T(8,128)(2,1)S(1)}, u32[]{:S(2)}, u32[]{:S(2)}) async-start(bf16[64,16,256]{2,1,0:T(8,128)(2,1)} %broadcast_select_fusion.2), calls=%async_computation.2 | async-start | bytes 1048576 | tf_op jit(solution)/shard_map/all_to_all | solution.py:31
  58.8 0.6 gather_fusion.1
  59.4 0.9 broadcast_select_fusion.3
  60.3 15.3 %all-to-all-done.2 = bf16[64,16,256]{2,1,0:T(8,128)(2,1)S(1)} async-done(((bf16[64,16,256]{2,1,0:T(8,128)(2,1)}), bf16[64,16,256]{2,1,0:T(8,128)(2,1)S(1)}, u32[]{:S(2)}, u32[]{:S(2)}) %all-to-all-start.2) | async-done | bytes 524320 | tf_op jit(solution)/shard_map/all_to_all | solution.py:31
  75.7 7.3 %all-to-all-start.1 = ((bf16[64,16,256]{2,1,0:T(8,128)(2,1)}), bf16[64,16,256]{2,1,0:T(8,128)(2,1)S(1)}, u32[]{:S(2)}, u32[]{:S(2)}) async-start(bf16[64,16,256]{2,1,0:T(8,128)(2,1)} %broadcast_select_fusion.3), calls=%async_computation.1 | async-start | bytes 1048576 | tf_op jit(solution)/shard_map/all_to_all | solution.py:31
  82.9 0.3 gather.12
  83.3 0.6 gather_fusion.4
  83.9 0.6 gather_fusion.3
  84.5 0.9 broadcast_select_fusion
  85.4 0.9 broadcast_select_fusion.1
  86.4 13.2 %all-to-all-done.1 = bf16[64,16,256]{2,1,0:T(8,128)(2,1)S(1)} async-done(((bf16[64,16,256]{2,1,0:T(8,128)(2,1)}), bf16[64,16,256]{2,1,0:T(8,128)(2,1)S(1)}, u32[]{:S(2)}, u32[]{:S(2)}) %all-to-all-start.1) | async-done | bytes 524320 | tf_op jit(solution)/shard_map/all_to_all | solution.py:31
  99.5 7.4 %all-to-all-start.3 = ((bf16[64,16,256]{2,1,0:T(8,128)(2,1)}), bf16[64,16,256]{2,1,0:T(8,128)(2,1)}, u32[]{:S(2)}, u32[]{:S(2)}) async-start(bf16[64,16,256]{2,1,0:T(8,128)(2,1)} %broadcast_select_fusion.1), calls=%async_computation.3 | async-start | bytes 1048576 | tf_op jit(solution)/shard_map/all_to_all | solution.py:31
  107.0 1.3 fusion.11
  108.3 2.0 fusion.7
  110.2 4.5 %fusion.10 = f32[32,256,256]{2,1,0:T(8,128)} fusion(bf16[32,32,256]{2,1,0:T(8,128)(2,1)S(1)} %bitcast.59, bf16[32,32,256]{2,1,0:T(8,128)(2,1)S(1)} %gather.12, pred[256]{0:T(512)(128)(4,1)S(1)} %broadcast_bitcast_fusion), kind=kOutput, calls=%fused_computation.35 | convolution fusion | flops 134479872 | bytes 9437440 | tf_op jit(solution)/shard_map/fwa,fwb->fab/dot_general | solution.py:10
  114.8 8.7 %all-to-all-done.3 = bf16[64,16,256]{2,1,0:T(8,128)(2,1)} async-done(((bf16[64,16,256]{2,1,0:T(8,128)(2,1)}), bf16[64,16,256]{2,1,0:T(8,128)(2,1)}, u32[]{:S(2)}, u32[]{:S(2)}) %all-to-all-start.3) | async-done | bytes 524320 | tf_op jit(solution)/shard_map/all_to_all | solution.py:31
  123.5 7.2 %all-to-all-start.4 = ((bf16[64,16,256]{2,1,0:T(8,128)(2,1)}), bf16[64,16,256]{2,1,0:T(8,128)(2,1)S(1)}, u32[]{:S(2)}, u32[]{:S(2)}) async-start(bf16[64,16,256]{2,1,0:T(8,128)(2,1)} %broadcast_select_fusion), calls=%async_computation.4 | async-start | bytes 1048576 | tf_op jit(solution)/shard_map/all_to_all | solution.py:31
  130.7 0.2 reduce-scatter.5.cloned.1.call-start
  131.0 6.7 %fusion.5 = (f32[1,32,1,128,128]{4,3,1,2,0:T(8,128)}, f32[1,32,1,128,128]{4,3,1,2,0:T(8,128)}) fusion(f32[32,256,256]{2,1,0:T(8,128)} %fusion.10), kind=kLoop, calls=%fused_computation.22 | loop fusion | flops 1048576 | bytes 12582912 | tf_op jit(solution)/shard_map/stack | solution.py:13
  137.7 2.3 fusion.9
  140.0 2.6 fusion.3
  142.6 4.7 %all-to-all-done.4 = bf16[64,16,256]{2,1,0:T(8,128)(2,1)S(1)} async-done(((bf16[64,16,256]{2,1,0:T(8,128)(2,1)}), bf16[64,16,256]{2,1,0:T(8,128)(2,1)S(1)}, u32[]{:S(2)}, u32[]{:S(2)}) %all-to-all-start.4) | async-done | bytes 524320 | tf_op jit(solution)/shard_map/all_to_all | solution.py:31
  147.3 1.3 fusion.8
  148.6 0.0 copy-start
  148.7 0.6 fusion.1
  149.3 1.0 copy-done
  150.2 0.6 copy-done.3
  150.8 0.6 copy-done.4
  151.5 3.1 maximum_multiply_fusion
  154.6 4.3 %maximum_multiply_fusion.2 = (f32[1,32,2,128,128]{4,3,1,2,0:T(8,128)}, f32[1,32,2,128,128]{4,3,1,2,0:T(8,128)}) fusion(f32[1,32,1,128,128]{4,3,1,2,0:T(8,128)S(1)} %copy-done.2, f32[1,32,1,128,128]{4,3,1,2,0:T(8,128)S(1)} %copy-done.1, f32[1,32,1,128,128]{4,3,1,2,0:T(8,128)S(1)} %get-tuple-element.23, f32[1,32,1,128,128]{4,3,1,2,0:T(8,128)S(1)} %get-tuple-element.22), kind=kLoop, calls=%fused_computation.9 | loop fusion | flops 4194304 | bytes 16777216 | tf_op jit(solution)/shard_map/mul | solution.py:33
  158.9 5.6 %pad_maximum_fusion = f32[4,32,2,128,128]{4,3,1,2,0:T(8,128)S(1)} fusion(f32[1,32,2,128,128]{4,3,1,2,0:T(8,128)} %get-tuple-element.33, f32[1,32,2,128,128]{4,3,1,2,0:T(8,128)} %get-tuple-element.32, f32[1,32,2,128,128]{4,3,1,2,0:T(8,128)} %get-tuple-element.31, f32[1,32,2,128,128]{4,3,1,2,0:T(8,128)S(1)} %get-tuple-element.30), kind=kLoop, calls=%fused_computation.6 | loop fusion | flops 12582912 | bytes 33554432 | tf_op jit(solution)/shard_map/stack | solution.py:35
  164.5 1.6 copy.15
  166.1 11.7 %copy.22 = f32[4,8,1024,128]{3,1,2,0:T(8,128)} copy(f32[4,8,1024,128]{3,2,1,0:T(8,128)S(1)} %bitcast.56) | data formatting | bytes 33554432
  177.9 0.0 reduce-scatter.5.cloned.1.call-update
  177.9 145.5 %reduce-scatter.5.cloned.1.call-done = f32[8,131072]{1,0:T(8,128)} async-done(((f32[32,131072]{1,0:T(8,128)}), f32[8,131072]{1,0:T(8,128)}) %reduce-scatter.5.cloned.1.call-update) | async-done | bytes 4194320
  323.3 4.9 %copy.14 = f32[4,8,2,128,128]{4,3,2,1,0:T(8,128)} copy(f32[4,8,2,128,128]{4,1,3,2,0:T(8,128)} %bitcast.57) | data formatting | bytes 8388608 | tf_op jit(solution)/shard_map/reduce_scatter | solution.py:36
  (13 shorter events, 0.1 us)
Async XLA Ops:
  7.2 25.0 %copy-start.5 = (s32[4,64]{1,0:T(4,128)S(1)}, s32[4,64]{1,0:T(4,128)}, u32[]{:S(2)}) copy-start(s32[4,64]{1,0:T(4,128)} %param.6) | copy-start | bytes 3076
  17.5 32.3 %all-to-all-start = ((bf16[64,16,256]{2,1,0:T(8,128)(2,1)}), bf16[64,16,256]{2,1,0:T(8,128)(2,1)S(1)}, u32[]{:S(2)}, u32[]{:S(2)}) async-start(bf16[64,16,256]{2,1,0:T(8,128)(2,1)} %broadcast_select_fusion.4), calls=%async_computation | async-start | bytes 1048576 | tf_op jit(solution)/shard_map/all_to_all | solution.py:27
  51.4 24.3 %all-to-all-start.2 = ((bf16[64,16,256]{2,1,0:T(8,128)(2,1)}), bf16[64,16,256]{2,1,0:T(8,128)(2,1)S(1)}, u32[]{:S(2)}, u32[]{:S(2)}) async-start(bf16[64,16,256]{2,1,0:T(8,128)(2,1)} %broadcast_select_fusion.2), calls=%async_computation.2 | async-start | bytes 1048576 | tf_op jit(solution)/shard_map/all_to_all | solution.py:31
  75.7 23.9 %all-to-all-start.1 = ((bf16[64,16,256]{2,1,0:T(8,128)(2,1)}), bf16[64,16,256]{2,1,0:T(8,128)(2,1)S(1)}, u32[]{:S(2)}, u32[]{:S(2)}) async-start(bf16[64,16,256]{2,1,0:T(8,128)(2,1)} %broadcast_select_fusion.3), calls=%async_computation.1 | async-start | bytes 1048576 | tf_op jit(solution)/shard_map/all_to_all | solution.py:31
  99.5 23.9 %all-to-all-start.3 = ((bf16[64,16,256]{2,1,0:T(8,128)(2,1)}), bf16[64,16,256]{2,1,0:T(8,128)(2,1)}, u32[]{:S(2)}, u32[]{:S(2)}) async-start(bf16[64,16,256]{2,1,0:T(8,128)(2,1)} %broadcast_select_fusion.1), calls=%async_computation.3 | async-start | bytes 1048576 | tf_op jit(solution)/shard_map/all_to_all | solution.py:31
  123.5 23.8 %all-to-all-start.4 = ((bf16[64,16,256]{2,1,0:T(8,128)(2,1)}), bf16[64,16,256]{2,1,0:T(8,128)(2,1)S(1)}, u32[]{:S(2)}, u32[]{:S(2)}) async-start(bf16[64,16,256]{2,1,0:T(8,128)(2,1)} %broadcast_select_fusion), calls=%async_computation.4 | async-start | bytes 1048576 | tf_op jit(solution)/shard_map/all_to_all | solution.py:31
  130.7 192.6 %reduce-scatter.5.cloned.1.call-start = ((), (), s32[]{:S(2)}) async-start(), calls=%async_computation.6 | async-start | bytes 20971520
  148.6 1.6 copy-start
  148.6 2.2 copy-start.3
  148.6 2.8 copy-start.4
  151.5 3.1 copy-start.1
  151.5 3.1 copy-start.2
Sparse Core Ops, SparseCore 0:
  178.0 145.3 reduce-scatter.4
where the time goes:
time: 337 us; the launch traced here: 335 us
  waiting for transfers between devices  205 us (61%)
  starting transfers between devices  44.1 us (13%)
  local copies, waits for them, and re-layouts  32.7 us (10%)
  other arithmetic  30.2 us (9%)
  between operations  13.6 us (4%)
  matrix products  9.46 us (3%)
    unnamed x2, waiting for transfers between devices  145 us
    all_to_all x4, waiting for transfers between devices, on_device(): lax.all_to_all(outgoing, 'chan', split_axis=0, concat_axis=0, tiled=True)  41.9 us
    all_to_all x4, starting transfers between devices, on_device(): lax.all_to_all(outgoing, 'chan', split_axis=0, concat_axis=0, tiled=True)  29.3 us
    unnamed x15, local copies, waits for them, and re-layouts  19 us
    all_to_all x1, waiting for transfers between devices, on_device(): lax.all_to_all(pieces, 'chan', split_axis=0, concat_axis=0, tiled=True)  17.6 us
    all_to_all x1, starting transfers between devices, on_device(): lax.all_to_all(pieces, 'chan', split_axis=0, concat_axis=0, tiled=True)  14.6 us
    another operation x4, other arithmetic, cross_block(): return jnp.stack([real_part, imag_part], axis=1)  11.9 us
    dot_general x4, matrix products, cross_block(): jnp.einsum('fwa,fwb->fab', own_rows, other_rows, preferred_element_type=j...  9.46 us
  transfers between devices with their start and end apart: 6, of which 6 were waited for; matrix products, arithmetic and copies ran while one was open for 7% of the time, Pallas kernels for 0%

commit v1 on v0

v1 whole, which is shorter than its diff:
```python
import math

import jax
import jax.numpy as jnp
from jax import lax
from jax.sharding import PartitionSpec as P


def cross_block(own_rows, other_rows, chan_width):
    real_lhs = own_rows
    imag_lhs = jnp.stack([own_rows[:, :, 1], -own_rows[:, :, 0]], axis=2)
    lhs = jnp.stack([real_lhs, imag_lhs], axis=3)
    return jnp.einsum("fwkci,fwkj->fcij", lhs, other_rows, preferred_element_type=jnp.float32)


def on_device(spectra, plan, assignment):
    bin_count, win_local, _, chan_width = spectra.shape
    seg_count = lax.axis_size("seg")
    group_count = lax.axis_size("chan")
    win_count = win_local * seg_count
    scale = 1.0 / math.sqrt(win_count)
    local_slots = assignment - lax.axis_index("chan") * chan_width
    ordered = jnp.take(spectra, local_slots, axis=3)
    own_rows = lax.all_to_all(ordered, "seg", split_axis=0, concat_axis=1, tiled=True)
    my_bins = own_rows.shape[0]
    piece_rows = my_bins * win_count // group_count
    pieces = own_rows.reshape(group_count, piece_rows, 2 * chan_width)
    held = lax.all_to_all(pieces, "chan", split_axis=0, concat_axis=0, tiled=True)
    round_count = plan.shape[0]
    outgoing = jnp.take(held, plan.T, axis=0)
    arrived = lax.all_to_all(outgoing, "chan", split_axis=0, concat_axis=0, tiled=True)
    results = []
    for round_index in range(round_count):
        other_rows = arrived[:, round_index].reshape(my_bins, win_count, 2, chan_width)
        results.append(cross_block(own_rows, other_rows, chan_width) * scale)
    return jnp.stack(results)


def solution(mesh):
    in_specs = (P(None, "seg", None, "chan"), P(), P("chan"))
    out_specs = P(None, "seg", None, "chan", None)
    return jax.shard_map(
        on_device, mesh=mesh, in_specs=in_specs, out_specs=out_specs, check_vma=False
    )
```

time: 337 us -> 131 us (0.39)
  waiting for transfers between devices: 205 us -> 64.4 us
  other arithmetic: 30.2 us -> 7.26 us
  starting transfers between devices: 44.1 us -> 21.8 us
  local copies, waits for them, and re-layouts: 32.7 us -> 19 us
  between operations: 13.6 us -> 0.21 us
  blocking collectives: 0 us -> 11.5 us
    unnamed x2 -> x0, waiting for transfers between devices: 145 us -> none
    all_to_all x4 -> x1, starting transfers between devices: 29.3 us -> 7.44 us  [on_device(): lax.all_to_all(outgoing, 'chan', split_axis=0, concat_axis=0, tiled=True)]
    unnamed x15 -> x19, local copies, waits for them, and re-layouts: 19 us -> 3.86 us
    another operation x5 -> x2, other arithmetic: 17.5 us -> 3.13 us  [the longest x1 2.29 us: on_device(): return jnp.stack(results)]
    all_to_all x0 -> x1, blocking collectives: none -> 11.5 us  [on_device(): lax.all_to_all(ordered, 'seg', split_axis=0, concat_axis=1, tiled=True)]
    mul x2 -> x0, other arithmetic: 7.42 us -> none  [on_device(): block_result = cross_block(own_rows, other_rows, chan_width) * scale]
    another operation x0 -> x5, local copies, waits for them, and re-layouts: none -> 6.94 us  [the longest x4 5.92 us: on_device(): arrived[:, round_index].reshape(my_bins, win_count, 2, chan_width)]
    all_to_all x4 -> x1, waiting for transfers between devices: 41.9 us -> 47.6 us  [on_device(): lax.all_to_all(outgoing, 'chan', split_axis=0, concat_axis=0, tiled=True)]
  transfers between devices with their start and end apart: 6 -> 2, of which waited for: 6 -> 2; matrix products, arithmetic and copies ran while one was open for 7% -> 2% of each run, Pallas kernels for 0% -> 0%
where the time goes in v1:
time: 131 us
  waiting for transfers between devices  64.4 us (49%)
  starting transfers between devices  21.8 us (17%)
  local copies, waits for them, and re-layouts  19 us (15%)
  blocking collectives  11.5 us (9%)
  other arithmetic  7.26 us (6%)
  matrix products  6.52 us (5%)
    all_to_all x1, waiting for transfers between devices, on_device(): lax.all_to_all(outgoing, 'chan', split_axis=0, concat_axis=0, tiled=True)  47.6 us
    all_to_all x1, waiting for transfers between devices, on_device(): lax.all_to_all(pieces, 'chan', split_axis=0, concat_axis=0, tiled=True)  16.9 us
    all_to_all x1, starting transfers between devices, on_device(): lax.all_to_all(pieces, 'chan', split_axis=0, concat_axis=0, tiled=True)  14.4 us
    all_to_all x1, blocking collectives, on_device(): lax.all_to_all(ordered, 'seg', split_axis=0, concat_axis=1, tiled=True)  11.5 us
    all_to_all x1, starting transfers between devices, on_device(): lax.all_to_all(outgoing, 'chan', split_axis=0, concat_axis=0, tiled=True)  7.44 us
    dot_general x4, matrix products, cross_block(): jnp.einsum('fwkci,fwkj->fcij', lhs, other_rows, preferred_element_type=jn...  6.52 us
    another operation x4, local copies, waits for them, and re-layouts, on_device(): arrived[:, round_index].reshape(my_bins, win_count, 2, chan_width)  5.92 us
    unnamed x19, local copies, waits for them, and re-layouts  3.86 us
  transfers between devices with their start and end apart: 2, of which 2 were waited for; matrix products, arithmetic and copies ran while one was open for 2% of the time, Pallas kernels for 0%

profile of v1, /device:TPU:2, one launch (start us, length us, event | category | flops | bytes accessed | tf_op | source)
XLA Modules:
  0.0 130.8 jit_solution(9304834242603706841)
XLA Ops:
  0.0 0.7 compare_and_fusion.1
  0.7 3.5 %copy.30 = bf16[32,32,2,128]{1,0,2,3:T(8,128)(2,1)S(1)} copy(bf16[32,32,2,128]{3,2,1,0:T(2,128)(2,1)} %param.3) | data formatting | bytes 1048576 | tf_op args[0]
  4.1 2.1 %gather_fusion = bf16[128,32,32,2]{2,1,3,0:T(8,128)(2,1)} fusion(bf16[32,32,2,128]{1,0,2,3:T(8,128)(2,1)S(1)} %copy.30, s32[1024]{0:T(1024)S(1)} %pad_clamp_fusion.1), kind=kCustom, calls=%fused_computation | custom fusion | bytes 1049088 | tf_op jit(solution)/shard_map/jit(_take)/gather | solution.py:23
  6.3 1.9 %select_bitcast_fusion = bf16[32,32,2,128]{1,0,2,3:T(8,128)(2,1)S(1)} fusion(bf16[128,32,32,2]{2,1,3,0:T(8,128)(2,1)} %gather_fusion, pred[128]{0:T(512)(128)(4,1)S(1)} %get-tuple-element.5), kind=kLoop, calls=%fused_computation.3 | loop fusion | flops 262144 | bytes 1048704 | tf_op jit(solution)/shard_map/jit(_take)/select_n | solution.py:23
  8.1 2.1 %copy.31 = bf16[32,32,2,128]{3,1,2,0:T(8,128)(2,1)S(1)} copy(bf16[32,32,2,128]{1,0,2,3:T(8,128)(2,1)S(1)} %select_bitcast_fusion) | data formatting | bytes 1048576 | tf_op jit(solution)/shard_map/jit(_take)/select_n | solution.py:23
  10.2 0.0 copy-start.7
  10.2 11.5 %all_to_all.28 = bf16[32,32,2,128]{3,1,2,0:T(8,128)(2,1)S(1)} all-to-all(bf16[32,32,2,128]{3,1,2,0:T(8,128)(2,1)S(1)} %copy.31), channel_id=1, replica_groups=mesh['chan'=64,'seg'=4] {'seg'}, dimensions={0} | all-to-all | bytes 1048576 | tf_op jit(solution)/shard_map/all_to_all | solution.py:24
  21.7 0.5 copy.38
  22.3 1.1 reshape.15
  23.4 14.4 %all-to-all-start.1 = ((bf16[64,16,256]{2,1,0:T(8,128)(2,1)}), bf16[64,16,256]{2,1,0:T(8,128)(2,1)S(1)}, u32[]{:S(2)}, u32[]{:S(2)}) async-start(bf16[64,16,256]{2,1,0:T(8,128)(2,1)} %reshape.15), calls=%async_computation.1 | async-start | bytes 1048576 | tf_op jit(solution)/shard_map/all_to_all | solution.py:28
  37.8 0.0 copy-done.7
  37.8 0.1 copy.37
  37.9 0.1 copy.39
  38.0 0.1 reshape.26
  38.2 16.9 %all-to-all-done.1 = bf16[64,16,256]{2,1,0:T(8,128)(2,1)S(1)} async-done(((bf16[64,16,256]{2,1,0:T(8,128)(2,1)}), bf16[64,16,256]{2,1,0:T(8,128)(2,1)S(1)}, u32[]{:S(2)}, u32[]{:S(2)}) %all-to-all-start.1) | async-done | bytes 524320 | tf_op jit(solution)/shard_map/all_to_all | solution.py:28
  55.0 0.8 gather_fusion.1
  55.8 1.5 %broadcast_select_fusion = bf16[64,4,16,256]{3,2,1,0:T(8,128)(2,1)} fusion(bf16[64,4,16,256]{3,2,1,0:T(8,128)(2,1)S(1)} %bitcast.62, pred[64,4]{1,0:T(8,128)(4,1)S(1)} %copy.37), kind=kLoop, calls=%fused_computation.4 | loop fusion | flops 1048576 | bytes 4194560 | tf_op jit(solution)/shard_map/jit(_take)/select_n | solution.py:30
  57.3 7.4 %all-to-all-start.2 = ((bf16[64,4,16,256]{3,2,1,0:T(8,128)(2,1)}), bf16[64,4,16,256]{3,2,1,0:T(8,128)(2,1)S(1)}, u32[]{:S(2)}, u32[]{:S(2)}) async-start(bf16[64,4,16,256]{3,2,1,0:T(8,128)(2,1)} %broadcast_select_fusion), calls=%async_computation.2 | async-start | bytes 4194304 | tf_op jit(solution)/shard_map/all_to_all | solution.py:31
  64.8 1.0 copy.36
  65.9 0.2 copy.60
  66.1 0.2 copy.61
  66.3 0.1 neg.3
  66.3 0.8 maximum_bitcast_fusion
  67.2 47.6 %all-to-all-done.2 = bf16[64,4,16,256]{3,2,1,0:T(8,128)(2,1)S(1)} async-done(((bf16[64,4,16,256]{3,2,1,0:T(8,128)(2,1)}), bf16[64,4,16,256]{3,2,1,0:T(8,128)(2,1)S(1)}, u32[]{:S(2)}, u32[]{:S(2)}) %all-to-all-start.2) | async-done | bytes 2097184 | tf_op jit(solution)/shard_map/all_to_all | solution.py:31
  114.8 1.2 fusion.12
  116.0 0.0 copy-start.1
  116.0 0.0 copy-start.4
  116.0 2.1 %reshape_squeeze.12 = bf16[8,128,2,128]{3,2,1,0:T(2,128)(2,1)} reshape(bf16[64,1,16,256]{3,2,1,0:T(8,128)(2,1)} %get-tuple-element.7) | data formatting | bytes 1048576 | tf_op jit(solution)/shard_map/reshape;squeeze | solution.py:34
  118.0 2.0 %reshape_squeeze.15 = bf16[8,128,2,128]{3,2,1,0:T(2,128)(2,1)} reshape(bf16[64,1,16,256]{3,2,1,0:T(8,128)(2,1)} %get-tuple-element.8) | data formatting | bytes 1048576 | tf_op jit(solution)/shard_map/reshape;squeeze | solution.py:34
  120.0 0.0 copy-start.2
  120.0 0.0 copy-start.5
  120.0 0.0 copy-start.6
  120.0 0.0 copy-done.1
  120.0 0.0 copy-done.4
  120.0 1.6 %fusion.1 = f32[1,8,2,128,128]{4,3,2,1,0:T(8,128)S(1)} fusion(bf16[8,128,2,128,1]{3,2,1,0,4:T(2,128)(2,1)} %bitcast.67, bf16[8,128,2,1,128]{1,4,2,3,0:T(8,128)(2,1)S(1)} %copy-done.4, bf16[8,128,2,1,128]{1,4,2,3,0:T(8,128)(2,1)S(1)} %copy-done.1), kind=kOutput, calls=%fused_computation.10 | convolution fusion | flops 135004160 | bytes 2621440 | tf_op jit(solution)/shard_map/fwkci,fwkj->fcij/dot_general | solution.py:13
  121.6 0.0 copy-done.2
  121.6 0.0 copy-done.5
  121.6 0.0 copy-done.6
  121.6 0.4 fusion.7
  122.0 1.0 reshape_squeeze.14
  123.0 0.0 copy-start.3
  123.0 2.8 %fusion.5 = f32[1,8,2,128,128]{4,3,2,1,0:T(8,128)} fusion(bf16[8,128,2,128,1]{3,2,1,0,4:T(2,128)(2,1)} %bitcast.70, bf16[8,128,2,1,128]{1,4,2,3,0:T(8,128)(2,1)} %maximum_bitcast_fusion, bf16[8,128,2,1,128]{1,4,2,3,0:T(8,128)(2,1)} %copy.36), kind=kOutput, calls=%fused_computation.14 | convolution fusion | flops 135004160 | bytes 2621440 | tf_op jit(solution)/shard_map/fwkci,fwkj->fcij/dot_general | solution.py:13
  125.8 1.0 reshape_squeeze.13
  126.8 0.0 copy-start
  126.8 0.0 copy-done.3
  126.8 1.7 %fusion.3 = f32[1,8,2,128,128]{4,3,2,1,0:T(8,128)S(1)} fusion(bf16[8,128,2,128,1]{3,2,1,0,4:T(2,128)(2,1)} %bitcast.69, bf16[8,128,2,1,128]{1,4,2,3,0:T(8,128)(2,1)} %maximum_bitcast_fusion, bf16[8,128,2,1,128]{1,4,2,3,0:T(8,128)(2,1)S(1)} %copy-done.3), kind=kOutput, calls=%fused_computation.12 | convolution fusion | flops 135004160 | bytes 2621440 | tf_op jit(solution)/shard_map/fwkci,fwkj->fcij/dot_general | solution.py:13
  128.5 0.0 copy-done
  128.5 2.3 %pad_maximum_fusion = f32[4,8,2,128,128]{4,3,2,1,0:T(8,128)} fusion(f32[1,8,2,128,128]{4,3,2,1,0:T(8,128)S(1)} %fusion.7, f32[1,8,2,128,128]{4,3,2,1,0:T(8,128)S(1)} %copy-done, f32[1,8,2,128,128]{4,3,2,1,0:T(8,128)S(1)} %fusion.3, f32[1,8,2,128,128]{4,3,2,1,0:T(8,128)S(1)} %fusion.1), kind=kLoop, calls=%fused_computation.2 | loop fusion | flops 3145728 | bytes 8388608 | tf_op jit(solution)/shard_map/stack | solution.py:36
  (6 shorter events, 0.1 us)
Async XLA Ops:
  10.2 27.6 %copy-start.7 = (s32[4,64]{1,0:T(4,128)S(1)}, s32[4,64]{1,0:T(4,128)}, u32[]{:S(2)}) copy-start(s32[4,64]{1,0:T(4,128)} %param.4) | copy-start | bytes 3076
  23.4 31.6 %all-to-all-start.1 = ((bf16[64,16,256]{2,1,0:T(8,128)(2,1)}), bf16[64,16,256]{2,1,0:T(8,128)(2,1)S(1)}, u32[]{:S(2)}, u32[]{:S(2)}) async-start(bf16[64,16,256]{2,1,0:T(8,128)(2,1)} %reshape.15), calls=%async_computation.1 | async-start | bytes 1048576 | tf_op jit(solution)/shard_map/all_to_all | solution.py:28
  57.3 57.4 %all-to-all-start.2 = ((bf16[64,4,16,256]{3,2,1,0:T(8,128)(2,1)}), bf16[64,4,16,256]{3,2,1,0:T(8,128)(2,1)S(1)}, u32[]{:S(2)}, u32[]{:S(2)}) async-start(bf16[64,4,16,256]{3,2,1,0:T(8,128)(2,1)} %broadcast_select_fusion), calls=%async_computation.2 | async-start | bytes 4194304 | tf_op jit(solution)/shard_map/all_to_all | solution.py:31
  116.0 4.0 %copy-start.1 = (bf16[8,128,2,1,128]{1,4,2,3,0:T(8,128)(2,1)S(1)}, bf16[8,128,2,1,128]{1,4,2,3,0:T(8,128)(2,1)}, u32[]{:S(2)}) copy-start(bf16[8,128,2,1,128]{1,4,2,3,0:T(8,128)(2,1)} %copy.36) | copy-start | bytes 1572868
  116.0 4.0 %copy-start.4 = (bf16[8,128,2,1,128]{1,4,2,3,0:T(8,128)(2,1)S(1)}, bf16[8,128,2,1,128]{1,4,2,3,0:T(8,128)(2,1)}, u32[]{:S(2)}) copy-start(bf16[8,128,2,1,128]{1,4,2,3,0:T(8,128)(2,1)} %maximum_bitcast_fusion) | copy-start | bytes 1572868
  120.0 1.6 %copy-start.2 = (bf16[8,128,2,1,128]{1,4,2,3,0:T(8,128)(2,1)S(1)}, bf16[8,128,2,1,128]{1,4,2,3,0:T(8,128)(2,1)}, u32[]{:S(2)}) copy-start(bf16[8,128,2,1,128]{1,4,2,3,0:T(8,128)(2,1)} %copy.36) | copy-start | bytes 1572868
  120.0 1.6 %copy-start.5 = (bf16[8,128,2,1,128]{1,4,2,3,0:T(8,128)(2,1)S(1)}, bf16[8,128,2,1,128]{1,4,2,3,0:T(8,128)(2,1)}, u32[]{:S(2)}) copy-start(bf16[8,128,2,1,128]{1,4,2,3,0:T(8,128)(2,1)} %maximum_bitcast_fusion) | copy-start | bytes 1572868
  120.0 1.6 %copy-start.6 = (bf16[8,128,2,128]{3,2,1,0:T(2,128)(2,1)S(1)}, bf16[8,128,2,128]{3,2,1,0:T(2,128)(2,1)}, u32[]{:S(2)}) copy-start(bf16[8,128,2,128]{3,2,1,0:T(2,128)(2,1)} %reshape_squeeze.15) | copy-start | bytes 1572868
  123.0 3.8 %copy-start.3 = (bf16[8,128,2,1,128]{1,4,2,3,0:T(8,128)(2,1)S(1)}, bf16[8,128,2,1,128]{1,4,2,3,0:T(8,128)(2,1)}, u32[]{:S(2)}) copy-start(bf16[8,128,2,1,128]{1,4,2,3,0:T(8,128)(2,1)} %copy.36) | copy-start | bytes 1572868
  126.8 1.7 %copy-start = (f32[1,8,2,128,128]{4,3,2,1,0:T(8,128)S(1)}, f32[1,8,2,128,128]{4,3,2,1,0:T(8,128)}, u32[]{:S(2)}) copy-start(f32[1,8,2,128,128]{4,3,2,1,0:T(8,128)} %fusion.5) | copy-start | bytes 3145732

commit v2 on v1

v2 whole, which is shorter than its diff:
```python
import functools
import math

import jax
import jax.numpy as jnp
from jax import lax
from jax.experimental import pallas as pl
from jax.sharding import PartitionSpec as P


def cross_kernel(bins, scale, lhs_ref, rhs_ref, out_ref):
    pieces = rhs_ref.shape[0]
    per_bin = pieces // bins
    chan = out_ref.shape[3]
    for f in range(bins):
        block = rhs_ref[f * per_bin:(f + 1) * per_bin, 0]
        block = block.reshape(per_bin * block.shape[1], block.shape[2])
        acc = jnp.dot(lhs_ref[f, 0], block[:, :chan], preferred_element_type=jnp.float32)
        acc = acc + jnp.dot(lhs_ref[f, 1], block[:, chan:], preferred_element_type=jnp.float32)
        out_ref[0, f] = (acc * scale).reshape(2, chan, chan)


def cross_spectra(lhs, arrived, scale):
    bins, _, two_chan, windows = lhs.shape
    chan = two_chan // 2
    pieces, rounds, rows, _ = arrived.shape
    return pl.pallas_call(
        functools.partial(cross_kernel, bins, scale),
        grid=(rounds,),
        in_specs=[
            pl.BlockSpec((bins, 2, two_chan, windows), lambda r: (0, 0, 0, 0)),
            pl.BlockSpec((pieces, 1, rows, two_chan), lambda r: (0, r, 0, 0)),
        ],
        out_specs=pl.BlockSpec((1, bins, 2, chan, chan), lambda r: (r, 0, 0, 0, 0)),
        out_shape=jax.ShapeDtypeStruct((rounds, bins, 2, chan, chan), jnp.float32),
        cost_estimate=pl.CostEstimate(
            flops=2 * rounds * bins * 2 * two_chan * windows * chan,
            bytes_accessed=lhs.size * 2 + arrived.size * 2 + rounds * bins * 2 * chan * chan * 4,
            transcendentals=0,
        ),
    )(lhs, arrived)


def on_device(spectra, plan, assignment):
    bin_count, win_local, _, chan_width = spectra.shape
    seg_count = lax.axis_size("seg")
    group_count = lax.axis_size("chan")
    seg_index = lax.axis_index("seg")
    win_count = win_local * seg_count
    my_bins = bin_count // seg_count
    scale = 1.0 / math.sqrt(win_count)
    local_slots = assignment - lax.axis_index("chan") * chan_width
    onehot = (local_slots[None, :] == jnp.arange(chan_width, dtype=local_slots.dtype)[:, None])
    ordered = jnp.einsum(
        "fwkm,mc->fwkc", spectra, onehot.astype(spectra.dtype), preferred_element_type=jnp.float32
    ).astype(spectra.dtype)
    per_bin = group_count // my_bins
    win_piece = win_local // per_bin
    rows = ordered.reshape(seg_count, my_bins, per_bin, win_piece, 2 * chan_width)
    send = rows.transpose(1, 2, 0, 3, 4).reshape(group_count * seg_count, win_piece, 2 * chan_width)
    held = lax.all_to_all(send, ("chan", "seg"), split_axis=0, concat_axis=0, tiled=True)
    held = held.reshape(group_count, seg_count * win_piece, 2 * chan_width)
    outgoing = jnp.take(held, plan.T, axis=0)
    arrived = lax.all_to_all(outgoing, "chan", split_axis=0, concat_axis=0, tiled=True)
    ranges = ordered.reshape(seg_count, my_bins, win_local, 2 * chan_width)
    by_shift = [lax.dynamic_index_in_dim(ranges, seg_index, 0, keepdims=False)]
    for shift in range(1, seg_count):
        part = lax.dynamic_index_in_dim(ranges, (seg_index + shift) % seg_count, 0, keepdims=False)
        pairs = [(i, (i + shift) % seg_count) for i in range(seg_count)]
        by_shift.append(lax.ppermute(part, "seg", pairs))
    by_shift = jnp.stack(by_shift)
    order = (seg_index - jnp.arange(seg_count)) % seg_count
    own = jnp.take(by_shift, order, axis=0)
    own = own.reshape(seg_count, my_bins, per_bin, win_piece, 2, chan_width)
    own = own.transpose(1, 4, 5, 2, 0, 3).reshape(my_bins, 2, chan_width, win_count)
    lhs_k0 = jnp.concatenate([own[:, 0], own[:, 1]], axis=1)
    lhs_k1 = jnp.concatenate([own[:, 1], -own[:, 0]], axis=1)
    lhs = jnp.stack([lhs_k0, lhs_k1], axis=1)
    return cross_spectra(lhs, arrived, scale)


def solution(mesh):
    in_specs = (P(None, "seg", None, "chan"), P(), P("chan"))
    out_specs = P(None, "seg", None, "chan", None)
    return jax.shard_map(
        on_device, mesh=mesh, in_specs=in_specs, out_specs=out_specs, check_vma=False
    )
```

time: 131 us -> 107 us (0.82)
  blocking collectives: 11.5 us -> 0 us
  matrix products: 6.52 us -> 0.29 us
  waiting for transfers between devices: 64.4 us -> 58.8 us
  Pallas kernels: 0 us -> 5.26 us
  local copies, waits for them, and re-layouts: 19 us -> 14 us
  other arithmetic: 7.26 us -> 5.37 us
    all_to_all x1, waiting for transfers between devices: 47.6 us -> 26.5 us  [on_device(): lax.all_to_all(outgoing, 'chan', split_axis=0, concat_axis=0, tiled=True)]
    ppermute x0 -> x3, waiting for transfers between devices: none -> 13.5 us  [on_device(): by_shift.append(lax.ppermute(part, 'seg', pairs))]
    all_to_all x1 -> x0, blocking collectives: 11.5 us -> none  [on_device(): lax.all_to_all(ordered, 'seg', split_axis=0, concat_axis=1, tiled=True)]
    another operation x5 -> x0, local copies, waits for them, and re-layouts: 6.94 us -> none  [the longest x4 5.92 us: on_device(): arrived[:, round_index].reshape(my_bins, win_count, 2, chan_width)]
    dot_general x4 -> x1, matrix products: 6.52 us -> 0.29 us  [on_device(): jnp.einsum('fwkm,mc->fwkc', spectra, onehot.astype(spectra.dtype), prefer...]
    pallas_call x0 -> x1, Pallas kernels: none -> 5.26 us  [cross_spectra(): pl.pallas_call(functools.partial(cross_kernel, bins, scale), grid=(rounds...]
    select_n x1 -> x0, local copies, waits for them, and re-layouts: 2.07 us -> none  [on_device(): ordered = jnp.take(spectra, local_slots, axis=3)]
    all_to_all x1, waiting for transfers between devices: 16.9 us -> 18.8 us  [on_device(): lax.all_to_all(send, ('chan', 'seg'), split_axis=0, concat_axis=0, tiled=...]
  transfers between devices with their start and end apart: 2 -> 5, of which waited for: 2 -> 4; matrix products, arithmetic and copies ran while one was open for 2% -> 9% of each run, Pallas kernels for 0% -> 0%
where the time goes in v2:
time: 107 us
  waiting for transfers between devices  58.8 us (55%)
  starting transfers between devices  22.7 us (21%)
  local copies, waits for them, and re-layouts  14 us (13%)
  other arithmetic  5.37 us (5%)
  Pallas kernels  5.26 us (5%)
    all_to_all x1, waiting for transfers between devices, on_device(): lax.all_to_all(outgoing, 'chan', split_axis=0, concat_axis=0, tiled=True)  26.5 us
    all_to_all x1, waiting for transfers between devices, on_device(): lax.all_to_all(send, ('chan', 'seg'), split_axis=0, concat_axis=0, tiled=...  18.8 us
    all_to_all x1, starting transfers between devices, on_device(): lax.all_to_all(send, ('chan', 'seg'), split_axis=0, concat_axis=0, tiled=...  14.7 us
    ppermute x3, waiting for transfers between devices, on_device(): by_shift.append(lax.ppermute(part, 'seg', pairs))  13.5 us
    all_to_all x1, starting transfers between devices, on_device(): lax.all_to_all(outgoing, 'chan', split_axis=0, concat_axis=0, tiled=True)  7.05 us
    pallas_call x1, Pallas kernels, cross_spectra(): pl.pallas_call(functools.partial(cross_kernel, bins, scale), grid=(rounds...  5.26 us
    unnamed x8, local copies, waits for them, and re-layouts  3.06 us
    select_n x2, other arithmetic, on_device(): outgoing = jnp.take(held, plan.T, axis=0)  2.75 us
  transfers between devices with their start and end apart: 5, of which 4 were waited for; matrix products, arithmetic and copies ran while one was open for 9% of the time, Pallas kernels for 0%

profile of v2, /device:TPU:2, one launch (start us, length us, event | category | flops | bytes accessed | tf_op | source)
XLA Modules:
  0.0 106.7 jit_solution(2006126745435107646)
XLA Ops:
  0.0 0.0 copy-start
  0.0 0.7 broadcast_subtract_fusion
  0.7 0.3 copy-done
  1.1 0.3 fusion
  1.4 0.0 copy-start.2
  1.4 0.5 copy.14
  1.9 0.3 reshape.79
  2.3 1.2 %copy.15 = bf16[8,8,4,4,256]{4,3,2,1,0:T(4,128)(2,1)} copy(bf16[8,8,4,4,256]{4,0,2,3,1:T(8,128)(2,1)S(1)} %bitcast.44) | data formatting | bytes 1048576 | tf_op jit(solution)/shard_map/transpose | solution.py:60
  3.5 14.7 %all-to-all-start = ((bf16[256,4,256]{2,1,0:T(4,128)(2,1)}), bf16[256,4,256]{2,1,0:T(4,128)(2,1)S(1)}, u32[]{:S(2)}, u32[]{:S(2)}) async-start(bf16[256,4,256]{2,1,0:T(4,128)(2,1)} %bitcast.19), calls=%async_computation | async-start | bytes 1048576 | tf_op jit(solution)/shard_map/all_to_all | solution.py:61
  18.2 0.0 copy-done.2
  18.2 0.1 copy.13
  18.3 0.1 copy.16
  18.4 0.1 reshape.92
  18.5 18.8 %all-to-all-done = bf16[256,4,256]{2,1,0:T(4,128)(2,1)S(1)} async-done(((bf16[256,4,256]{2,1,0:T(4,128)(2,1)}), bf16[256,4,256]{2,1,0:T(4,128)(2,1)S(1)}, u32[]{:S(2)}, u32[]{:S(2)}) %all-to-all-start) | async-done | bytes 524320 | tf_op jit(solution)/shard_map/all_to_all | solution.py:61
  37.3 0.1 reshape.81
  37.5 2.1 %gather_fusion.1 = bf16[256,16,256]{2,1,0:T(8,128)(2,1)} fusion(bf16[64,16,256]{2,1,0:T(8,128)(2,1)S(1)} %reshape.81, s32[1024]{0:T(1024)S(1)} %pad_clamp_fusion), kind=kCustom, calls=%fused_computation.1 | custom fusion | bytes 4195328 | tf_op jit(solution)/shard_map/jit(_take)/gather | solution.py:63
  39.5 2.7 %broadcast_select_fusion = bf16[64,4,16,256]{3,2,1,0:T(8,128)(2,1)} fusion(bf16[64,4,16,256]{3,2,1,0:T(8,128)(2,1)} %bitcast.41, pred[64,4]{1,0:T(8,128)(4,1)S(1)} %copy.13), kind=kLoop, calls=%fused_computation.2 | loop fusion | flops 1048576 | bytes 4194560 | tf_op jit(solution)/shard_map/jit(_take)/select_n | solution.py:63
  42.3 7.1 %all-to-all-start.1 = ((bf16[64,4,16,256]{3,2,1,0:T(8,128)(2,1)}), bf16[64,4,16,256]{3,2,1,0:T(8,128)(2,1)S(1)}, u32[]{:S(2)}, u32[]{:S(2)}) async-start(bf16[64,4,16,256]{3,2,1,0:T(8,128)(2,1)} %broadcast_select_fusion), calls=%async_computation.1 | async-start | bytes 4194304 | tf_op jit(solution)/shard_map/all_to_all | solution.py:64
  49.4 1.3 %copy.8 = bf16[32,32,2,128]{3,2,1,0:T(2,128)(2,1)} copy(bf16[32,32,2,128]{3,1,2,0:T(8,128)(2,1)S(1)} %fusion) | data formatting | bytes 1048576 | tf_op jit(solution)/shard_map/convert_element_type | solution.py:56
  50.7 1.4 %reshape.77 = bf16[4,8,32,256]{3,2,1,0:T(8,128)(2,1)S(1)} reshape(bf16[32,32,2,128]{3,2,1,0:T(2,128)(2,1)} %copy.8) | data formatting | bytes 1048576 | tf_op jit(solution)/shard_map/reshape | solution.py:65
  52.2 0.1 collective-permute-start.2
  52.3 0.8 collective-permute-start.1
  53.0 0.1 collective-permute-start
  53.2 6.3 %collective-permute-done.2 = bf16[8,32,256]{2,1,0:T(8,128)(2,1)S(1)} collective-permute-done((bf16[8,32,256]{2,1,0:T(8,128)(2,1)S(1)}, bf16[8,32,256]{2,1,0:T(8,128)(2,1)S(1)}, u32[]{:S(2)}, u32[]{:S(2)}) %collective-permute-start.2) | collective-permute-done | bytes 131104 | tf_op jit(solution)/shard_map/ppermute | solution.py:70
  59.5 7.2 %collective-permute-done.1 = bf16[8,32,256]{2,1,0:T(8,128)(2,1)S(1)} collective-permute-done((bf16[8,32,256]{2,1,0:T(8,128)(2,1)S(1)}, bf16[8,32,256]{2,1,0:T(8,128)(2,1)S(1)}, u32[]{:S(2)}, u32[]{:S(2)}) %collective-permute-start.1) | collective-permute-done | bytes 131104 | tf_op jit(solution)/shard_map/ppermute | solution.py:70
  66.7 0.0 collective-permute-done
  66.7 0.1 pad_maximum_fusion.1
  66.8 1.4 %gather_fusion = bf16[4,8,32,256]{3,2,1,0:T(8,128)(2,1)} fusion(bf16[4,8,32,256]{3,2,1,0:T(8,128)(2,1)S(1)} %pad_maximum_fusion.1, s32[1024]{0:T(1024)S(1)} %pad_clamp_fusion.1), kind=kCustom, calls=%fused_computation | custom fusion | bytes 1048592 | tf_op jit(solution)/shard_map/jit(_take)/gather | solution.py:73
  68.2 1.2 %gather.11 = bf16[4,8,8,4,2,128]{5,4,3,2,1,0:T(2,128)(2,1)S(1)} reshape(bf16[4,8,32,256]{3,2,1,0:T(8,128)(2,1)} %gather_fusion) | data formatting | bytes 1048576 | tf_op jit(solution)/shard_map/jit(_take)/gather | solution.py:73
  69.3 0.5 fusion.2
  69.8 0.3 copy.9
  70.2 0.7 fusion.9
  70.9 1.1 %copy.19 = bf16[8,1,128,128]{3,2,0,1:T(8,128)(2,1)S(1)} copy(bf16[8,1,128,128]{2,0,3,1:T(8,128)(2,1)} %get-tuple-element.5) | data formatting | bytes 524288
  72.1 0.2 copy.18
  72.4 0.2 maximum_bitcast_fusion
  72.5 1.1 %pad_maximum_fusion.lhs_ref = bf16[8,2,256,128]{3,2,1,0:T(8,128)(2,1)} fusion(bf16[8,1,256,128]{3,2,1,0:T(8,128)(2,1)S(1)} %get-tuple-element.12, bf16[8,1,256,128]{3,2,1,0:T(8,128)(2,1)S(1)} %get-tuple-element.11), kind=kLoop, calls=%fused_computation.5 | loop fusion | flops 524288 | bytes 2097152 | tf_op jit(solution)/shard_map/stack | solution.py:78
  73.6 26.5 %all-to-all-done.1.rhs_ref = bf16[64,4,16,256]{3,2,1,0:T(8,128)(2,1)S(1)} async-done(((bf16[64,4,16,256]{3,2,1,0:T(8,128)(2,1)}), bf16[64,4,16,256]{3,2,1,0:T(8,128)(2,1)S(1)}, u32[]{:S(2)}, u32[]{:S(2)}) %all-to-all-start.1) | async-done | bytes 2097184 | tf_op jit(solution)/shard_map/all_to_all | solution.py:64
  100.1 0.0 copy-start.1
  100.1 1.3 %copy-done.1 = bf16[64,4,16,256]{3,2,1,0:T(8,128)(2,1)} copy-done((bf16[64,4,16,256]{3,2,1,0:T(8,128)(2,1)}, bf16[64,4,16,256]{3,2,1,0:T(8,128)(2,1)S(1)}, u32[]{:S(2)}) %copy-start.1) | copy-done | bytes 2097176
  101.4 5.3 %shard_map.37 = f32[4,8,2,128,128]{4,3,2,1,0:T(8,128)} custom-call(bf16[8,2,256,128]{3,2,1,0:T(8,128)(2,1)} %pad_maximum_fusion.lhs_ref, bf16[64,4,16,256]{3,2,1,0:T(8,128)(2,1)} %copy-done.1), custom_call_target="tpu_custom_call" | custom-call | flops 536870912 | bytes 7340032 | tf_op jit(solution)/shard_map/pallas_call | solution.py:27
  (8 shorter events, 0.1 us)
Async XLA Ops:
  0.0 1.1 copy-start
  1.4 16.8 %copy-start.2 = (s32[4,64]{1,0:T(4,128)S(1)}, s32[4,64]{1,0:T(4,128)}, u32[]{:S(2)}) copy-start(s32[4,64]{1,0:T(4,128)} %param.4) | copy-start | bytes 3076
  3.5 33.9 %all-to-all-start = ((bf16[256,4,256]{2,1,0:T(4,128)(2,1)}), bf16[256,4,256]{2,1,0:T(4,128)(2,1)S(1)}, u32[]{:S(2)}, u32[]{:S(2)}) async-start(bf16[256,4,256]{2,1,0:T(4,128)(2,1)} %bitcast.19), calls=%async_computation | async-start | bytes 1048576 | tf_op jit(solution)/shard_map/all_to_all | solution.py:61
  42.3 57.8 %all-to-all-start.1 = ((bf16[64,4,16,256]{3,2,1,0:T(8,128)(2,1)}), bf16[64,4,16,256]{3,2,1,0:T(8,128)(2,1)S(1)}, u32[]{:S(2)}, u32[]{:S(2)}) async-start(bf16[64,4,16,256]{3,2,1,0:T(8,128)(2,1)} %broadcast_select_fusion), calls=%async_computation.1 | async-start | bytes 4194304 | tf_op jit(solution)/shard_map/all_to_all | solution.py:64
  52.2 7.3 %collective-permute-start.2 = (bf16[8,32,256]{2,1,0:T(8,128)(2,1)S(1)}, bf16[8,32,256]{2,1,0:T(8,128)(2,1)S(1)}, u32[]{:S(2)}, u32[]{:S(2)}) collective-permute-start(bf16[8,32,256]{2,1,0:T(8,128)(2,1)S(1)} %get-tuple-element.8), channel_id=1, source_target_pairs={{0,3},{1,0},{2,1},{3,2},{4,7},{5,4},{6,5},{7,6},{8,11},{9,8},{10,9... | collective-permute-start | bytes 393224 | tf_op jit(solution)/shard_map/ppermute | solution.py:70
  52.3 14.4 %collective-permute-start.1 = (bf16[8,32,256]{2,1,0:T(8,128)(2,1)S(1)}, bf16[8,32,256]{2,1,0:T(8,128)(2,1)S(1)}, u32[]{:S(2)}, u32[]{:S(2)}) collective-permute-start(bf16[8,32,256]{2,1,0:T(8,128)(2,1)S(1)} %get-tuple-element.9), channel_id=1, source_target_pairs={{0,2},{1,3},{2,0},{3,1},{4,6},{5,7},{6,4},{7,5},{8,10},{9,11},{10,... | collective-permute-start | bytes 393224 | tf_op jit(solution)/shard_map/ppermute | solution.py:70
  53.0 13.7 %collective-permute-start = (bf16[8,32,256]{2,1,0:T(8,128)(2,1)S(1)}, bf16[8,32,256]{2,1,0:T(8,128)(2,1)S(1)}, u32[]{:S(2)}, u32[]{:S(2)}) collective-permute-start(bf16[8,32,256]{2,1,0:T(8,128)(2,1)S(1)} %get-tuple-element.10), channel_id=1, source_target_pairs={{0,1},{1,2},{2,3},{3,0},{4,5},{5,6},{6,7},{7,4},{8,9},{9,10},{10,1... | collective-permute-start | bytes 393224 | tf_op jit(solution)/shard_map/ppermute | solution.py:70
  100.1 1.3 %copy-start.1 = (bf16[64,4,16,256]{3,2,1,0:T(8,128)(2,1)}, bf16[64,4,16,256]{3,2,1,0:T(8,128)(2,1)S(1)}, u32[]{:S(2)}) copy-start(bf16[64,4,16,256]{3,2,1,0:T(8,128)(2,1)S(1)} %all-to-all-done.1.rhs_ref) | copy-start | bytes 6291460

commit v3 on v2

v3 whole, which is shorter than its diff:
```python
import functools
import math

import jax
import jax.numpy as jnp
from jax import lax
from jax.experimental import pallas as pl
from jax.experimental.pallas import tpu as pltpu
from jax.sharding import PartitionSpec as P


def cross_kernel(bins_per_step, scale, lhs_ref, rhs_ref, out_ref):
    step = pl.program_id(0)
    pieces, rounds, rows, two_chan = rhs_ref.shape
    bins = lhs_ref.shape[0]
    per_bin = pieces // bins
    chan = two_chan // 2
    for b in range(bins_per_step):
        f = step * bins_per_step + b
        lhs = lhs_ref[f]
        for r in range(rounds):
            block = rhs_ref[pl.ds(f * per_bin, per_bin), r]
            block = block.reshape(per_bin * rows, two_chan)
            block = jnp.concatenate([block[:, :chan], block[:, chan:]], axis=0)
            acc = jnp.dot(lhs, block, preferred_element_type=jnp.float32)
            out_ref[r, b] = (acc * scale).reshape(2, chan, chan)


def cross_spectra(lhs, arrived, scale):
    bins, two_chan, _ = lhs.shape
    chan = two_chan // 2
    pieces, rounds, rows, _ = arrived.shape
    bins_per_step = 2
    return pl.pallas_call(
        functools.partial(cross_kernel, bins_per_step, scale),
        grid=(bins // bins_per_step,),
        in_specs=[
            pl.BlockSpec(memory_space=pltpu.VMEM),
            pl.BlockSpec(memory_space=pltpu.VMEM),
        ],
        out_specs=pl.BlockSpec((rounds, bins_per_step, 2, chan, chan), lambda g: (0, g, 0, 0, 0)),
        out_shape=jax.ShapeDtypeStruct((rounds, bins, 2, chan, chan), jnp.float32),
        cost_estimate=pl.CostEstimate(
            flops=2 * rounds * bins * two_chan * two_chan * chan,
            bytes_accessed=lhs.size * 2 + arrived.size * 2 + rounds * bins * 2 * chan * chan * 4,
            transcendentals=0,
        ),
    )(lhs, arrived)


def on_device(spectra, plan, assignment):
    bin_count, win_local, _, chan_width = spectra.shape
    seg_count = lax.axis_size("seg")
    group_count = lax.axis_size("chan")
    seg_index = lax.axis_index("seg")
    win_count = win_local * seg_count
    my_bins = bin_count // seg_count
    scale = 1.0 / math.sqrt(win_count)
    local_slots = assignment - lax.axis_index("chan") * chan_width
    onehot = (local_slots[None, :] == jnp.arange(chan_width, dtype=local_slots.dtype)[:, None])
    ordered = jnp.einsum(
        "fwkm,mc->fwkc", spectra, onehot.astype(spectra.dtype), preferred_element_type=jnp.float32
    ).astype(spectra.dtype)
    per_bin = group_count // my_bins
    win_piece = win_local // per_bin
    rows = ordered.reshape(seg_count, my_bins, per_bin, win_piece, 2 * chan_width)
    send = rows.transpose(1, 2, 0, 3, 4).reshape(group_count * seg_count, win_piece, 2 * chan_width)
    round_count = plan.shape[0]
    held = lax.all_to_all(send, ("chan", "seg"), split_axis=0, concat_axis=0, tiled=True)
    held = held.reshape(group_count, seg_count * win_piece, 2 * chan_width)
    pick = plan.T.reshape(-1)[:, None] == jnp.arange(group_count, dtype=plan.dtype)[None, :]
    outgoing = jnp.dot(
        pick.astype(held.dtype), held.reshape(group_count, -1), preferred_element_type=jnp.float32
    ).astype(held.dtype).reshape(group_count, round_count, seg_count * win_piece, 2 * chan_width)
    arrived = lax.all_to_all(outgoing, "chan", split_axis=0, concat_axis=0, tiled=True)
    ranges = ordered.reshape(seg_count, my_bins, win_local, 2 * chan_width)
    by_shift = [lax.dynamic_index_in_dim(ranges, seg_index, 0, keepdims=False)]
    for shift in range(1, seg_count):
        part = lax.dynamic_index_in_dim(ranges, (seg_index + shift) % seg_count, 0, keepdims=False)
        pairs = [(i, (i + shift) % seg_count) for i in range(seg_count)]
        by_shift.append(lax.ppermute(part, "seg", pairs))
    by_shift = jnp.stack(by_shift)
    order = (seg_index - jnp.arange(seg_count)) % seg_count
    own = jnp.take(by_shift, order, axis=0)
    own = own.reshape(seg_count, my_bins, per_bin, win_piece, 2, chan_width)
    own = own.transpose(1, 5, 4, 2, 0, 3).reshape(my_bins, chan_width, 2, win_count)
    imag_rows = jnp.stack([own[:, :, 1], -own[:, :, 0]], axis=2)
    lhs = jnp.stack([own, imag_rows], axis=1).reshape(my_bins, 2 * chan_width, 2 * win_count)
    return cross_spectra(lhs, arrived, scale)


def solution(mesh):
    in_specs = (P(None, "seg", None, "chan"), P(), P("chan"))
    out_specs = P(None, "seg", None, "chan", None)
    return jax.shard_map(
        on_device, mesh=mesh, in_specs=in_specs, out_specs=out_specs, check_vma=False
    )
```

time: 107 us -> 107 us (level)
  local copies, waits for them, and re-layouts: 14 us -> 18 us
  waiting for transfers between devices: 58.8 us -> 55.8 us
  other arithmetic: 5.37 us -> 2.54 us
  matrix products: 0.29 us -> 2.07 us
    another operation x0 -> x2, local copies, waits for them, and re-layouts: none -> 3.99 us  [the longest x1 2.82 us: on_device(): jnp.stack([own, imag_rows], axis=1)]
    all_to_all x1, waiting for transfers between devices: 26.5 us -> 23.4 us  [on_device(): lax.all_to_all(outgoing, 'chan', split_axis=0, concat_axis=0, tiled=True)]
    select_n x2 -> x0, other arithmetic: 2.75 us -> none  [on_device(): outgoing = jnp.take(held, plan.T, axis=0)]
    reshape x1, local copies, waits for them, and re-layouts: 0.12 us -> 2.52 us  [on_device(): jnp.stack([own, imag_rows], axis=1)]
    gather x1 -> x0, local copies, waits for them, and re-layouts: 2.07 us -> none  [on_device(): outgoing = jnp.take(held, plan.T, axis=0)]
    dot_general x0 -> x1, matrix products: none -> 1.78 us  [on_device(): jnp.dot(pick.astype(held.dtype), held.reshape(group_count, -1), preferred...]
    unnamed x8 -> x7, local copies, waits for them, and re-layouts: 3.06 us -> 3.65 us
  transfers between devices with their start and end apart: 5 -> 5, of which waited for: 4 -> 4; matrix products, arithmetic and copies ran while one was open for 9% -> 12% of each run, Pallas kernels for 0% -> 0%
where the time goes in v3:
time: 107 us
  waiting for transfers between devices  55.8 us (52%)
  starting transfers between devices  22.7 us (21%)
  local copies, waits for them, and re-layouts  18 us (17%)
  Pallas kernels  5.14 us (5%)
  other arithmetic  2.54 us (2%)
  matrix products  2.07 us (2%)
    all_to_all x1, waiting for transfers between devices, on_device(): lax.all_to_all(outgoing, 'chan', split_axis=0, concat_axis=0, tiled=True)  23.4 us
    all_to_all x1, waiting for transfers between devices, on_device(): lax.all_to_all(send, ('chan', 'seg'), split_axis=0, concat_axis=0, tiled=...  19 us
    all_to_all x1, starting transfers between devices, on_device(): lax.all_to_all(send, ('chan', 'seg'), split_axis=0, concat_axis=0, tiled=...  14.7 us
    ppermute x3, waiting for transfers between devices, on_device(): by_shift.append(lax.ppermute(part, 'seg', pairs))  13.5 us
    all_to_all x1, starting transfers between devices, on_device(): lax.all_to_all(outgoing, 'chan', split_axis=0, concat_axis=0, tiled=True)  7.05 us
    pallas_call x1, Pallas kernels, cross_spectra(): pl.pallas_call(functools.partial(cross_kernel, bins_per_step, scale), gri...  5.14 us
    unnamed x7, local copies, waits for them, and re-layouts  3.65 us
    another operation x1, local copies, waits for them, and re-layouts, on_device(): jnp.stack([own, imag_rows], axis=1)  2.82 us
  transfers between devices with their start and end apart: 5, of which 4 were waited for; matrix products, arithmetic and copies ran while one was open for 12% of the time, Pallas kernels for 0%

profile of v3, /device:TPU:2, one launch (start us, length us, event | category | flops | bytes accessed | tf_op | source)
XLA Modules:
  0.0 106.6 jit_solution(10284646303545809836)
XLA Ops:
  0.0 0.0 copy-start
  0.0 0.7 broadcast_subtract_fusion
  0.7 0.3 copy-done
  1.1 0.3 fusion
  1.4 0.0 copy-start.2
  1.4 0.5 copy.11
  1.9 0.3 reshape.79
  2.3 1.2 %copy.12 = bf16[8,8,4,4,256]{4,3,2,1,0:T(4,128)(2,1)} copy(bf16[8,8,4,4,256]{4,0,2,3,1:T(8,128)(2,1)S(1)} %bitcast.39) | data formatting | bytes 1048576 | tf_op jit(solution)/shard_map/transpose | solution.py:67
  3.5 14.7 %all-to-all-start = ((bf16[256,4,256]{2,1,0:T(4,128)(2,1)}), bf16[256,4,256]{2,1,0:T(4,128)(2,1)S(1)}, u32[]{:S(2)}, u32[]{:S(2)}) async-start(bf16[256,4,256]{2,1,0:T(4,128)(2,1)} %bitcast.16), calls=%async_computation | async-start | bytes 1048576 | tf_op jit(solution)/shard_map/all_to_all | solution.py:69
  18.2 0.0 copy-done.2
  18.2 0.1 copy.10
  18.3 0.1 eq.37
  18.4 19.0 %all-to-all-done = bf16[256,4,256]{2,1,0:T(4,128)(2,1)S(1)} async-done(((bf16[256,4,256]{2,1,0:T(4,128)(2,1)}), bf16[256,4,256]{2,1,0:T(4,128)(2,1)S(1)}, u32[]{:S(2)}, u32[]{:S(2)}) %all-to-all-start) | async-done | bytes 524320 | tf_op jit(solution)/shard_map/all_to_all | solution.py:69
  37.3 1.2 %reshape_reshape.3 = bf16[64,4096]{1,0:T(8,128)(2,1)} reshape(bf16[256,4,256]{2,1,0:T(4,128)(2,1)S(1)} %all-to-all-done) | data formatting | bytes 1048576 | tf_op jit(solution)/shard_map/reshape;reshape | solution.py:73
  38.5 1.8 %convolution_convert_fusion = bf16[256,4096]{1,0:T(8,128)(2,1)S(1)} fusion(bf16[64,4096]{1,0:T(8,128)(2,1)} %reshape_reshape.3, s32[256]{0:T(256)S(1)} %eq.37), kind=kOutput, calls=%fused_computation.1 | convolution fusion | flops 135282688 | bytes 2622464 | tf_op jit(solution)/shard_map/dot_general | solution.py:72
  40.3 2.0 %copy.14 = bf16[32,8,16,256]{3,2,1,0:T(8,128)(2,1)} copy(bf16[32,8,16,256]{3,1,2,0:T(8,128)(2,1)S(1)} %bitcast.36) | data formatting | bytes 4194304
  42.3 7.1 %all-to-all-start.1 = ((bf16[64,4,16,256]{3,2,1,0:T(8,128)(2,1)}), bf16[64,4,16,256]{3,2,1,0:T(8,128)(2,1)S(1)}, u32[]{:S(2)}, u32[]{:S(2)}) async-start(bf16[64,4,16,256]{3,2,1,0:T(8,128)(2,1)} %bitcast.35), calls=%async_computation.1 | async-start | bytes 4194304 | tf_op jit(solution)/shard_map/all_to_all | solution.py:75
  49.4 1.3 %copy.6 = bf16[32,32,2,128]{3,2,1,0:T(2,128)(2,1)} copy(bf16[32,32,2,128]{3,1,2,0:T(8,128)(2,1)S(1)} %fusion) | data formatting | bytes 1048576 | tf_op jit(solution)/shard_map/convert_element_type | solution.py:63
  50.7 1.4 %reshape.76 = bf16[4,8,32,256]{3,2,1,0:T(8,128)(2,1)S(1)} reshape(bf16[32,32,2,128]{3,2,1,0:T(2,128)(2,1)} %copy.6) | data formatting | bytes 1048576 | tf_op jit(solution)/shard_map/reshape | solution.py:76
  52.1 0.1 collective-permute-start.2
  52.2 0.8 collective-permute-start.1
  53.0 0.1 collective-permute-start
  53.2 6.3 %collective-permute-done.2 = bf16[8,32,256]{2,1,0:T(8,128)(2,1)S(1)} collective-permute-done((bf16[8,32,256]{2,1,0:T(8,128)(2,1)S(1)}, bf16[8,32,256]{2,1,0:T(8,128)(2,1)S(1)}, u32[]{:S(2)}, u32[]{:S(2)}) %collective-permute-start.2) | collective-permute-done | bytes 131104 | tf_op jit(solution)/shard_map/ppermute | solution.py:81
  59.5 7.2 %collective-permute-done.1 = bf16[8,32,256]{2,1,0:T(8,128)(2,1)S(1)} collective-permute-done((bf16[8,32,256]{2,1,0:T(8,128)(2,1)S(1)}, bf16[8,32,256]{2,1,0:T(8,128)(2,1)S(1)}, u32[]{:S(2)}, u32[]{:S(2)}) %collective-permute-start.1) | collective-permute-done | bytes 131104 | tf_op jit(solution)/shard_map/ppermute | solution.py:81
  66.7 0.0 collective-permute-done
  66.7 0.1 pad_maximum_fusion.1
  66.7 1.4 %gather_fusion = bf16[4,8,32,256]{3,2,1,0:T(8,128)(2,1)} fusion(bf16[4,8,32,256]{3,2,1,0:T(8,128)(2,1)S(1)} %pad_maximum_fusion.1, s32[1024]{0:T(1024)S(1)} %pad_clamp_fusion), kind=kCustom, calls=%fused_computation | custom fusion | bytes 1048592 | tf_op jit(solution)/shard_map/jit(_take)/gather | solution.py:84
  68.1 1.2 %gather.7 = bf16[4,8,8,4,2,128]{5,4,3,2,1,0:T(2,128)(2,1)S(1)} reshape(bf16[4,8,32,256]{3,2,1,0:T(8,128)(2,1)} %gather_fusion) | data formatting | bytes 1048576 | tf_op jit(solution)/shard_map/jit(_take)/gather | solution.py:84
  69.3 0.5 fusion.2
  69.8 0.3 copy.7
  70.2 0.1 fusion.10
  70.2 0.1 maximum_bitcast_fusion
  70.3 1.1 %pad_maximum_fusion = bf16[8,2,128,2,128]{2,0,4,3,1:T(8,128)(2,1)} fusion(bf16[8,1,128,2,128]{2,0,4,3,1:T(8,128)(2,1)S(1)} %maximum_bitcast_fusion, bf16[8,1,128,2,128]{2,0,4,3,1:T(8,128)(2,1)S(1)} %bitcast.38), kind=kLoop, calls=%fused_computation.4 | loop fusion | flops 524288 | bytes 2097152 | tf_op jit(solution)/shard_map/stack | solution.py:88
  71.4 2.8 %copy.9 = bf16[8,2,128,2,128]{4,3,2,1,0:T(2,128)(2,1)} copy(bf16[8,2,128,2,128]{2,0,4,3,1:T(8,128)(2,1)} %pad_maximum_fusion) | data formatting | bytes 2097152 | tf_op jit(solution)/shard_map/stack | solution.py:88
  74.2 2.5 %reshape.78.lhs_ref = bf16[8,256,256]{2,1,0:T(8,128)(2,1)} reshape(bf16[8,2,128,2,128]{4,3,2,1,0:T(2,128)(2,1)} %copy.9) | data formatting | bytes 2097152 | tf_op jit(solution)/shard_map/reshape | solution.py:88
  76.7 23.4 %all-to-all-done.1.rhs_ref = bf16[64,4,16,256]{3,2,1,0:T(8,128)(2,1)S(1)} async-done(((bf16[64,4,16,256]{3,2,1,0:T(8,128)(2,1)}), bf16[64,4,16,256]{3,2,1,0:T(8,128)(2,1)S(1)}, u32[]{:S(2)}, u32[]{:S(2)}) %all-to-all-start.1) | async-done | bytes 2097184 | tf_op jit(solution)/shard_map/all_to_all | solution.py:75
  100.1 0.0 copy-start.1
  100.1 1.3 %copy-done.1 = bf16[64,4,16,256]{3,2,1,0:T(8,128)(2,1)} copy-done((bf16[64,4,16,256]{3,2,1,0:T(8,128)(2,1)}, bf16[64,4,16,256]{3,2,1,0:T(8,128)(2,1)S(1)}, u32[]{:S(2)}) %copy-start.1) | copy-done | bytes 2097176
  101.4 5.1 %shard_map.37 = f32[4,8,2,128,128]{4,3,2,1,0:T(8,128)} custom-call(bf16[8,256,256]{2,1,0:T(8,128)(2,1)} %reshape.78.lhs_ref, bf16[64,4,16,256]{3,2,1,0:T(8,128)(2,1)} %copy-done.1), custom_call_target="tpu_custom_call" | custom-call | flops 536870912 | bytes 7340032 | tf_op jit(solution)/shard_map/pallas_call | solution.py:34
  (4 shorter events, 0.1 us)
Async XLA Ops:
  0.0 1.1 copy-start
  1.4 16.8 %copy-start.2 = (s32[4,64]{1,0:T(4,128)S(1)}, s32[4,64]{1,0:T(4,128)}, u32[]{:S(2)}) copy-start(s32[4,64]{1,0:T(4,128)} %param.4) | copy-start | bytes 3076
  3.5 33.9 %all-to-all-start = ((bf16[256,4,256]{2,1,0:T(4,128)(2,1)}), bf16[256,4,256]{2,1,0:T(4,128)(2,1)S(1)}, u32[]{:S(2)}, u32[]{:S(2)}) async-start(bf16[256,4,256]{2,1,0:T(4,128)(2,1)} %bitcast.16), calls=%async_computation | async-start | bytes 1048576 | tf_op jit(solution)/shard_map/all_to_all | solution.py:69
  42.3 57.8 %all-to-all-start.1 = ((bf16[64,4,16,256]{3,2,1,0:T(8,128)(2,1)}), bf16[64,4,16,256]{3,2,1,0:T(8,128)(2,1)S(1)}, u32[]{:S(2)}, u32[]{:S(2)}) async-start(bf16[64,4,16,256]{3,2,1,0:T(8,128)(2,1)} %bitcast.35), calls=%async_computation.1 | async-start | bytes 4194304 | tf_op jit(solution)/shard_map/all_to_all | solution.py:75
  52.1 7.3 %collective-permute-start.2 = (bf16[8,32,256]{2,1,0:T(8,128)(2,1)S(1)}, bf16[8,32,256]{2,1,0:T(8,128)(2,1)S(1)}, u32[]{:S(2)}, u32[]{:S(2)}) collective-permute-start(bf16[8,32,256]{2,1,0:T(8,128)(2,1)S(1)} %get-tuple-element.8), channel_id=1, source_target_pairs={{0,3},{1,0},{2,1},{3,2},{4,7},{5,4},{6,5},{7,6},{8,11},{9,8},{10,9... | collective-permute-start | bytes 393224 | tf_op jit(solution)/shard_map/ppermute | solution.py:81
  52.2 14.4 %collective-permute-start.1 = (bf16[8,32,256]{2,1,0:T(8,128)(2,1)S(1)}, bf16[8,32,256]{2,1,0:T(8,128)(2,1)S(1)}, u32[]{:S(2)}, u32[]{:S(2)}) collective-permute-start(bf16[8,32,256]{2,1,0:T(8,128)(2,1)S(1)} %get-tuple-element.9), channel_id=1, source_target_pairs={{0,2},{1,3},{2,0},{3,1},{4,6},{5,7},{6,4},{7,5},{8,10},{9,11},{10,... | collective-permute-start | bytes 393224 | tf_op jit(solution)/shard_map/ppermute | solution.py:81
  53.0 13.7 %collective-permute-start = (bf16[8,32,256]{2,1,0:T(8,128)(2,1)S(1)}, bf16[8,32,256]{2,1,0:T(8,128)(2,1)S(1)}, u32[]{:S(2)}, u32[]{:S(2)}) collective-permute-start(bf16[8,32,256]{2,1,0:T(8,128)(2,1)S(1)} %get-tuple-element.10), channel_id=1, source_target_pairs={{0,1},{1,2},{2,3},{3,0},{4,5},{5,6},{6,7},{7,4},{8,9},{9,10},{10,1... | collective-permute-start | bytes 393224 | tf_op jit(solution)/shard_map/ppermute | solution.py:81
  100.1 1.3 %copy-start.1 = (bf16[64,4,16,256]{3,2,1,0:T(8,128)(2,1)}, bf16[64,4,16,256]{3,2,1,0:T(8,128)(2,1)S(1)}, u32[]{:S(2)}) copy-start(bf16[64,4,16,256]{3,2,1,0:T(8,128)(2,1)S(1)} %all-to-all-done.1.rhs_ref) | copy-start | bytes 6291460

commit v4 on v2

--- a/solution.py
+++ b/solution.py
@@ -8,33 +8,35 @@
 from jax.sharding import PartitionSpec as P
 
 
-def cross_kernel(bins, scale, lhs_ref, rhs_ref, out_ref):
-    pieces = rhs_ref.shape[0]
-    per_bin = pieces // bins
-    chan = out_ref.shape[3]
-    for f in range(bins):
-        block = rhs_ref[f * per_bin:(f + 1) * per_bin, 0]
-        block = block.reshape(per_bin * block.shape[1], block.shape[2])
-        acc = jnp.dot(lhs_ref[f, 0], block[:, :chan], preferred_element_type=jnp.float32)
-        acc = acc + jnp.dot(lhs_ref[f, 1], block[:, chan:], preferred_element_type=jnp.float32)
-        out_ref[0, f] = (acc * scale).reshape(2, chan, chan)
+def cross_kernel(scale, lhs_ref, rhs_ref, out_ref):
+    per_bin, rounds, rows, two_chan = rhs_ref.shape
+    chan = two_chan // 2
+    columns = []
+    for r in range(rounds):
+        block = rhs_ref[:, r].reshape(per_bin * rows, two_chan)
+        columns.append(jnp.concatenate([block[:, :chan], block[:, chan:]], axis=0))
+    rhs = jnp.concatenate(columns, axis=1)
+    acc = jnp.dot(lhs_ref[0], rhs, preferred_element_type=jnp.float32) * scale
+    for r in range(rounds):
+        out_ref[r, 0] = acc[:, r * chan:(r + 1) * chan].reshape(2, chan, chan)
 
 
 def cross_spectra(lhs, arrived, scale):
-    bins, _, two_chan, windows = lhs.shape
+    bins, two_chan, two_win = lhs.shape
     chan = two_chan // 2
     pieces, rounds, rows, _ = arrived.shape
+    per_bin = pieces // bins
     return pl.pallas_call(
-        functools.partial(cross_kernel, bins, scale),
-        grid=(rounds,),
+        functools.partial(cross_kernel, scale),
+        grid=(bins,),
         in_specs=[
-            pl.BlockSpec((bins, 2, two_chan, windows), lambda r: (0, 0, 0, 0)),
-            pl.BlockSpec((pieces, 1, rows, two_chan), lambda r: (0, r, 0, 0)),
+            pl.BlockSpec((1, two_chan, two_win), lambda f: (f, 0, 0)),
+            pl.BlockSpec((per_bin, rounds, rows, two_chan), lambda f: (f, 0, 0, 0)),
         ],
-        out_specs=pl.BlockSpec((1, bins, 2, chan, chan), lambda r: (r, 0, 0, 0, 0)),
+        out_specs=pl.BlockSpec((rounds, 1, 2, chan, chan), lambda f: (0, f, 0, 0, 0)),
         out_shape=jax.ShapeDtypeStruct((rounds, bins, 2, chan, chan), jnp.float32),
         cost_estimate=pl.CostEstimate(
-            flops=2 * rounds * bins * 2 * two_chan * windows * chan,
+            flops=2 * rounds * bins * two_chan * two_win * chan,
             bytes_accessed=lhs.size * 2 + arrived.size * 2 + rounds * bins * 2 * chan * chan * 4,
             transcendentals=0,
         ),
@@ -60,7 +62,7 @@
     send = rows.transpose(1, 2, 0, 3, 4).reshape(group_count * seg_count, win_piece, 2 * chan_width)
     held = lax.all_to_all(send, ("chan", "seg"), split_axis=0, concat_axis=0, tiled=True)
     held = held.reshape(group_count, seg_count * win_piece, 2 * chan_width)
-    outgoing = jnp.take(held, plan.T, axis=0)
+    outgoing = held.at[plan.T].get(mode="promise_in_bounds")
     arrived = lax.all_to_all(outgoing, "chan", split_axis=0, concat_axis=0, tiled=True)
     ranges = ordered.reshape(seg_count, my_bins, win_local, 2 * chan_width)
     by_shift = [lax.dynamic_index_in_dim(ranges, seg_index, 0, keepdims=False)]
@@ -72,10 +74,9 @@
     order = (seg_index - jnp.arange(seg_count)) % seg_count
     own = jnp.take(by_shift, order, axis=0)
     own = own.reshape(seg_count, my_bins, per_bin, win_piece, 2, chan_width)
-    own = own.transpose(1, 4, 5, 2, 0, 3).reshape(my_bins, 2, chan_width, win_count)
-    lhs_k0 = jnp.concatenate([own[:, 0], own[:, 1]], axis=1)
-    lhs_k1 = jnp.concatenate([own[:, 1], -own[:, 0]], axis=1)
-    lhs = jnp.stack([lhs_k0, lhs_k1], axis=1)
+    own = own.transpose(1, 5, 4, 2, 0, 3).reshape(my_bins, chan_width, 2, win_count)
+    imag_rows = jnp.stack([own[:, :, 1], -own[:, :, 0]], axis=2)
+    lhs = jnp.stack([own, imag_rows], axis=1).reshape(my_bins, 2 * chan_width, 2 * win_count)
     return cross_spectra(lhs, arrived, scale)
 
 

time: 107 us -> 106 us (level)
  local copies, waits for them, and re-layouts: 14 us -> 17.1 us
  waiting for transfers between devices: 58.8 us -> 55.8 us
  other arithmetic: 5.37 us -> 2.55 us
  Pallas kernels: 5.26 us -> 7.2 us
    all_to_all x1, waiting for transfers between devices: 26.5 us -> 23.4 us  [on_device(): lax.all_to_all(outgoing, 'chan', split_axis=0, concat_axis=0, tiled=True)]
    another operation x0 -> x1, local copies, waits for them, and re-layouts: none -> 2.82 us  [on_device(): jnp.stack([own, imag_rows], axis=1)]
    select_n x2 -> x1, other arithmetic: 2.75 us -> 0.01 us  [on_device(): outgoing = held.at[plan.T].get(mode='promise_in_bounds')]
    reshape x0 -> x1, local copies, waits for them, and re-layouts: none -> 2.52 us  [on_device(): jnp.stack([own, imag_rows], axis=1)]
    pallas_call x1, Pallas kernels: 5.26 us -> 7.2 us  [cross_spectra(): pl.pallas_call(functools.partial(cross_kernel, scale), grid=(bins,), in_s...]
    unnamed x8 -> x6, local copies, waits for them, and re-layouts: 3.06 us -> 1.68 us
  transfers between devices with their start and end apart: 5 -> 5, of which waited for: 4 -> 4; matrix products, arithmetic and copies ran while one was open for 9% -> 12% of each run, Pallas kernels for 0% -> 0%
where the time goes in v4:
time: 106 us
  waiting for transfers between devices  55.8 us (53%)
  starting transfers between devices  22.7 us (21%)
  local copies, waits for them, and re-layouts  17.1 us (16%)
  Pallas kernels  7.2 us (7%)
  other arithmetic  2.55 us (2%)
    all_to_all x1, waiting for transfers between devices, on_device(): lax.all_to_all(outgoing, 'chan', split_axis=0, concat_axis=0, tiled=True)  23.4 us
    all_to_all x1, waiting for transfers between devices, on_device(): lax.all_to_all(send, ('chan', 'seg'), split_axis=0, concat_axis=0, tiled=...  18.9 us
    all_to_all x1, starting transfers between devices, on_device(): lax.all_to_all(send, ('chan', 'seg'), split_axis=0, concat_axis=0, tiled=...  14.7 us
    ppermute x3, waiting for transfers between devices, on_device(): by_shift.append(lax.ppermute(part, 'seg', pairs))  13.5 us
    pallas_call x1, Pallas kernels, cross_spectra(): pl.pallas_call(functools.partial(cross_kernel, scale), grid=(bins,), in_s...  7.2 us
    all_to_all x1, starting transfers between devices, on_device(): lax.all_to_all(outgoing, 'chan', split_axis=0, concat_axis=0, tiled=True)  7.05 us
    another operation x1, local copies, waits for them, and re-layouts, on_device(): jnp.stack([own, imag_rows], axis=1)  2.82 us
    gather x2, local copies, waits for them, and re-layouts, on_device(): own = jnp.take(by_shift, order, axis=0)  2.53 us
  transfers between devices with their start and end apart: 5, of which 4 were waited for; matrix products, arithmetic and copies ran while one was open for 12% of the time, Pallas kernels for 0%

profile of v4, /device:TPU:2, one launch (start us, length us, event | category | flops | bytes accessed | tf_op | source)
XLA Modules:
  0.0 105.9 jit_solution(8949734854512732983)
XLA Ops:
  0.0 0.0 copy-start
  0.0 0.7 broadcast_subtract_fusion
  0.7 0.3 copy-done
  1.1 0.3 fusion
  1.4 0.0 copy-start.2
  1.4 0.5 copy.10
  1.9 0.3 reshape.78
  2.3 1.2 %copy.11 = bf16[8,8,4,4,256]{4,3,2,1,0:T(4,128)(2,1)} copy(bf16[8,8,4,4,256]{4,0,2,3,1:T(8,128)(2,1)S(1)} %bitcast.36) | data formatting | bytes 1048576 | tf_op jit(solution)/shard_map/transpose | solution.py:62
  3.5 14.7 %all-to-all-start = ((bf16[256,4,256]{2,1,0:T(4,128)(2,1)}), bf16[256,4,256]{2,1,0:T(4,128)(2,1)S(1)}, u32[]{:S(2)}, u32[]{:S(2)}) async-start(bf16[256,4,256]{2,1,0:T(4,128)(2,1)} %bitcast.15), calls=%async_computation | async-start | bytes 1048576 | tf_op jit(solution)/shard_map/all_to_all | solution.py:63
  18.2 0.0 copy-done.2
  18.2 0.1 copy.12
  18.3 0.1 reshape.91
  18.4 18.9 %all-to-all-done = bf16[256,4,256]{2,1,0:T(4,128)(2,1)S(1)} async-done(((bf16[256,4,256]{2,1,0:T(4,128)(2,1)}), bf16[256,4,256]{2,1,0:T(4,128)(2,1)S(1)}, u32[]{:S(2)}, u32[]{:S(2)}) %all-to-all-start) | async-done | bytes 524320 | tf_op jit(solution)/shard_map/all_to_all | solution.py:63
  37.3 0.1 reshape.80
  37.5 2.1 %gather_fusion.1 = bf16[256,16,256]{2,1,0:T(8,128)(2,1)} fusion(bf16[64,16,256]{2,1,0:T(8,128)(2,1)S(1)} %reshape.80, s32[1024]{0:T(1024)S(1)} %pad_clamp_fusion), kind=kCustom, calls=%fused_computation.1 | custom fusion | bytes 4195328 | tf_op jit(solution)/shard_map/gather | solution.py:65
  39.5 7.1 %all-to-all-start.1 = ((bf16[64,4,16,256]{3,2,1,0:T(8,128)(2,1)}), bf16[64,4,16,256]{3,2,1,0:T(8,128)(2,1)S(1)}, u32[]{:S(2)}, u32[]{:S(2)}) async-start(bf16[64,4,16,256]{3,2,1,0:T(8,128)(2,1)} %bitcast.33), calls=%async_computation.1 | async-start | bytes 4194304 | tf_op jit(solution)/shard_map/all_to_all | solution.py:66
  46.6 1.3 %copy.6 = bf16[32,32,2,128]{3,2,1,0:T(2,128)(2,1)} copy(bf16[32,32,2,128]{3,1,2,0:T(8,128)(2,1)S(1)} %fusion) | data formatting | bytes 1048576 | tf_op jit(solution)/shard_map/convert_element_type | solution.py:58
  48.0 1.4 %reshape.75 = bf16[4,8,32,256]{3,2,1,0:T(8,128)(2,1)S(1)} reshape(bf16[32,32,2,128]{3,2,1,0:T(2,128)(2,1)} %copy.6) | data formatting | bytes 1048576 | tf_op jit(solution)/shard_map/reshape | solution.py:67
  49.4 0.1 collective-permute-start.2
  49.5 0.8 collective-permute-start.1
  50.3 0.1 collective-permute-start
  50.5 6.3 %collective-permute-done.2 = bf16[8,32,256]{2,1,0:T(8,128)(2,1)S(1)} collective-permute-done((bf16[8,32,256]{2,1,0:T(8,128)(2,1)S(1)}, bf16[8,32,256]{2,1,0:T(8,128)(2,1)S(1)}, u32[]{:S(2)}, u32[]{:S(2)}) %collective-permute-start.2) | collective-permute-done | bytes 131104 | tf_op jit(solution)/shard_map/ppermute | solution.py:72
  56.7 7.2 %collective-permute-done.1 = bf16[8,32,256]{2,1,0:T(8,128)(2,1)S(1)} collective-permute-done((bf16[8,32,256]{2,1,0:T(8,128)(2,1)S(1)}, bf16[8,32,256]{2,1,0:T(8,128)(2,1)S(1)}, u32[]{:S(2)}, u32[]{:S(2)}) %collective-permute-start.1) | collective-permute-done | bytes 131104 | tf_op jit(solution)/shard_map/ppermute | solution.py:72
  63.9 0.0 collective-permute-done
  63.9 0.1 pad_maximum_fusion.1
  64.0 1.4 %gather_fusion = bf16[4,8,32,256]{3,2,1,0:T(8,128)(2,1)} fusion(bf16[4,8,32,256]{3,2,1,0:T(8,128)(2,1)S(1)} %pad_maximum_fusion.1, s32[1024]{0:T(1024)S(1)} %pad_clamp_fusion.1), kind=kCustom, calls=%fused_computation | custom fusion | bytes 1048592 | tf_op jit(solution)/shard_map/jit(_take)/gather | solution.py:75
  65.4 1.2 %gather.10 = bf16[4,8,8,4,2,128]{5,4,3,2,1,0:T(2,128)(2,1)S(1)} reshape(bf16[4,8,32,256]{3,2,1,0:T(8,128)(2,1)} %gather_fusion) | data formatting | bytes 1048576 | tf_op jit(solution)/shard_map/jit(_take)/gather | solution.py:75
  66.6 0.5 fusion.2
  67.1 0.3 copy.7
  67.4 0.1 fusion.9
  67.5 0.1 maximum_bitcast_fusion
  67.6 1.1 %pad_maximum_fusion = bf16[8,2,128,2,128]{2,0,4,3,1:T(8,128)(2,1)} fusion(bf16[8,1,128,2,128]{2,0,4,3,1:T(8,128)(2,1)S(1)} %maximum_bitcast_fusion, bf16[8,1,128,2,128]{2,0,4,3,1:T(8,128)(2,1)S(1)} %bitcast.35), kind=kLoop, calls=%fused_computation.4 | loop fusion | flops 524288 | bytes 2097152 | tf_op jit(solution)/shard_map/stack | solution.py:79
  68.6 2.8 %copy.9 = bf16[8,2,128,2,128]{4,3,2,1,0:T(2,128)(2,1)} copy(bf16[8,2,128,2,128]{2,0,4,3,1:T(8,128)(2,1)} %pad_maximum_fusion) | data formatting | bytes 2097152 | tf_op jit(solution)/shard_map/stack | solution.py:79
  71.5 2.5 %reshape.77.lhs_ref = bf16[8,256,256]{2,1,0:T(8,128)(2,1)} reshape(bf16[8,2,128,2,128]{4,3,2,1,0:T(2,128)(2,1)} %copy.9) | data formatting | bytes 2097152 | tf_op jit(solution)/shard_map/reshape | solution.py:79
  74.0 23.4 %all-to-all-done.1.rhs_ref = bf16[64,4,16,256]{3,2,1,0:T(8,128)(2,1)S(1)} async-done(((bf16[64,4,16,256]{3,2,1,0:T(8,128)(2,1)}), bf16[64,4,16,256]{3,2,1,0:T(8,128)(2,1)S(1)}, u32[]{:S(2)}, u32[]{:S(2)}) %all-to-all-start.1) | async-done | bytes 2097184 | tf_op jit(solution)/shard_map/all_to_all | solution.py:66
  97.4 0.0 copy-start.1
  97.4 1.3 %copy-done.1 = bf16[64,4,16,256]{3,2,1,0:T(8,128)(2,1)} copy-done((bf16[64,4,16,256]{3,2,1,0:T(8,128)(2,1)}, bf16[64,4,16,256]{3,2,1,0:T(8,128)(2,1)S(1)}, u32[]{:S(2)}) %copy-start.1) | copy-done | bytes 2097176
  98.7 7.2 %shard_map.37 = f32[4,8,2,128,128]{4,3,2,1,0:T(8,128)} custom-call(bf16[8,256,256]{2,1,0:T(8,128)(2,1)} %reshape.77.lhs_ref, bf16[64,4,16,256]{3,2,1,0:T(8,128)(2,1)} %copy-done.1), custom_call_target="tpu_custom_call" | custom-call | flops 536870912 | bytes 7340032 | tf_op jit(solution)/shard_map/pallas_call | solution.py:29
  (6 shorter events, 0.1 us)
Async XLA Ops:
  0.0 1.1 copy-start
  1.4 16.8 %copy-start.2 = (s32[4,64]{1,0:T(4,128)S(1)}, s32[4,64]{1,0:T(4,128)}, u32[]{:S(2)}) copy-start(s32[4,64]{1,0:T(4,128)} %param.4) | copy-start | bytes 3076
  3.5 33.9 %all-to-all-start = ((bf16[256,4,256]{2,1,0:T(4,128)(2,1)}), bf16[256,4,256]{2,1,0:T(4,128)(2,1)S(1)}, u32[]{:S(2)}, u32[]{:S(2)}) async-start(bf16[256,4,256]{2,1,0:T(4,128)(2,1)} %bitcast.15), calls=%async_computation | async-start | bytes 1048576 | tf_op jit(solution)/shard_map/all_to_all | solution.py:63
  39.5 57.8 %all-to-all-start.1 = ((bf16[64,4,16,256]{3,2,1,0:T(8,128)(2,1)}), bf16[64,4,16,256]{3,2,1,0:T(8,128)(2,1)S(1)}, u32[]{:S(2)}, u32[]{:S(2)}) async-start(bf16[64,4,16,256]{3,2,1,0:T(8,128)(2,1)} %bitcast.33), calls=%async_computation.1 | async-start | bytes 4194304 | tf_op jit(solution)/shard_map/all_to_all | solution.py:66
  49.4 7.3 %collective-permute-start.2 = (bf16[8,32,256]{2,1,0:T(8,128)(2,1)S(1)}, bf16[8,32,256]{2,1,0:T(8,128)(2,1)S(1)}, u32[]{:S(2)}, u32[]{:S(2)}) collective-permute-start(bf16[8,32,256]{2,1,0:T(8,128)(2,1)S(1)} %get-tuple-element.8), channel_id=1, source_target_pairs={{0,3},{1,0},{2,1},{3,2},{4,7},{5,4},{6,5},{7,6},{8,11},{9,8},{10,9... | collective-permute-start | bytes 393224 | tf_op jit(solution)/shard_map/ppermute | solution.py:72
  49.5 14.4 %collective-permute-start.1 = (bf16[8,32,256]{2,1,0:T(8,128)(2,1)S(1)}, bf16[8,32,256]{2,1,0:T(8,128)(2,1)S(1)}, u32[]{:S(2)}, u32[]{:S(2)}) collective-permute-start(bf16[8,32,256]{2,1,0:T(8,128)(2,1)S(1)} %get-tuple-element.9), channel_id=1, source_target_pairs={{0,2},{1,3},{2,0},{3,1},{4,6},{5,7},{6,4},{7,5},{8,10},{9,11},{10,... | collective-permute-start | bytes 393224 | tf_op jit(solution)/shard_map/ppermute | solution.py:72
  50.3 13.7 %collective-permute-start = (bf16[8,32,256]{2,1,0:T(8,128)(2,1)S(1)}, bf16[8,32,256]{2,1,0:T(8,128)(2,1)S(1)}, u32[]{:S(2)}, u32[]{:S(2)}) collective-permute-start(bf16[8,32,256]{2,1,0:T(8,128)(2,1)S(1)} %get-tuple-element.10), channel_id=1, source_target_pairs={{0,1},{1,2},{2,3},{3,0},{4,5},{5,6},{6,7},{7,4},{8,9},{9,10},{10,1... | collective-permute-start | bytes 393224 | tf_op jit(solution)/shard_map/ppermute | solution.py:72
  97.4 1.3 %copy-start.1 = (bf16[64,4,16,256]{3,2,1,0:T(8,128)(2,1)}, bf16[64,4,16,256]{3,2,1,0:T(8,128)(2,1)S(1)}, u32[]{:S(2)}) copy-start(bf16[64,4,16,256]{3,2,1,0:T(8,128)(2,1)S(1)} %all-to-all-done.1.rhs_ref) | copy-start | bytes 6291460

commit v5 on v3

--- a/solution.py
+++ b/solution.py
@@ -65,13 +65,9 @@
     win_piece = win_local // per_bin
     rows = ordered.reshape(seg_count, my_bins, per_bin, win_piece, 2 * chan_width)
     send = rows.transpose(1, 2, 0, 3, 4).reshape(group_count * seg_count, win_piece, 2 * chan_width)
-    round_count = plan.shape[0]
     held = lax.all_to_all(send, ("chan", "seg"), split_axis=0, concat_axis=0, tiled=True)
     held = held.reshape(group_count, seg_count * win_piece, 2 * chan_width)
-    pick = plan.T.reshape(-1)[:, None] == jnp.arange(group_count, dtype=plan.dtype)[None, :]
-    outgoing = jnp.dot(
-        pick.astype(held.dtype), held.reshape(group_count, -1), preferred_element_type=jnp.float32
-    ).astype(held.dtype).reshape(group_count, round_count, seg_count * win_piece, 2 * chan_width)
+    outgoing = held.at[plan.T].get(mode="promise_in_bounds")
     arrived = lax.all_to_all(outgoing, "chan", split_axis=0, concat_axis=0, tiled=True)
     ranges = ordered.reshape(seg_count, my_bins, win_local, 2 * chan_width)
     by_shift = [lax.dynamic_index_in_dim(ranges, seg_index, 0, keepdims=False)]

time: 107 us -> 104 us (0.972)
  matrix products: 2.07 us -> 0.29 us
    gather x0 -> x1, local copies, waits for them, and re-layouts: none -> 2.07 us  [on_device(): outgoing = held.at[plan.T].get(mode='promise_in_bounds')]
    unnamed x7 -> x6, local copies, waits for them, and re-layouts: 3.65 us -> 1.68 us
    dot_general x1 -> x0, matrix products: 1.78 us -> none  [on_device(): jnp.dot(pick.astype(held.dtype), held.reshape(group_count, -1), preferred...]
    another operation x1 -> x0, local copies, waits for them, and re-layouts: 1.17 us -> none  [on_device(): held.reshape(group_count, -1)]
  transfers between devices with their start and end apart: 5 -> 5, of which waited for: 4 -> 4; matrix products, arithmetic and copies ran while one was open for 12% -> 13% of each run, Pallas kernels for 0% -> 0%
where the time goes in v5:
time: 104 us
  waiting for transfers between devices  55.8 us (54%)
  starting transfers between devices  22.7 us (22%)
  local copies, waits for them, and re-layouts  17.1 us (16%)
  Pallas kernels  5.14 us (5%)
  other arithmetic  2.55 us (2%)
    all_to_all x1, waiting for transfers between devices, on_device(): lax.all_to_all(outgoing, 'chan', split_axis=0, concat_axis=0, tiled=True)  23.4 us
    all_to_all x1, waiting for transfers between devices, on_device(): lax.all_to_all(send, ('chan', 'seg'), split_axis=0, concat_axis=0, tiled=...  18.9 us
    all_to_all x1, starting transfers between devices, on_device(): lax.all_to_all(send, ('chan', 'seg'), split_axis=0, concat_axis=0, tiled=...  14.7 us
    ppermute x3, waiting for transfers between devices, on_device(): by_shift.append(lax.ppermute(part, 'seg', pairs))  13.5 us
    all_to_all x1, starting transfers between devices, on_device(): lax.all_to_all(outgoing, 'chan', split_axis=0, concat_axis=0, tiled=True)  7.05 us
    pallas_call x1, Pallas kernels, cross_spectra(): pl.pallas_call(functools.partial(cross_kernel, bins_per_step, scale), gri...  5.14 us
    another operation x1, local copies, waits for them, and re-layouts, on_device(): jnp.stack([own, imag_rows], axis=1)  2.82 us
    gather x2, local copies, waits for them, and re-layouts, on_device(): own = jnp.take(by_shift, order, axis=0)  2.53 us
  transfers between devices with their start and end apart: 5, of which 4 were waited for; matrix products, arithmetic and copies ran while one was open for 13% of the time, Pallas kernels for 0%

profile of v5, /device:TPU:2, one launch (start us, length us, event | category | flops | bytes accessed | tf_op | source)
XLA Modules:
  0.0 103.8 jit_solution(3485556361906813752)
XLA Ops:
  0.0 0.0 copy-start
  0.0 0.7 broadcast_subtract_fusion
  0.7 0.3 copy-done
  1.1 0.3 fusion
  1.4 0.0 copy-start.2
  1.4 0.5 copy.10
  1.9 0.3 reshape.78
  2.3 1.2 %copy.11 = bf16[8,8,4,4,256]{4,3,2,1,0:T(4,128)(2,1)} copy(bf16[8,8,4,4,256]{4,0,2,3,1:T(8,128)(2,1)S(1)} %bitcast.36) | data formatting | bytes 1048576 | tf_op jit(solution)/shard_map/transpose | solution.py:67
  3.5 14.7 %all-to-all-start = ((bf16[256,4,256]{2,1,0:T(4,128)(2,1)}), bf16[256,4,256]{2,1,0:T(4,128)(2,1)S(1)}, u32[]{:S(2)}, u32[]{:S(2)}) async-start(bf16[256,4,256]{2,1,0:T(4,128)(2,1)} %bitcast.15), calls=%async_computation | async-start | bytes 1048576 | tf_op jit(solution)/shard_map/all_to_all | solution.py:68
  18.2 0.0 copy-done.2
  18.2 0.1 copy.12
  18.3 0.1 reshape.91
  18.4 18.9 %all-to-all-done = bf16[256,4,256]{2,1,0:T(4,128)(2,1)S(1)} async-done(((bf16[256,4,256]{2,1,0:T(4,128)(2,1)}), bf16[256,4,256]{2,1,0:T(4,128)(2,1)S(1)}, u32[]{:S(2)}, u32[]{:S(2)}) %all-to-all-start) | async-done | bytes 524320 | tf_op jit(solution)/shard_map/all_to_all | solution.py:68
  37.3 0.1 reshape.80
  37.5 2.1 %gather_fusion.1 = bf16[256,16,256]{2,1,0:T(8,128)(2,1)} fusion(bf16[64,16,256]{2,1,0:T(8,128)(2,1)S(1)} %reshape.80, s32[1024]{0:T(1024)S(1)} %pad_clamp_fusion), kind=kCustom, calls=%fused_computation.1 | custom fusion | bytes 4195328 | tf_op jit(solution)/shard_map/gather | solution.py:70
  39.5 7.1 %all-to-all-start.1 = ((bf16[64,4,16,256]{3,2,1,0:T(8,128)(2,1)}), bf16[64,4,16,256]{3,2,1,0:T(8,128)(2,1)S(1)}, u32[]{:S(2)}, u32[]{:S(2)}) async-start(bf16[64,4,16,256]{3,2,1,0:T(8,128)(2,1)} %bitcast.33), calls=%async_computation.1 | async-start | bytes 4194304 | tf_op jit(solution)/shard_map/all_to_all | solution.py:71
  46.6 1.3 %copy.6 = bf16[32,32,2,128]{3,2,1,0:T(2,128)(2,1)} copy(bf16[32,32,2,128]{3,1,2,0:T(8,128)(2,1)S(1)} %fusion) | data formatting | bytes 1048576 | tf_op jit(solution)/shard_map/convert_element_type | solution.py:63
  48.0 1.4 %reshape.75 = bf16[4,8,32,256]{3,2,1,0:T(8,128)(2,1)S(1)} reshape(bf16[32,32,2,128]{3,2,1,0:T(2,128)(2,1)} %copy.6) | data formatting | bytes 1048576 | tf_op jit(solution)/shard_map/reshape | solution.py:72
  49.4 0.1 collective-permute-start.2
  49.5 0.8 collective-permute-start.1
  50.3 0.1 collective-permute-start
  50.5 6.3 %collective-permute-done.2 = bf16[8,32,256]{2,1,0:T(8,128)(2,1)S(1)} collective-permute-done((bf16[8,32,256]{2,1,0:T(8,128)(2,1)S(1)}, bf16[8,32,256]{2,1,0:T(8,128)(2,1)S(1)}, u32[]{:S(2)}, u32[]{:S(2)}) %collective-permute-start.2) | collective-permute-done | bytes 131104 | tf_op jit(solution)/shard_map/ppermute | solution.py:77
  56.7 7.2 %collective-permute-done.1 = bf16[8,32,256]{2,1,0:T(8,128)(2,1)S(1)} collective-permute-done((bf16[8,32,256]{2,1,0:T(8,128)(2,1)S(1)}, bf16[8,32,256]{2,1,0:T(8,128)(2,1)S(1)}, u32[]{:S(2)}, u32[]{:S(2)}) %collective-permute-start.1) | collective-permute-done | bytes 131104 | tf_op jit(solution)/shard_map/ppermute | solution.py:77
  63.9 0.0 collective-permute-done
  63.9 0.1 pad_maximum_fusion.1
  64.0 1.4 %gather_fusion = bf16[4,8,32,256]{3,2,1,0:T(8,128)(2,1)} fusion(bf16[4,8,32,256]{3,2,1,0:T(8,128)(2,1)S(1)} %pad_maximum_fusion.1, s32[1024]{0:T(1024)S(1)} %pad_clamp_fusion.1), kind=kCustom, calls=%fused_computation | custom fusion | bytes 1048592 | tf_op jit(solution)/shard_map/jit(_take)/gather | solution.py:80
  65.4 1.2 %gather.10 = bf16[4,8,8,4,2,128]{5,4,3,2,1,0:T(2,128)(2,1)S(1)} reshape(bf16[4,8,32,256]{3,2,1,0:T(8,128)(2,1)} %gather_fusion) | data formatting | bytes 1048576 | tf_op jit(solution)/shard_map/jit(_take)/gather | solution.py:80
  66.6 0.5 fusion.2
  67.1 0.3 copy.7
  67.4 0.1 fusion.9
  67.5 0.1 maximum_bitcast_fusion
  67.6 1.1 %pad_maximum_fusion = bf16[8,2,128,2,128]{2,0,4,3,1:T(8,128)(2,1)} fusion(bf16[8,1,128,2,128]{2,0,4,3,1:T(8,128)(2,1)S(1)} %maximum_bitcast_fusion, bf16[8,1,128,2,128]{2,0,4,3,1:T(8,128)(2,1)S(1)} %bitcast.35), kind=kLoop, calls=%fused_computation.4 | loop fusion | flops 524288 | bytes 2097152 | tf_op jit(solution)/shard_map/stack | solution.py:84
  68.6 2.8 %copy.9 = bf16[8,2,128,2,128]{4,3,2,1,0:T(2,128)(2,1)} copy(bf16[8,2,128,2,128]{2,0,4,3,1:T(8,128)(2,1)} %pad_maximum_fusion) | data formatting | bytes 2097152 | tf_op jit(solution)/shard_map/stack | solution.py:84
  71.5 2.5 %reshape.77.lhs_ref = bf16[8,256,256]{2,1,0:T(8,128)(2,1)} reshape(bf16[8,2,128,2,128]{4,3,2,1,0:T(2,128)(2,1)} %copy.9) | data formatting | bytes 2097152 | tf_op jit(solution)/shard_map/reshape | solution.py:84
  74.0 23.4 %all-to-all-done.1.rhs_ref = bf16[64,4,16,256]{3,2,1,0:T(8,128)(2,1)S(1)} async-done(((bf16[64,4,16,256]{3,2,1,0:T(8,128)(2,1)}), bf16[64,4,16,256]{3,2,1,0:T(8,128)(2,1)S(1)}, u32[]{:S(2)}, u32[]{:S(2)}) %all-to-all-start.1) | async-done | bytes 2097184 | tf_op jit(solution)/shard_map/all_to_all | solution.py:71
  97.4 0.0 copy-start.1
  97.4 1.3 %copy-done.1 = bf16[64,4,16,256]{3,2,1,0:T(8,128)(2,1)} copy-done((bf16[64,4,16,256]{3,2,1,0:T(8,128)(2,1)}, bf16[64,4,16,256]{3,2,1,0:T(8,128)(2,1)S(1)}, u32[]{:S(2)}) %copy-start.1) | copy-done | bytes 2097176
  98.7 5.1 %shard_map.37 = f32[4,8,2,128,128]{4,3,2,1,0:T(8,128)} custom-call(bf16[8,256,256]{2,1,0:T(8,128)(2,1)} %reshape.77.lhs_ref, bf16[64,4,16,256]{3,2,1,0:T(8,128)(2,1)} %copy-done.1), custom_call_target="tpu_custom_call" | custom-call | flops 536870912 | bytes 7340032 | tf_op jit(solution)/shard_map/pallas_call | solution.py:34
  (6 shorter events, 0.1 us)
Async XLA Ops:
  0.0 1.1 %copy-start = (bf16[32,32,2,128]{3,2,1,0:T(2,128)(2,1)S(1)}, bf16[32,32,2,128]{3,2,1,0:T(2,128)(2,1)}, u32[]{:S(2)}) copy-start(bf16[32,32,2,128]{3,2,1,0:T(2,128)(2,1)} %param.3) | copy-start | bytes 1572868
  1.4 16.8 %copy-start.2 = (s32[4,64]{1,0:T(4,128)S(1)}, s32[4,64]{1,0:T(4,128)}, u32[]{:S(2)}) copy-start(s32[4,64]{1,0:T(4,128)} %param.4) | copy-start | bytes 3076
  3.5 33.9 %all-to-all-start = ((bf16[256,4,256]{2,1,0:T(4,128)(2,1)}), bf16[256,4,256]{2,1,0:T(4,128)(2,1)S(1)}, u32[]{:S(2)}, u32[]{:S(2)}) async-start(bf16[256,4,256]{2,1,0:T(4,128)(2,1)} %bitcast.15), calls=%async_computation | async-start | bytes 1048576 | tf_op jit(solution)/shard_map/all_to_all | solution.py:68
  39.5 57.8 %all-to-all-start.1 = ((bf16[64,4,16,256]{3,2,1,0:T(8,128)(2,1)}), bf16[64,4,16,256]{3,2,1,0:T(8,128)(2,1)S(1)}, u32[]{:S(2)}, u32[]{:S(2)}) async-start(bf16[64,4,16,256]{3,2,1,0:T(8,128)(2,1)} %bitcast.33), calls=%async_computation.1 | async-start | bytes 4194304 | tf_op jit(solution)/shard_map/all_to_all | solution.py:71
  49.4 7.3 %collective-permute-start.2 = (bf16[8,32,256]{2,1,0:T(8,128)(2,1)S(1)}, bf16[8,32,256]{2,1,0:T(8,128)(2,1)S(1)}, u32[]{:S(2)}, u32[]{:S(2)}) collective-permute-start(bf16[8,32,256]{2,1,0:T(8,128)(2,1)S(1)} %get-tuple-element.8), channel_id=1, source_target_pairs={{0,3},{1,0},{2,1},{3,2},{4,7},{5,4},{6,5},{7,6},{8,11},{9,8},{10,9... | collective-permute-start | bytes 393224 | tf_op jit(solution)/shard_map/ppermute | solution.py:77
  49.5 14.4 %collective-permute-start.1 = (bf16[8,32,256]{2,1,0:T(8,128)(2,1)S(1)}, bf16[8,32,256]{2,1,0:T(8,128)(2,1)S(1)}, u32[]{:S(2)}, u32[]{:S(2)}) collective-permute-start(bf16[8,32,256]{2,1,0:T(8,128)(2,1)S(1)} %get-tuple-element.9), channel_id=1, source_target_pairs={{0,2},{1,3},{2,0},{3,1},{4,6},{5,7},{6,4},{7,5},{8,10},{9,11},{10,... | collective-permute-start | bytes 393224 | tf_op jit(solution)/shard_map/ppermute | solution.py:77
  50.3 13.7 %collective-permute-start = (bf16[8,32,256]{2,1,0:T(8,128)(2,1)S(1)}, bf16[8,32,256]{2,1,0:T(8,128)(2,1)S(1)}, u32[]{:S(2)}, u32[]{:S(2)}) collective-permute-start(bf16[8,32,256]{2,1,0:T(8,128)(2,1)S(1)} %get-tuple-element.10), channel_id=1, source_target_pairs={{0,1},{1,2},{2,3},{3,0},{4,5},{5,6},{6,7},{7,4},{8,9},{9,10},{10,1... | collective-permute-start | bytes 393224 | tf_op jit(solution)/shard_map/ppermute | solution.py:77
  97.4 1.3 %copy-start.1 = (bf16[64,4,16,256]{3,2,1,0:T(8,128)(2,1)}, bf16[64,4,16,256]{3,2,1,0:T(8,128)(2,1)S(1)}, u32[]{:S(2)}) copy-start(bf16[64,4,16,256]{3,2,1,0:T(8,128)(2,1)S(1)} %all-to-all-done.1.rhs_ref) | copy-start | bytes 6291460

commit v6 on v4

--- a/solution.py
+++ b/solution.py
@@ -9,16 +9,17 @@
 
 
 def cross_kernel(scale, lhs_ref, rhs_ref, out_ref):
-    per_bin, rounds, rows, two_chan = rhs_ref.shape
+    step_bins = lhs_ref.shape[0]
+    pieces, rounds, rows, two_chan = rhs_ref.shape
+    per_bin = pieces // step_bins
     chan = two_chan // 2
-    columns = []
-    for r in range(rounds):
-        block = rhs_ref[:, r].reshape(per_bin * rows, two_chan)
-        columns.append(jnp.concatenate([block[:, :chan], block[:, chan:]], axis=0))
-    rhs = jnp.concatenate(columns, axis=1)
-    acc = jnp.dot(lhs_ref[0], rhs, preferred_element_type=jnp.float32) * scale
-    for r in range(rounds):
-        out_ref[r, 0] = acc[:, r * chan:(r + 1) * chan].reshape(2, chan, chan)
+    for b in range(step_bins):
+        lhs = lhs_ref[b]
+        for r in range(rounds):
+            block = rhs_ref[b * per_bin:(b + 1) * per_bin, r].reshape(per_bin * rows, two_chan)
+            block = jnp.concatenate([block[:, :chan], block[:, chan:]], axis=0)
+            acc = jnp.dot(lhs, block, preferred_element_type=jnp.float32)
+            out_ref[r, b] = (acc * scale).reshape(2, chan, chan)
 
 
 def cross_spectra(lhs, arrived, scale):
@@ -26,14 +27,15 @@
     chan = two_chan // 2
     pieces, rounds, rows, _ = arrived.shape
     per_bin = pieces // bins
+    step_bins = 4
     return pl.pallas_call(
         functools.partial(cross_kernel, scale),
-        grid=(bins,),
+        grid=(bins // step_bins,),
         in_specs=[
-            pl.BlockSpec((1, two_chan, two_win), lambda f: (f, 0, 0)),
-            pl.BlockSpec((per_bin, rounds, rows, two_chan), lambda f: (f, 0, 0, 0)),
+            pl.BlockSpec((step_bins, two_chan, two_win), lambda g: (g, 0, 0)),
+            pl.BlockSpec((step_bins * per_bin, rounds, rows, two_chan), lambda g: (g, 0, 0, 0)),
         ],
-        out_specs=pl.BlockSpec((rounds, 1, 2, chan, chan), lambda f: (0, f, 0, 0, 0)),
+        out_specs=pl.BlockSpec((rounds, step_bins, 2, chan, chan), lambda g: (0, g, 0, 0, 0)),
         out_shape=jax.ShapeDtypeStruct((rounds, bins, 2, chan, chan), jnp.float32),
         cost_estimate=pl.CostEstimate(
             flops=2 * rounds * bins * two_chan * two_win * chan,

time: 106 us -> 103 us (0.972)
  Pallas kernels: 7.2 us -> 4.12 us
    pallas_call x1, Pallas kernels: 7.2 us -> 4.12 us  [cross_spectra(): pl.pallas_call(functools.partial(cross_kernel, scale), grid=(bins // step...]
  transfers between devices with their start and end apart: 5 -> 5, of which waited for: 4 -> 4; matrix products, arithmetic and copies ran while one was open for 12% -> 13% of each run, Pallas kernels for 0% -> 0%
where the time goes in v6:
time: 103 us
  waiting for transfers between devices  55.8 us (54%)
  starting transfers between devices  22.7 us (22%)
  local copies, waits for them, and re-layouts  17.1 us (17%)
  Pallas kernels  4.12 us (4%)
  other arithmetic  2.55 us (2%)
    all_to_all x1, waiting for transfers between devices, on_device(): lax.all_to_all(outgoing, 'chan', split_axis=0, concat_axis=0, tiled=True)  23.4 us
    all_to_all x1, waiting for transfers between devices, on_device(): lax.all_to_all(send, ('chan', 'seg'), split_axis=0, concat_axis=0, tiled=...  18.9 us
    all_to_all x1, starting transfers between devices, on_device(): lax.all_to_all(send, ('chan', 'seg'), split_axis=0, concat_axis=0, tiled=...  14.7 us
    ppermute x3, waiting for transfers between devices, on_device(): by_shift.append(lax.ppermute(part, 'seg', pairs))  13.5 us
    all_to_all x1, starting transfers between devices, on_device(): lax.all_to_all(outgoing, 'chan', split_axis=0, concat_axis=0, tiled=True)  7.05 us
    pallas_call x1, Pallas kernels, cross_spectra(): pl.pallas_call(functools.partial(cross_kernel, scale), grid=(bins // step...  4.12 us
    another operation x1, local copies, waits for them, and re-layouts, on_device(): jnp.stack([own, imag_rows], axis=1)  2.82 us
    gather x2, local copies, waits for them, and re-layouts, on_device(): own = jnp.take(by_shift, order, axis=0)  2.53 us
  transfers between devices with their start and end apart: 5, of which 4 were waited for; matrix products, arithmetic and copies ran while one was open for 13% of the time, Pallas kernels for 0%

profile of v6, /device:TPU:2, one launch (start us, length us, event | category | flops | bytes accessed | tf_op | source)
XLA Modules:
  0.0 102.8 jit_solution(12474500620901057254)
XLA Ops:
  0.0 0.0 copy-start
  0.0 0.7 broadcast_subtract_fusion
  0.7 0.3 copy-done
  1.1 0.3 fusion
  1.4 0.0 copy-start.2
  1.4 0.5 copy.10
  1.9 0.3 reshape.78
  2.3 1.2 %copy.11 = bf16[8,8,4,4,256]{4,3,2,1,0:T(4,128)(2,1)} copy(bf16[8,8,4,4,256]{4,0,2,3,1:T(8,128)(2,1)S(1)} %bitcast.36) | data formatting | bytes 1048576 | tf_op jit(solution)/shard_map/transpose | solution.py:64
  3.5 14.7 %all-to-all-start = ((bf16[256,4,256]{2,1,0:T(4,128)(2,1)}), bf16[256,4,256]{2,1,0:T(4,128)(2,1)S(1)}, u32[]{:S(2)}, u32[]{:S(2)}) async-start(bf16[256,4,256]{2,1,0:T(4,128)(2,1)} %bitcast.15), calls=%async_computation | async-start | bytes 1048576 | tf_op jit(solution)/shard_map/all_to_all | solution.py:65
  18.2 0.0 copy-done.2
  18.2 0.1 copy.12
  18.3 0.1 reshape.91
  18.4 18.9 %all-to-all-done = bf16[256,4,256]{2,1,0:T(4,128)(2,1)S(1)} async-done(((bf16[256,4,256]{2,1,0:T(4,128)(2,1)}), bf16[256,4,256]{2,1,0:T(4,128)(2,1)S(1)}, u32[]{:S(2)}, u32[]{:S(2)}) %all-to-all-start) | async-done | bytes 524320 | tf_op jit(solution)/shard_map/all_to_all | solution.py:65
  37.3 0.1 reshape.80
  37.5 2.1 %gather_fusion.1 = bf16[256,16,256]{2,1,0:T(8,128)(2,1)} fusion(bf16[64,16,256]{2,1,0:T(8,128)(2,1)S(1)} %reshape.80, s32[1024]{0:T(1024)S(1)} %pad_clamp_fusion), kind=kCustom, calls=%fused_computation.1 | custom fusion | bytes 4195328 | tf_op jit(solution)/shard_map/gather | solution.py:67
  39.5 7.1 %all-to-all-start.1 = ((bf16[64,4,16,256]{3,2,1,0:T(8,128)(2,1)}), bf16[64,4,16,256]{3,2,1,0:T(8,128)(2,1)S(1)}, u32[]{:S(2)}, u32[]{:S(2)}) async-start(bf16[64,4,16,256]{3,2,1,0:T(8,128)(2,1)} %bitcast.33), calls=%async_computation.1 | async-start | bytes 4194304 | tf_op jit(solution)/shard_map/all_to_all | solution.py:68
  46.6 1.3 %copy.6 = bf16[32,32,2,128]{3,2,1,0:T(2,128)(2,1)} copy(bf16[32,32,2,128]{3,1,2,0:T(8,128)(2,1)S(1)} %fusion) | data formatting | bytes 1048576 | tf_op jit(solution)/shard_map/convert_element_type | solution.py:60
  48.0 1.4 %reshape.75 = bf16[4,8,32,256]{3,2,1,0:T(8,128)(2,1)S(1)} reshape(bf16[32,32,2,128]{3,2,1,0:T(2,128)(2,1)} %copy.6) | data formatting | bytes 1048576 | tf_op jit(solution)/shard_map/reshape | solution.py:69
  49.4 0.1 collective-permute-start.2
  49.5 0.8 collective-permute-start.1
  50.3 0.1 collective-permute-start
  50.5 6.3 %collective-permute-done.2 = bf16[8,32,256]{2,1,0:T(8,128)(2,1)S(1)} collective-permute-done((bf16[8,32,256]{2,1,0:T(8,128)(2,1)S(1)}, bf16[8,32,256]{2,1,0:T(8,128)(2,1)S(1)}, u32[]{:S(2)}, u32[]{:S(2)}) %collective-permute-start.2) | collective-permute-done | bytes 131104 | tf_op jit(solution)/shard_map/ppermute | solution.py:74
  56.7 7.2 %collective-permute-done.1 = bf16[8,32,256]{2,1,0:T(8,128)(2,1)S(1)} collective-permute-done((bf16[8,32,256]{2,1,0:T(8,128)(2,1)S(1)}, bf16[8,32,256]{2,1,0:T(8,128)(2,1)S(1)}, u32[]{:S(2)}, u32[]{:S(2)}) %collective-permute-start.1) | collective-permute-done | bytes 131104 | tf_op jit(solution)/shard_map/ppermute | solution.py:74
  63.9 0.0 collective-permute-done
  63.9 0.1 pad_maximum_fusion.1
  64.0 1.4 %gather_fusion = bf16[4,8,32,256]{3,2,1,0:T(8,128)(2,1)} fusion(bf16[4,8,32,256]{3,2,1,0:T(8,128)(2,1)S(1)} %pad_maximum_fusion.1, s32[1024]{0:T(1024)S(1)} %pad_clamp_fusion.1), kind=kCustom, calls=%fused_computation | custom fusion | bytes 1048592 | tf_op jit(solution)/shard_map/jit(_take)/gather | solution.py:77
  65.4 1.2 %gather.10 = bf16[4,8,8,4,2,128]{5,4,3,2,1,0:T(2,128)(2,1)S(1)} reshape(bf16[4,8,32,256]{3,2,1,0:T(8,128)(2,1)} %gather_fusion) | data formatting | bytes 1048576 | tf_op jit(solution)/shard_map/jit(_take)/gather | solution.py:77
  66.6 0.5 fusion.2
  67.1 0.3 copy.7
  67.4 0.1 fusion.9
  67.5 0.1 maximum_bitcast_fusion
  67.6 1.1 %pad_maximum_fusion = bf16[8,2,128,2,128]{2,0,4,3,1:T(8,128)(2,1)} fusion(bf16[8,1,128,2,128]{2,0,4,3,1:T(8,128)(2,1)S(1)} %maximum_bitcast_fusion, bf16[8,1,128,2,128]{2,0,4,3,1:T(8,128)(2,1)S(1)} %bitcast.35), kind=kLoop, calls=%fused_computation.4 | loop fusion | flops 524288 | bytes 2097152 | tf_op jit(solution)/shard_map/stack | solution.py:81
  68.6 2.8 %copy.9 = bf16[8,2,128,2,128]{4,3,2,1,0:T(2,128)(2,1)} copy(bf16[8,2,128,2,128]{2,0,4,3,1:T(8,128)(2,1)} %pad_maximum_fusion) | data formatting | bytes 2097152 | tf_op jit(solution)/shard_map/stack | solution.py:81
  71.5 2.5 %reshape.77.lhs_ref = bf16[8,256,256]{2,1,0:T(8,128)(2,1)} reshape(bf16[8,2,128,2,128]{4,3,2,1,0:T(2,128)(2,1)} %copy.9) | data formatting | bytes 2097152 | tf_op jit(solution)/shard_map/reshape | solution.py:81
  74.0 23.4 %all-to-all-done.1.rhs_ref = bf16[64,4,16,256]{3,2,1,0:T(8,128)(2,1)S(1)} async-done(((bf16[64,4,16,256]{3,2,1,0:T(8,128)(2,1)}), bf16[64,4,16,256]{3,2,1,0:T(8,128)(2,1)S(1)}, u32[]{:S(2)}, u32[]{:S(2)}) %all-to-all-start.1) | async-done | bytes 2097184 | tf_op jit(solution)/shard_map/all_to_all | solution.py:68
  97.4 0.0 copy-start.1
  97.4 1.3 %copy-done.1 = bf16[64,4,16,256]{3,2,1,0:T(8,128)(2,1)} copy-done((bf16[64,4,16,256]{3,2,1,0:T(8,128)(2,1)}, bf16[64,4,16,256]{3,2,1,0:T(8,128)(2,1)S(1)}, u32[]{:S(2)}) %copy-start.1) | copy-done | bytes 2097176
  98.7 4.1 %shard_map.37 = f32[4,8,2,128,128]{4,3,2,1,0:T(8,128)} custom-call(bf16[8,256,256]{2,1,0:T(8,128)(2,1)} %reshape.77.lhs_ref, bf16[64,4,16,256]{3,2,1,0:T(8,128)(2,1)} %copy-done.1), custom_call_target="tpu_custom_call" | custom-call | flops 536870912 | bytes 7340032 | tf_op jit(solution)/shard_map/pallas_call | solution.py:31
  (6 shorter events, 0.1 us)
Async XLA Ops:
  0.0 1.1 %copy-start = (bf16[32,32,2,128]{3,2,1,0:T(2,128)(2,1)S(1)}, bf16[32,32,2,128]{3,2,1,0:T(2,128)(2,1)}, u32[]{:S(2)}) copy-start(bf16[32,32,2,128]{3,2,1,0:T(2,128)(2,1)} %param.3) | copy-start | bytes 1572868
  1.4 16.8 %copy-start.2 = (s32[4,64]{1,0:T(4,128)S(1)}, s32[4,64]{1,0:T(4,128)}, u32[]{:S(2)}) copy-start(s32[4,64]{1,0:T(4,128)} %param.4) | copy-start | bytes 3076
  3.5 33.9 %all-to-all-start = ((bf16[256,4,256]{2,1,0:T(4,128)(2,1)}), bf16[256,4,256]{2,1,0:T(4,128)(2,1)S(1)}, u32[]{:S(2)}, u32[]{:S(2)}) async-start(bf16[256,4,256]{2,1,0:T(4,128)(2,1)} %bitcast.15), calls=%async_computation | async-start | bytes 1048576 | tf_op jit(solution)/shard_map/all_to_all | solution.py:65
  39.5 57.8 %all-to-all-start.1 = ((bf16[64,4,16,256]{3,2,1,0:T(8,128)(2,1)}), bf16[64,4,16,256]{3,2,1,0:T(8,128)(2,1)S(1)}, u32[]{:S(2)}, u32[]{:S(2)}) async-start(bf16[64,4,16,256]{3,2,1,0:T(8,128)(2,1)} %bitcast.33), calls=%async_computation.1 | async-start | bytes 4194304 | tf_op jit(solution)/shard_map/all_to_all | solution.py:68
  49.4 7.3 %collective-permute-start.2 = (bf16[8,32,256]{2,1,0:T(8,128)(2,1)S(1)}, bf16[8,32,256]{2,1,0:T(8,128)(2,1)S(1)}, u32[]{:S(2)}, u32[]{:S(2)}) collective-permute-start(bf16[8,32,256]{2,1,0:T(8,128)(2,1)S(1)} %get-tuple-element.8), channel_id=1, source_target_pairs={{0,3},{1,0},{2,1},{3,2},{4,7},{5,4},{6,5},{7,6},{8,11},{9,8},{10,9... | collective-permute-start | bytes 393224 | tf_op jit(solution)/shard_map/ppermute | solution.py:74
  49.5 14.4 %collective-permute-start.1 = (bf16[8,32,256]{2,1,0:T(8,128)(2,1)S(1)}, bf16[8,32,256]{2,1,0:T(8,128)(2,1)S(1)}, u32[]{:S(2)}, u32[]{:S(2)}) collective-permute-start(bf16[8,32,256]{2,1,0:T(8,128)(2,1)S(1)} %get-tuple-element.9), channel_id=1, source_target_pairs={{0,2},{1,3},{2,0},{3,1},{4,6},{5,7},{6,4},{7,5},{8,10},{9,11},{10,... | collective-permute-start | bytes 393224 | tf_op jit(solution)/shard_map/ppermute | solution.py:74
  50.3 13.7 %collective-permute-start = (bf16[8,32,256]{2,1,0:T(8,128)(2,1)S(1)}, bf16[8,32,256]{2,1,0:T(8,128)(2,1)S(1)}, u32[]{:S(2)}, u32[]{:S(2)}) collective-permute-start(bf16[8,32,256]{2,1,0:T(8,128)(2,1)S(1)} %get-tuple-element.10), channel_id=1, source_target_pairs={{0,1},{1,2},{2,3},{3,0},{4,5},{5,6},{6,7},{7,4},{8,9},{9,10},{10,1... | collective-permute-start | bytes 393224 | tf_op jit(solution)/shard_map/ppermute | solution.py:74
  97.4 1.3 %copy-start.1 = (bf16[64,4,16,256]{3,2,1,0:T(8,128)(2,1)}, bf16[64,4,16,256]{3,2,1,0:T(8,128)(2,1)S(1)}, u32[]{:S(2)}) copy-start(bf16[64,4,16,256]{3,2,1,0:T(8,128)(2,1)S(1)} %all-to-all-done.1.rhs_ref) | copy-start | bytes 6291460

commit v7 on v6

--- a/solution.py
+++ b/solution.py
@@ -60,11 +60,11 @@
     ).astype(spectra.dtype)
     per_bin = group_count // my_bins
     win_piece = win_local // per_bin
-    rows = ordered.reshape(seg_count, my_bins, per_bin, win_piece, 2 * chan_width)
-    send = rows.transpose(1, 2, 0, 3, 4).reshape(group_count * seg_count, win_piece, 2 * chan_width)
-    held = lax.all_to_all(send, ("chan", "seg"), split_axis=0, concat_axis=0, tiled=True)
-    held = held.reshape(group_count, seg_count * win_piece, 2 * chan_width)
-    outgoing = held.at[plan.T].get(mode="promise_in_bounds")
+    send = ordered.reshape(seg_count * group_count, win_piece, 2 * chan_width)
+    held = lax.all_to_all(send, ("seg", "chan"), split_axis=0, concat_axis=0, tiled=True)
+    sources = (jnp.arange(seg_count, dtype=plan.dtype) * group_count)[None, None, :] + plan.T[:, :, None]
+    outgoing = held.at[sources].get(mode="promise_in_bounds")
+    outgoing = outgoing.reshape(group_count, plan.shape[0], seg_count * win_piece, 2 * chan_width)
     arrived = lax.all_to_all(outgoing, "chan", split_axis=0, concat_axis=0, tiled=True)
     ranges = ordered.reshape(seg_count, my_bins, win_local, 2 * chan_width)
     by_shift = [lax.dynamic_index_in_dim(ranges, seg_index, 0, keepdims=False)]

time: 103 us -> 113 us (1.097)
  local copies, waits for them, and re-layouts: 17.1 us -> 26.6 us
    gather x1, local copies, waits for them, and re-layouts: 2.07 us -> 8.55 us  [on_device(): outgoing = held.at[sources].get(mode='promise_in_bounds')]
    reshape x2, local copies, waits for them, and re-layouts: 0.46 us -> 5.08 us  [the longest x1 3.95 us: on_device(): outgoing.reshape(group_count, plan.shape[0], seg_count * win_piece, 2 * c...]
    convert_element_type x2 -> x1, local copies, waits for them, and re-layouts: 1.86 us -> 0.51 us  [on_device(): ordered = jnp.einsum('fwkm,mc->fwkc', spectra, onehot.astype(spectra.dtyp...]
  transfers between devices with their start and end apart: 5 -> 5, of which waited for: 4 -> 4; matrix products, arithmetic and copies ran while one was open for 13% -> 11% of each run, Pallas kernels for 0% -> 0%
where the time goes in v7:
time: 113 us
  waiting for transfers between devices  56.4 us (50%)
  local copies, waits for them, and re-layouts  26.6 us (24%)
  starting transfers between devices  22.8 us (20%)
  Pallas kernels  4.12 us (4%)
  other arithmetic  2.65 us (2%)
    all_to_all x1, waiting for transfers between devices, on_device(): lax.all_to_all(outgoing, 'chan', split_axis=0, concat_axis=0, tiled=True)  23.8 us
    all_to_all x1, waiting for transfers between devices, on_device(): lax.all_to_all(send, ('seg', 'chan'), split_axis=0, concat_axis=0, tiled=...  18.8 us
    all_to_all x1, starting transfers between devices, on_device(): lax.all_to_all(send, ('seg', 'chan'), split_axis=0, concat_axis=0, tiled=...  14.7 us
    ppermute x3, waiting for transfers between devices, on_device(): by_shift.append(lax.ppermute(part, 'seg', pairs))  13.8 us
    gather x1, local copies, waits for them, and re-layouts, on_device(): outgoing = held.at[sources].get(mode='promise_in_bounds')  8.55 us
    all_to_all x1, starting transfers between devices, on_device(): lax.all_to_all(outgoing, 'chan', split_axis=0, concat_axis=0, tiled=True)  7.06 us
    pallas_call x1, Pallas kernels, cross_spectra(): pl.pallas_call(functools.partial(cross_kernel, scale), grid=(bins // step...  4.12 us
    reshape x1, local copies, waits for them, and re-layouts, on_device(): outgoing.reshape(group_count, plan.shape[0], seg_count * win_piece, 2 * c...  3.95 us
  transfers between devices with their start and end apart: 5, of which 4 were waited for; matrix products, arithmetic and copies ran while one was open for 11% of the time, Pallas kernels for 0%

profile of v7, /device:TPU:2, one launch (start us, length us, event | category | flops | bytes accessed | tf_op | source)
XLA Modules:
  0.0 113.0 jit_solution(4929680201785609989)
XLA Ops:
  0.0 0.0 copy-start
  0.0 0.7 broadcast_subtract_fusion
  0.7 0.3 copy-done
  1.1 0.0 copy-start.2
  1.1 0.3 fusion
  1.4 0.5 copy.7
  1.9 1.1 %reshape.95 = bf16[256,4,256]{2,1,0:T(4,128)(2,1)} reshape(bf16[32,32,2,128]{3,2,1,0:T(2,128)(2,1)S(1)} %copy.7) | data formatting | bytes 1048576 | tf_op jit(solution)/shard_map/reshape | solution.py:63
  3.0 14.7 %all-to-all-start = ((bf16[256,4,256]{2,1,0:T(4,128)(2,1)}), bf16[256,4,256]{2,1,0:T(4,128)(2,1)S(1)}, u32[]{:S(2)}, u32[]{:S(2)}) async-start(bf16[256,4,256]{2,1,0:T(4,128)(2,1)} %reshape.95), calls=%async_computation | async-start | bytes 1048576 | tf_op jit(solution)/shard_map/all_to_all | solution.py:64
  17.7 0.0 copy-done.2
  17.7 0.1 copy.12
  17.8 0.1 compare_select_fusion
  18.0 0.2 reshape.107
  18.1 18.8 %all-to-all-done = bf16[256,4,256]{2,1,0:T(4,128)(2,1)S(1)} async-done(((bf16[256,4,256]{2,1,0:T(4,128)(2,1)}), bf16[256,4,256]{2,1,0:T(4,128)(2,1)S(1)}, u32[]{:S(2)}, u32[]{:S(2)}) %all-to-all-start) | async-done | bytes 524320 | tf_op jit(solution)/shard_map/all_to_all | solution.py:64
  36.9 8.6 %gather_fusion.1 = bf16[1024,4,256]{2,1,0:T(4,128)(2,1)} fusion(bf16[256,4,256]{2,1,0:T(4,128)(2,1)S(1)} %all-to-all-done, s32[1024]{0:T(1024)S(1)} %broadcast_clamp_fusion), kind=kCustom, calls=%fused_computation.1 | custom fusion | bytes 4198400 | tf_op jit(solution)/shard_map/gather | solution.py:66
  45.4 4.0 %reshape.96 = bf16[64,4,16,256]{3,2,1,0:T(8,128)(2,1)} reshape(bf16[1024,4,256]{2,1,0:T(4,128)(2,1)} %gather_fusion.1) | data formatting | bytes 4194304 | tf_op jit(solution)/shard_map/reshape | solution.py:67
  49.4 7.1 %all-to-all-start.1 = ((bf16[64,4,16,256]{3,2,1,0:T(8,128)(2,1)}), bf16[64,4,16,256]{3,2,1,0:T(8,128)(2,1)S(1)}, u32[]{:S(2)}, u32[]{:S(2)}) async-start(bf16[64,4,16,256]{3,2,1,0:T(8,128)(2,1)} %reshape.96), calls=%async_computation.1 | async-start | bytes 4194304 | tf_op jit(solution)/shard_map/all_to_all | solution.py:68
  56.5 1.1 reshape.92
  57.6 1.1 constant_dynamic-slice_fusion
  58.7 0.1 collective-permute-start.2
  58.8 0.9 collective-permute-start.1
  59.8 0.0 collective-permute-start
  59.8 7.0 %collective-permute-done.2 = bf16[8,32,256]{2,1,0:T(8,128)(2,1)S(1)} collective-permute-done((bf16[8,32,256]{2,1,0:T(8,128)(2,1)S(1)}, bf16[8,32,256]{2,1,0:T(8,128)(2,1)S(1)}, u32[]{:S(2)}, u32[]{:S(2)}) %collective-permute-start.2) | collective-permute-done | bytes 131104 | tf_op jit(solution)/shard_map/ppermute | solution.py:74
  66.8 6.9 %collective-permute-done.1 = bf16[8,32,256]{2,1,0:T(8,128)(2,1)S(1)} collective-permute-done((bf16[8,32,256]{2,1,0:T(8,128)(2,1)S(1)}, bf16[8,32,256]{2,1,0:T(8,128)(2,1)S(1)}, u32[]{:S(2)}, u32[]{:S(2)}) %collective-permute-start.1) | collective-permute-done | bytes 131104 | tf_op jit(solution)/shard_map/ppermute | solution.py:74
  73.7 0.0 collective-permute-done
  73.7 0.1 pad_maximum_fusion.1
  73.7 1.4 %gather_fusion = bf16[4,8,32,256]{3,2,1,0:T(8,128)(2,1)} fusion(bf16[4,8,32,256]{3,2,1,0:T(8,128)(2,1)S(1)} %pad_maximum_fusion.1, s32[1024]{0:T(1024)S(1)} %pad_clamp_fusion), kind=kCustom, calls=%fused_computation | custom fusion | bytes 1048592 | tf_op jit(solution)/shard_map/jit(_take)/gather | solution.py:77
  75.1 1.2 %gather.10 = bf16[4,8,8,4,2,128]{5,4,3,2,1,0:T(2,128)(2,1)S(1)} reshape(bf16[4,8,32,256]{3,2,1,0:T(8,128)(2,1)} %gather_fusion) | data formatting | bytes 1048576 | tf_op jit(solution)/shard_map/jit(_take)/gather | solution.py:77
  76.3 0.5 fusion.2
  76.8 0.3 copy.8
  77.2 0.1 fusion.9
  77.2 0.1 maximum_bitcast_fusion
  77.3 1.1 pad_maximum_fusion
  78.3 2.8 %copy.10 = bf16[8,2,128,2,128]{4,3,2,1,0:T(2,128)(2,1)} copy(bf16[8,2,128,2,128]{2,0,4,3,1:T(8,128)(2,1)} %pad_maximum_fusion) | data formatting | bytes 2097152 | tf_op jit(solution)/shard_map/stack | solution.py:81
  81.2 2.5 %reshape.94.lhs_ref = bf16[8,256,256]{2,1,0:T(8,128)(2,1)} reshape(bf16[8,2,128,2,128]{4,3,2,1,0:T(2,128)(2,1)} %copy.10) | data formatting | bytes 2097152 | tf_op jit(solution)/shard_map/reshape | solution.py:81
  83.7 23.8 %all-to-all-done.1.rhs_ref = bf16[64,4,16,256]{3,2,1,0:T(8,128)(2,1)S(1)} async-done(((bf16[64,4,16,256]{3,2,1,0:T(8,128)(2,1)}), bf16[64,4,16,256]{3,2,1,0:T(8,128)(2,1)S(1)}, u32[]{:S(2)}, u32[]{:S(2)}) %all-to-all-start.1) | async-done | bytes 2097184 | tf_op jit(solution)/shard_map/all_to_all | solution.py:68
  107.5 0.0 copy-start.1
  107.5 1.3 %copy-done.1 = bf16[64,4,16,256]{3,2,1,0:T(8,128)(2,1)} copy-done((bf16[64,4,16,256]{3,2,1,0:T(8,128)(2,1)}, bf16[64,4,16,256]{3,2,1,0:T(8,128)(2,1)S(1)}, u32[]{:S(2)}) %copy-start.1) | copy-done | bytes 2097176
  108.8 4.1 %shard_map.37 = f32[4,8,2,128,128]{4,3,2,1,0:T(8,128)} custom-call(bf16[8,256,256]{2,1,0:T(8,128)(2,1)} %reshape.94.lhs_ref, bf16[64,4,16,256]{3,2,1,0:T(8,128)(2,1)} %copy-done.1), custom_call_target="tpu_custom_call" | custom-call | flops 536870912 | bytes 7340032 | tf_op jit(solution)/shard_map/pallas_call | solution.py:31
  (5 shorter events, 0.0 us)
Async XLA Ops:
  0.0 1.1 copy-start
  1.1 16.6 %copy-start.2 = (s32[4,64]{1,0:T(4,128)S(1)}, s32[4,64]{1,0:T(4,128)}, u32[]{:S(2)}) copy-start(s32[4,64]{1,0:T(4,128)} %param.4) | copy-start | bytes 3076
  3.0 33.9 %all-to-all-start = ((bf16[256,4,256]{2,1,0:T(4,128)(2,1)}), bf16[256,4,256]{2,1,0:T(4,128)(2,1)S(1)}, u32[]{:S(2)}, u32[]{:S(2)}) async-start(bf16[256,4,256]{2,1,0:T(4,128)(2,1)} %reshape.95), calls=%async_computation | async-start | bytes 1048576 | tf_op jit(solution)/shard_map/all_to_all | solution.py:64
  49.4 58.1 %all-to-all-start.1 = ((bf16[64,4,16,256]{3,2,1,0:T(8,128)(2,1)}), bf16[64,4,16,256]{3,2,1,0:T(8,128)(2,1)S(1)}, u32[]{:S(2)}, u32[]{:S(2)}) async-start(bf16[64,4,16,256]{3,2,1,0:T(8,128)(2,1)} %reshape.96), calls=%async_computation.1 | async-start | bytes 4194304 | tf_op jit(solution)/shard_map/all_to_all | solution.py:68
  58.7 8.0 %collective-permute-start.2 = (bf16[8,32,256]{2,1,0:T(8,128)(2,1)S(1)}, bf16[8,32,256]{2,1,0:T(8,128)(2,1)S(1)}, u32[]{:S(2)}, u32[]{:S(2)}) collective-permute-start(bf16[8,32,256]{2,1,0:T(8,128)(2,1)S(1)} %get-tuple-element.8), channel_id=1, source_target_pairs={{0,3},{1,0},{2,1},{3,2},{4,7},{5,4},{6,5},{7,6},{8,11},{9,8},{10,9... | collective-permute-start | bytes 393224 | tf_op jit(solution)/shard_map/ppermute | solution.py:74
  58.8 14.8 %collective-permute-start.1 = (bf16[8,32,256]{2,1,0:T(8,128)(2,1)S(1)}, bf16[8,32,256]{2,1,0:T(8,128)(2,1)S(1)}, u32[]{:S(2)}, u32[]{:S(2)}) collective-permute-start(bf16[8,32,256]{2,1,0:T(8,128)(2,1)S(1)} %get-tuple-element.9), channel_id=1, source_target_pairs={{0,2},{1,3},{2,0},{3,1},{4,6},{5,7},{6,4},{7,5},{8,10},{9,11},{10,... | collective-permute-start | bytes 393224 | tf_op jit(solution)/shard_map/ppermute | solution.py:74
  59.8 13.9 %collective-permute-start = (bf16[8,32,256]{2,1,0:T(8,128)(2,1)S(1)}, bf16[8,32,256]{2,1,0:T(8,128)(2,1)S(1)}, u32[]{:S(2)}, u32[]{:S(2)}) collective-permute-start(bf16[8,32,256]{2,1,0:T(8,128)(2,1)S(1)} %get-tuple-element.10), channel_id=1, source_target_pairs={{0,1},{1,2},{2,3},{3,0},{4,5},{5,6},{6,7},{7,4},{8,9},{9,10},{10,1... | collective-permute-start | bytes 393224 | tf_op jit(solution)/shard_map/ppermute | solution.py:74
  107.5 1.3 %copy-start.1 = (bf16[64,4,16,256]{3,2,1,0:T(8,128)(2,1)}, bf16[64,4,16,256]{3,2,1,0:T(8,128)(2,1)S(1)}, u32[]{:S(2)}) copy-start(bf16[64,4,16,256]{3,2,1,0:T(8,128)(2,1)S(1)} %all-to-all-done.1.rhs_ref) | copy-start | bytes 6291460

commit v8 on v6

--- a/solution.py
+++ b/solution.py
@@ -5,18 +5,21 @@
 import jax.numpy as jnp
 from jax import lax
 from jax.experimental import pallas as pl
+from jax.experimental.pallas import tpu as pltpu
 from jax.sharding import PartitionSpec as P
 
 
 def cross_kernel(scale, lhs_ref, rhs_ref, out_ref):
     step_bins = lhs_ref.shape[0]
     pieces, rounds, rows, two_chan = rhs_ref.shape
-    per_bin = pieces // step_bins
+    per_bin = pieces // (step_bins * pl.num_programs(0))
     chan = two_chan // 2
+    first = pl.program_id(0) * step_bins
     for b in range(step_bins):
         lhs = lhs_ref[b]
         for r in range(rounds):
-            block = rhs_ref[b * per_bin:(b + 1) * per_bin, r].reshape(per_bin * rows, two_chan)
+            block = rhs_ref[pl.ds((first + b) * per_bin, per_bin), r]
+            block = block.reshape(per_bin * rows, two_chan)
             block = jnp.concatenate([block[:, :chan], block[:, chan:]], axis=0)
             acc = jnp.dot(lhs, block, preferred_element_type=jnp.float32)
             out_ref[r, b] = (acc * scale).reshape(2, chan, chan)
@@ -33,7 +36,7 @@
         grid=(bins // step_bins,),
         in_specs=[
             pl.BlockSpec((step_bins, two_chan, two_win), lambda g: (g, 0, 0)),
-            pl.BlockSpec((step_bins * per_bin, rounds, rows, two_chan), lambda g: (g, 0, 0, 0)),
+            pl.BlockSpec(memory_space=pltpu.VMEM),
         ],
         out_specs=pl.BlockSpec((rounds, step_bins, 2, chan, chan), lambda g: (0, g, 0, 0, 0)),
         out_shape=jax.ShapeDtypeStruct((rounds, bins, 2, chan, chan), jnp.float32),
@@ -42,7 +45,7 @@
             bytes_accessed=lhs.size * 2 + arrived.size * 2 + rounds * bins * 2 * chan * chan * 4,
             transcendentals=0,
         ),
-    )(lhs, arrived)
+    )(lhs, pltpu.with_memory_space_constraint(arrived, pltpu.VMEM))
 
 
 def on_device(spectra, plan, assignment):

time: 103 us -> 102 us (level)
  local copies, waits for them, and re-layouts: 17.1 us -> 15.8 us
    unnamed x6 -> x4, local copies, waits for them, and re-layouts: 1.68 us -> 0.35 us
where the time goes in v8:
time: 102 us; the launch traced here: 101 us
  waiting for transfers between devices  55.8 us (55%)
  starting transfers between devices  22.7 us (22%)
  local copies, waits for them, and re-layouts  15.8 us (15%)
  Pallas kernels  3.77 us (4%)
  other arithmetic  2.57 us (3%)
    all_to_all x1, waiting for transfers between devices, on_device(): lax.all_to_all(outgoing, 'chan', split_axis=0, concat_axis=0, tiled=True)  23.3 us
    all_to_all x1, waiting for transfers between devices, on_device(): lax.all_to_all(send, ('chan', 'seg'), split_axis=0, concat_axis=0, tiled=...  18.9 us
    all_to_all x1, starting transfers between devices, on_device(): lax.all_to_all(send, ('chan', 'seg'), split_axis=0, concat_axis=0, tiled=...  14.7 us
    ppermute x3, waiting for transfers between devices, on_device(): by_shift.append(lax.ppermute(part, 'seg', pairs))  13.5 us
    all_to_all x1, starting transfers between devices, on_device(): lax.all_to_all(outgoing, 'chan', split_axis=0, concat_axis=0, tiled=True)  7.05 us
    pallas_call x1, Pallas kernels, cross_spectra(): pl.pallas_call(functools.partial(cross_kernel, scale), grid=(bins // step...  3.77 us
    another operation x1, local copies, waits for them, and re-layouts, on_device(): jnp.stack([own, imag_rows], axis=1)  2.82 us
    gather x2, local copies, waits for them, and re-layouts, on_device(): own = jnp.take(by_shift, order, axis=0)  2.54 us
  transfers between devices with their start and end apart: 5, of which 4 were waited for; matrix products, arithmetic and copies ran while one was open for 13% of the time, Pallas kernels for 0%

profile of v8, /device:TPU:2, one launch (start us, length us, event | category | flops | bytes accessed | tf_op | source)
XLA Modules:
  0.0 101.1 jit_solution(2870032049208309409)
XLA Ops:
  0.0 0.0 copy-start
  0.0 0.7 broadcast_subtract_fusion
  0.7 0.3 copy-done
  1.1 0.3 fusion
  1.4 0.0 copy-start.1
  1.4 0.5 copy.10
  1.9 0.3 reshape.78
  2.3 1.2 %copy.11 = bf16[8,8,4,4,256]{4,3,2,1,0:T(4,128)(2,1)} copy(bf16[8,8,4,4,256]{4,0,2,3,1:T(8,128)(2,1)S(1)} %bitcast.36) | data formatting | bytes 1048576 | tf_op jit(solution)/shard_map/transpose | solution.py:67
  3.5 14.7 %all-to-all-start = ((bf16[256,4,256]{2,1,0:T(4,128)(2,1)}), bf16[256,4,256]{2,1,0:T(4,128)(2,1)S(1)}, u32[]{:S(2)}, u32[]{:S(2)}) async-start(bf16[256,4,256]{2,1,0:T(4,128)(2,1)} %bitcast.15), calls=%async_computation | async-start | bytes 1048576 | tf_op jit(solution)/shard_map/all_to_all | solution.py:68
  18.2 0.0 copy-done.1
  18.2 0.1 copy.12
  18.3 0.1 reshape.91
  18.4 18.9 %all-to-all-done = bf16[256,4,256]{2,1,0:T(4,128)(2,1)S(1)} async-done(((bf16[256,4,256]{2,1,0:T(4,128)(2,1)}), bf16[256,4,256]{2,1,0:T(4,128)(2,1)S(1)}, u32[]{:S(2)}, u32[]{:S(2)}) %all-to-all-start) | async-done | bytes 524320 | tf_op jit(solution)/shard_map/all_to_all | solution.py:68
  37.3 0.1 reshape.80
  37.5 2.1 %gather_fusion.1 = bf16[256,16,256]{2,1,0:T(8,128)(2,1)} fusion(bf16[64,16,256]{2,1,0:T(8,128)(2,1)S(1)} %reshape.80, s32[1024]{0:T(1024)S(1)} %pad_clamp_fusion), kind=kCustom, calls=%fused_computation.1 | custom fusion | bytes 4195328 | tf_op jit(solution)/shard_map/gather | solution.py:70
  39.5 7.1 %all-to-all-start.1 = ((bf16[64,4,16,256]{3,2,1,0:T(8,128)(2,1)}), bf16[64,4,16,256]{3,2,1,0:T(8,128)(2,1)S(1)}, u32[]{:S(2)}, u32[]{:S(2)}) async-start(bf16[64,4,16,256]{3,2,1,0:T(8,128)(2,1)} %bitcast.33), calls=%async_computation.1 | async-start | bytes 4194304 | tf_op jit(solution)/shard_map/all_to_all | solution.py:71
  46.6 1.3 %copy.6 = bf16[32,32,2,128]{3,2,1,0:T(2,128)(2,1)} copy(bf16[32,32,2,128]{3,1,2,0:T(8,128)(2,1)S(1)} %fusion) | data formatting | bytes 1048576 | tf_op jit(solution)/shard_map/convert_element_type | solution.py:63
  48.0 1.4 %reshape.75 = bf16[4,8,32,256]{3,2,1,0:T(8,128)(2,1)S(1)} reshape(bf16[32,32,2,128]{3,2,1,0:T(2,128)(2,1)} %copy.6) | data formatting | bytes 1048576 | tf_op jit(solution)/shard_map/reshape | solution.py:72
  49.4 0.1 collective-permute-start.2
  49.5 0.8 collective-permute-start.1
  50.3 0.1 collective-permute-start
  50.5 6.3 %collective-permute-done.2 = bf16[8,32,256]{2,1,0:T(8,128)(2,1)S(1)} collective-permute-done((bf16[8,32,256]{2,1,0:T(8,128)(2,1)S(1)}, bf16[8,32,256]{2,1,0:T(8,128)(2,1)S(1)}, u32[]{:S(2)}, u32[]{:S(2)}) %collective-permute-start.2) | collective-permute-done | bytes 131104 | tf_op jit(solution)/shard_map/ppermute | solution.py:77
  56.7 7.2 %collective-permute-done.1 = bf16[8,32,256]{2,1,0:T(8,128)(2,1)S(1)} collective-permute-done((bf16[8,32,256]{2,1,0:T(8,128)(2,1)S(1)}, bf16[8,32,256]{2,1,0:T(8,128)(2,1)S(1)}, u32[]{:S(2)}, u32[]{:S(2)}) %collective-permute-start.1) | collective-permute-done | bytes 131104 | tf_op jit(solution)/shard_map/ppermute | solution.py:77
  63.9 0.0 collective-permute-done
  63.9 0.1 pad_maximum_fusion.1
  64.0 1.4 %gather_fusion = bf16[4,8,32,256]{3,2,1,0:T(8,128)(2,1)} fusion(bf16[4,8,32,256]{3,2,1,0:T(8,128)(2,1)S(1)} %pad_maximum_fusion.1, s32[1024]{0:T(1024)S(1)} %pad_clamp_fusion.1), kind=kCustom, calls=%fused_computation | custom fusion | bytes 1048592 | tf_op jit(solution)/shard_map/jit(_take)/gather | solution.py:80
  65.4 1.2 %gather.10 = bf16[4,8,8,4,2,128]{5,4,3,2,1,0:T(2,128)(2,1)S(1)} reshape(bf16[4,8,32,256]{3,2,1,0:T(8,128)(2,1)} %gather_fusion) | data formatting | bytes 1048576 | tf_op jit(solution)/shard_map/jit(_take)/gather | solution.py:80
  66.6 0.5 fusion.2
  67.1 0.3 copy.7
  67.4 0.1 fusion.9
  67.5 0.1 maximum_bitcast_fusion
  67.6 1.1 %pad_maximum_fusion = bf16[8,2,128,2,128]{2,0,4,3,1:T(8,128)(2,1)} fusion(bf16[8,1,128,2,128]{2,0,4,3,1:T(8,128)(2,1)S(1)} %maximum_bitcast_fusion, bf16[8,1,128,2,128]{2,0,4,3,1:T(8,128)(2,1)S(1)} %bitcast.35), kind=kLoop, calls=%fused_computation.4 | loop fusion | flops 524288 | bytes 2097152 | tf_op jit(solution)/shard_map/stack | solution.py:84
  68.7 2.8 %copy.9 = bf16[8,2,128,2,128]{4,3,2,1,0:T(2,128)(2,1)} copy(bf16[8,2,128,2,128]{2,0,4,3,1:T(8,128)(2,1)} %pad_maximum_fusion) | data formatting | bytes 2097152 | tf_op jit(solution)/shard_map/stack | solution.py:84
  71.5 2.5 %reshape.77.lhs_ref = bf16[8,256,256]{2,1,0:T(8,128)(2,1)} reshape(bf16[8,2,128,2,128]{4,3,2,1,0:T(2,128)(2,1)} %copy.9) | data formatting | bytes 2097152 | tf_op jit(solution)/shard_map/reshape | solution.py:84
  74.0 23.3 %all-to-all-done.1.rhs_ref = bf16[64,4,16,256]{3,2,1,0:T(8,128)(2,1)S(1)} async-done(((bf16[64,4,16,256]{3,2,1,0:T(8,128)(2,1)}), bf16[64,4,16,256]{3,2,1,0:T(8,128)(2,1)S(1)}, u32[]{:S(2)}, u32[]{:S(2)}) %all-to-all-start.1) | async-done | bytes 2097184 | tf_op jit(solution)/shard_map/all_to_all | solution.py:71
  97.4 3.8 %shard_map.37 = f32[4,8,2,128,128]{4,3,2,1,0:T(8,128)} custom-call(bf16[8,256,256]{2,1,0:T(8,128)(2,1)} %reshape.77.lhs_ref, bf16[64,4,16,256]{3,2,1,0:T(8,128)(2,1)S(1)} %all-to-all-done.1.rhs_ref), custom_call_target="tpu_custom_call" | custom-call | flops 536870912 | bytes 7340032 | tf_op jit(solution)/shard_map/pallas_call | solution.py:34
  (6 shorter events, 0.1 us)
Async XLA Ops:
  0.0 1.1 %copy-start = (bf16[32,32,2,128]{3,2,1,0:T(2,128)(2,1)S(1)}, bf16[32,32,2,128]{3,2,1,0:T(2,128)(2,1)}, u32[]{:S(2)}) copy-start(bf16[32,32,2,128]{3,2,1,0:T(2,128)(2,1)} %param.3) | copy-start | bytes 1572868
  1.4 16.8 %copy-start.1 = (s32[4,64]{1,0:T(4,128)S(1)}, s32[4,64]{1,0:T(4,128)}, u32[]{:S(2)}) copy-start(s32[4,64]{1,0:T(4,128)} %param.4) | copy-start | bytes 3076
  3.5 33.9 %all-to-all-start = ((bf16[256,4,256]{2,1,0:T(4,128)(2,1)}), bf16[256,4,256]{2,1,0:T(4,128)(2,1)S(1)}, u32[]{:S(2)}, u32[]{:S(2)}) async-start(bf16[256,4,256]{2,1,0:T(4,128)(2,1)} %bitcast.15), calls=%async_computation | async-start | bytes 1048576 | tf_op jit(solution)/shard_map/all_to_all | solution.py:68
  39.5 57.8 %all-to-all-start.1 = ((bf16[64,4,16,256]{3,2,1,0:T(8,128)(2,1)}), bf16[64,4,16,256]{3,2,1,0:T(8,128)(2,1)S(1)}, u32[]{:S(2)}, u32[]{:S(2)}) async-start(bf16[64,4,16,256]{3,2,1,0:T(8,128)(2,1)} %bitcast.33), calls=%async_computation.1 | async-start | bytes 4194304 | tf_op jit(solution)/shard_map/all_to_all | solution.py:71
  49.4 7.3 %collective-permute-start.2 = (bf16[8,32,256]{2,1,0:T(8,128)(2,1)S(1)}, bf16[8,32,256]{2,1,0:T(8,128)(2,1)S(1)}, u32[]{:S(2)}, u32[]{:S(2)}) collective-permute-start(bf16[8,32,256]{2,1,0:T(8,128)(2,1)S(1)} %get-tuple-element.8), channel_id=1, source_target_pairs={{0,3},{1,0},{2,1},{3,2},{4,7},{5,4},{6,5},{7,6},{8,11},{9,8},{10,9... | collective-permute-start | bytes 393224 | tf_op jit(solution)/shard_map/ppermute | solution.py:77
  49.5 14.4 %collective-permute-start.1 = (bf16[8,32,256]{2,1,0:T(8,128)(2,1)S(1)}, bf16[8,32,256]{2,1,0:T(8,128)(2,1)S(1)}, u32[]{:S(2)}, u32[]{:S(2)}) collective-permute-start(bf16[8,32,256]{2,1,0:T(8,128)(2,1)S(1)} %get-tuple-element.9), channel_id=1, source_target_pairs={{0,2},{1,3},{2,0},{3,1},{4,6},{5,7},{6,4},{7,5},{8,10},{9,11},{10,... | collective-permute-start | bytes 393224 | tf_op jit(solution)/shard_map/ppermute | solution.py:77
  50.3 13.7 %collective-permute-start = (bf16[8,32,256]{2,1,0:T(8,128)(2,1)S(1)}, bf16[8,32,256]{2,1,0:T(8,128)(2,1)S(1)}, u32[]{:S(2)}, u32[]{:S(2)}) collective-permute-start(bf16[8,32,256]{2,1,0:T(8,128)(2,1)S(1)} %get-tuple-element.10), channel_id=1, source_target_pairs={{0,1},{1,2},{2,3},{3,0},{4,5},{5,6},{6,7},{7,4},{8,9},{9,10},{10,1... | collective-permute-start | bytes 393224 | tf_op jit(solution)/shard_map/ppermute | solution.py:77

commit v9 on v8

--- a/solution.py
+++ b/solution.py
@@ -9,37 +9,50 @@
 from jax.sharding import PartitionSpec as P
 
 
-def cross_kernel(scale, lhs_ref, rhs_ref, out_ref):
-    step_bins = lhs_ref.shape[0]
+def cross_kernel(scale, lhs_hbm, rhs_ref, out_hbm, lhs_buf, out_buf, lhs_sems, out_sems):
+    bins = lhs_buf.shape[0]
     pieces, rounds, rows, two_chan = rhs_ref.shape
-    per_bin = pieces // (step_bins * pl.num_programs(0))
+    per_bin = pieces // bins
     chan = two_chan // 2
-    first = pl.program_id(0) * step_bins
-    for b in range(step_bins):
-        lhs = lhs_ref[b]
+    lhs_copies = [
+        pltpu.make_async_copy(lhs_hbm.at[f], lhs_buf.at[f], lhs_sems.at[f]) for f in range(bins)
+    ]
+    for copy in lhs_copies:
+        copy.start()
+    out_copies = []
+    for f in range(bins):
+        lhs_copies[f].wait()
+        lhs = lhs_buf[f]
         for r in range(rounds):
-            block = rhs_ref[pl.ds((first + b) * per_bin, per_bin), r]
-            block = block.reshape(per_bin * rows, two_chan)
+            block = rhs_ref[f * per_bin:(f + 1) * per_bin, r].reshape(per_bin * rows, two_chan)
             block = jnp.concatenate([block[:, :chan], block[:, chan:]], axis=0)
             acc = jnp.dot(lhs, block, preferred_element_type=jnp.float32)
-            out_ref[r, b] = (acc * scale).reshape(2, chan, chan)
+            out_buf[r, f] = (acc * scale).reshape(2, chan, chan)
+            copy = pltpu.make_async_copy(out_buf.at[r, f], out_hbm.at[r, f], out_sems.at[r, f])
+            copy.start()
+            out_copies.append(copy)
+    for copy in out_copies:
+        copy.wait()
 
 
 def cross_spectra(lhs, arrived, scale):
     bins, two_chan, two_win = lhs.shape
     chan = two_chan // 2
     pieces, rounds, rows, _ = arrived.shape
-    per_bin = pieces // bins
-    step_bins = 4
     return pl.pallas_call(
         functools.partial(cross_kernel, scale),
-        grid=(bins // step_bins,),
         in_specs=[
-            pl.BlockSpec((step_bins, two_chan, two_win), lambda g: (g, 0, 0)),
+            pl.BlockSpec(memory_space=pl.ANY),
             pl.BlockSpec(memory_space=pltpu.VMEM),
         ],
-        out_specs=pl.BlockSpec((rounds, step_bins, 2, chan, chan), lambda g: (0, g, 0, 0, 0)),
+        out_specs=pl.BlockSpec(memory_space=pl.ANY),
         out_shape=jax.ShapeDtypeStruct((rounds, bins, 2, chan, chan), jnp.float32),
+        scratch_shapes=[
+            pltpu.VMEM(lhs.shape, lhs.dtype),
+            pltpu.VMEM((rounds, bins, 2, chan, chan), jnp.float32),
+            pltpu.SemaphoreType.DMA((bins,)),
+            pltpu.SemaphoreType.DMA((rounds, bins)),
+        ],
         cost_estimate=pl.CostEstimate(
             flops=2 * rounds * bins * two_chan * two_win * chan,
             bytes_accessed=lhs.size * 2 + arrived.size * 2 + rounds * bins * 2 * chan * chan * 4,

time: 102 us -> 102 us (level)
  no operation moved by 1% of the time
where the time goes in v9:
time: 102 us
  waiting for transfers between devices  55.8 us (55%)
  starting transfers between devices  22.7 us (22%)
  local copies, waits for them, and re-layouts  15.8 us (15%)
  Pallas kernels  4.32 us (4%)
  other arithmetic  2.57 us (3%)
    all_to_all x1, waiting for transfers between devices, on_device(): lax.all_to_all(outgoing, 'chan', split_axis=0, concat_axis=0, tiled=True)  23.3 us
    all_to_all x1, waiting for transfers between devices, on_device(): lax.all_to_all(send, ('chan', 'seg'), split_axis=0, concat_axis=0, tiled=...  18.9 us
    all_to_all x1, starting transfers between devices, on_device(): lax.all_to_all(send, ('chan', 'seg'), split_axis=0, concat_axis=0, tiled=...  14.7 us
    ppermute x3, waiting for transfers between devices, on_device(): by_shift.append(lax.ppermute(part, 'seg', pairs))  13.5 us
    all_to_all x1, starting transfers between devices, on_device(): lax.all_to_all(outgoing, 'chan', split_axis=0, concat_axis=0, tiled=True)  7.05 us
    pallas_call x1, Pallas kernels, cross_spectra(): pl.pallas_call(functools.partial(cross_kernel, scale), in_specs=[pl.Block...  4.32 us
    another operation x1, local copies, waits for them, and re-layouts, on_device(): jnp.stack([own, imag_rows], axis=1)  2.82 us
    gather x2, local copies, waits for them, and re-layouts, on_device(): own = jnp.take(by_shift, order, axis=0)  2.54 us
  transfers between devices with their start and end apart: 5, of which 4 were waited for; matrix products, arithmetic and copies ran while one was open for 13% of the time, Pallas kernels for 0%

profile of v9, /device:TPU:2, one launch (start us, length us, event | category | flops | bytes accessed | tf_op | source)
XLA Modules:
  0.0 101.7 jit_solution(8020786044723086274)
XLA Ops:
  0.0 0.0 copy-start
  0.0 0.7 broadcast_subtract_fusion
  0.7 0.3 copy-done
  1.1 0.3 fusion
  1.4 0.0 copy-start.1
  1.4 0.5 copy.10
  1.9 0.3 reshape.78
  2.3 1.2 %copy.11 = bf16[8,8,4,4,256]{4,3,2,1,0:T(4,128)(2,1)} copy(bf16[8,8,4,4,256]{4,0,2,3,1:T(8,128)(2,1)S(1)} %bitcast.36) | data formatting | bytes 1048576 | tf_op jit(solution)/shard_map/transpose | solution.py:80
  3.5 14.7 %all-to-all-start = ((bf16[256,4,256]{2,1,0:T(4,128)(2,1)}), bf16[256,4,256]{2,1,0:T(4,128)(2,1)S(1)}, u32[]{:S(2)}, u32[]{:S(2)}) async-start(bf16[256,4,256]{2,1,0:T(4,128)(2,1)} %bitcast.15), calls=%async_computation | async-start | bytes 1048576 | tf_op jit(solution)/shard_map/all_to_all | solution.py:81
  18.2 0.0 copy-done.1
  18.2 0.1 copy.12
  18.3 0.1 reshape.91
  18.4 18.9 %all-to-all-done = bf16[256,4,256]{2,1,0:T(4,128)(2,1)S(1)} async-done(((bf16[256,4,256]{2,1,0:T(4,128)(2,1)}), bf16[256,4,256]{2,1,0:T(4,128)(2,1)S(1)}, u32[]{:S(2)}, u32[]{:S(2)}) %all-to-all-start) | async-done | bytes 524320 | tf_op jit(solution)/shard_map/all_to_all | solution.py:81
  37.3 0.1 reshape.80
  37.5 2.1 %gather_fusion.1 = bf16[256,16,256]{2,1,0:T(8,128)(2,1)} fusion(bf16[64,16,256]{2,1,0:T(8,128)(2,1)S(1)} %reshape.80, s32[1024]{0:T(1024)S(1)} %pad_clamp_fusion), kind=kCustom, calls=%fused_computation.1 | custom fusion | bytes 4195328 | tf_op jit(solution)/shard_map/gather | solution.py:83
  39.5 7.1 %all-to-all-start.1 = ((bf16[64,4,16,256]{3,2,1,0:T(8,128)(2,1)}), bf16[64,4,16,256]{3,2,1,0:T(8,128)(2,1)S(1)}, u32[]{:S(2)}, u32[]{:S(2)}) async-start(bf16[64,4,16,256]{3,2,1,0:T(8,128)(2,1)} %bitcast.33), calls=%async_computation.1 | async-start | bytes 4194304 | tf_op jit(solution)/shard_map/all_to_all | solution.py:84
  46.6 1.3 %copy.6 = bf16[32,32,2,128]{3,2,1,0:T(2,128)(2,1)} copy(bf16[32,32,2,128]{3,1,2,0:T(8,128)(2,1)S(1)} %fusion) | data formatting | bytes 1048576 | tf_op jit(solution)/shard_map/convert_element_type | solution.py:76
  48.0 1.4 %reshape.75 = bf16[4,8,32,256]{3,2,1,0:T(8,128)(2,1)S(1)} reshape(bf16[32,32,2,128]{3,2,1,0:T(2,128)(2,1)} %copy.6) | data formatting | bytes 1048576 | tf_op jit(solution)/shard_map/reshape | solution.py:85
  49.4 0.1 collective-permute-start.2
  49.5 0.8 collective-permute-start.1
  50.3 0.1 collective-permute-start
  50.5 6.3 %collective-permute-done.2 = bf16[8,32,256]{2,1,0:T(8,128)(2,1)S(1)} collective-permute-done((bf16[8,32,256]{2,1,0:T(8,128)(2,1)S(1)}, bf16[8,32,256]{2,1,0:T(8,128)(2,1)S(1)}, u32[]{:S(2)}, u32[]{:S(2)}) %collective-permute-start.2) | collective-permute-done | bytes 131104 | tf_op jit(solution)/shard_map/ppermute | solution.py:90
  56.7 7.2 %collective-permute-done.1 = bf16[8,32,256]{2,1,0:T(8,128)(2,1)S(1)} collective-permute-done((bf16[8,32,256]{2,1,0:T(8,128)(2,1)S(1)}, bf16[8,32,256]{2,1,0:T(8,128)(2,1)S(1)}, u32[]{:S(2)}, u32[]{:S(2)}) %collective-permute-start.1) | collective-permute-done | bytes 131104 | tf_op jit(solution)/shard_map/ppermute | solution.py:90
  63.9 0.0 collective-permute-done
  63.9 0.1 pad_maximum_fusion.1
  64.0 1.4 %gather_fusion = bf16[4,8,32,256]{3,2,1,0:T(8,128)(2,1)} fusion(bf16[4,8,32,256]{3,2,1,0:T(8,128)(2,1)S(1)} %pad_maximum_fusion.1, s32[1024]{0:T(1024)S(1)} %pad_clamp_fusion.1), kind=kCustom, calls=%fused_computation | custom fusion | bytes 1048592 | tf_op jit(solution)/shard_map/jit(_take)/gather | solution.py:93
  65.4 1.2 %gather.10 = bf16[4,8,8,4,2,128]{5,4,3,2,1,0:T(2,128)(2,1)S(1)} reshape(bf16[4,8,32,256]{3,2,1,0:T(8,128)(2,1)} %gather_fusion) | data formatting | bytes 1048576 | tf_op jit(solution)/shard_map/jit(_take)/gather | solution.py:93
  66.6 0.5 fusion.2
  67.1 0.3 copy.7
  67.4 0.1 fusion.9
  67.5 0.1 maximum_bitcast_fusion
  67.6 1.1 %pad_maximum_fusion = bf16[8,2,128,2,128]{2,0,4,3,1:T(8,128)(2,1)} fusion(bf16[8,1,128,2,128]{2,0,4,3,1:T(8,128)(2,1)S(1)} %maximum_bitcast_fusion, bf16[8,1,128,2,128]{2,0,4,3,1:T(8,128)(2,1)S(1)} %bitcast.35), kind=kLoop, calls=%fused_computation.4 | loop fusion | flops 524288 | bytes 2097152 | tf_op jit(solution)/shard_map/stack | solution.py:97
  68.7 2.8 %copy.9 = bf16[8,2,128,2,128]{4,3,2,1,0:T(2,128)(2,1)} copy(bf16[8,2,128,2,128]{2,0,4,3,1:T(8,128)(2,1)} %pad_maximum_fusion) | data formatting | bytes 2097152 | tf_op jit(solution)/shard_map/stack | solution.py:97
  71.5 2.5 %reshape.77.lhs_hbm = bf16[8,256,256]{2,1,0:T(8,128)(2,1)} reshape(bf16[8,2,128,2,128]{4,3,2,1,0:T(2,128)(2,1)} %copy.9) | data formatting | bytes 2097152 | tf_op jit(solution)/shard_map/reshape | solution.py:97
  74.0 23.3 %all-to-all-done.1.rhs_ref = bf16[64,4,16,256]{3,2,1,0:T(8,128)(2,1)S(1)} async-done(((bf16[64,4,16,256]{3,2,1,0:T(8,128)(2,1)}), bf16[64,4,16,256]{3,2,1,0:T(8,128)(2,1)S(1)}, u32[]{:S(2)}, u32[]{:S(2)}) %all-to-all-start.1) | async-done | bytes 2097184 | tf_op jit(solution)/shard_map/all_to_all | solution.py:84
  97.4 4.3 %shard_map.37 = f32[4,8,2,128,128]{4,3,2,1,0:T(8,128)} custom-call(bf16[8,256,256]{2,1,0:T(8,128)(2,1)} %reshape.77.lhs_hbm, bf16[64,4,16,256]{3,2,1,0:T(8,128)(2,1)S(1)} %all-to-all-done.1.rhs_ref), custom_call_target="tpu_custom_call" | custom-call | flops 536870912 | bytes 7340032 | tf_op jit(solution)/shard_map/pallas_call | solution.py:42
  (6 shorter events, 0.1 us)
Async XLA Ops:
  0.0 1.1 %copy-start = (bf16[32,32,2,128]{3,2,1,0:T(2,128)(2,1)S(1)}, bf16[32,32,2,128]{3,2,1,0:T(2,128)(2,1)}, u32[]{:S(2)}) copy-start(bf16[32,32,2,128]{3,2,1,0:T(2,128)(2,1)} %param.3) | copy-start | bytes 1572868
  1.4 16.8 %copy-start.1 = (s32[4,64]{1,0:T(4,128)S(1)}, s32[4,64]{1,0:T(4,128)}, u32[]{:S(2)}) copy-start(s32[4,64]{1,0:T(4,128)} %param.4) | copy-start | bytes 3076
  3.5 33.9 %all-to-all-start = ((bf16[256,4,256]{2,1,0:T(4,128)(2,1)}), bf16[256,4,256]{2,1,0:T(4,128)(2,1)S(1)}, u32[]{:S(2)}, u32[]{:S(2)}) async-start(bf16[256,4,256]{2,1,0:T(4,128)(2,1)} %bitcast.15), calls=%async_computation | async-start | bytes 1048576 | tf_op jit(solution)/shard_map/all_to_all | solution.py:81
  39.5 57.8 %all-to-all-start.1 = ((bf16[64,4,16,256]{3,2,1,0:T(8,128)(2,1)}), bf16[64,4,16,256]{3,2,1,0:T(8,128)(2,1)S(1)}, u32[]{:S(2)}, u32[]{:S(2)}) async-start(bf16[64,4,16,256]{3,2,1,0:T(8,128)(2,1)} %bitcast.33), calls=%async_computation.1 | async-start | bytes 4194304 | tf_op jit(solution)/shard_map/all_to_all | solution.py:84
  49.4 7.3 %collective-permute-start.2 = (bf16[8,32,256]{2,1,0:T(8,128)(2,1)S(1)}, bf16[8,32,256]{2,1,0:T(8,128)(2,1)S(1)}, u32[]{:S(2)}, u32[]{:S(2)}) collective-permute-start(bf16[8,32,256]{2,1,0:T(8,128)(2,1)S(1)} %get-tuple-element.8), channel_id=1, source_target_pairs={{0,3},{1,0},{2,1},{3,2},{4,7},{5,4},{6,5},{7,6},{8,11},{9,8},{10,9... | collective-permute-start | bytes 393224 | tf_op jit(solution)/shard_map/ppermute | solution.py:90
  49.5 14.4 %collective-permute-start.1 = (bf16[8,32,256]{2,1,0:T(8,128)(2,1)S(1)}, bf16[8,32,256]{2,1,0:T(8,128)(2,1)S(1)}, u32[]{:S(2)}, u32[]{:S(2)}) collective-permute-start(bf16[8,32,256]{2,1,0:T(8,128)(2,1)S(1)} %get-tuple-element.9), channel_id=1, source_target_pairs={{0,2},{1,3},{2,0},{3,1},{4,6},{5,7},{6,4},{7,5},{8,10},{9,11},{10,... | collective-permute-start | bytes 393224 | tf_op jit(solution)/shard_map/ppermute | solution.py:90
  50.3 13.7 %collective-permute-start = (bf16[8,32,256]{2,1,0:T(8,128)(2,1)S(1)}, bf16[8,32,256]{2,1,0:T(8,128)(2,1)S(1)}, u32[]{:S(2)}, u32[]{:S(2)}) collective-permute-start(bf16[8,32,256]{2,1,0:T(8,128)(2,1)S(1)} %get-tuple-element.10), channel_id=1, source_target_pairs={{0,1},{1,2},{2,3},{3,0},{4,5},{5,6},{6,7},{7,4},{8,9},{9,10},{10,1... | collective-permute-start | bytes 393224 | tf_op jit(solution)/shard_map/ppermute | solution.py:90

commit v10 on v8

--- a/solution.py
+++ b/solution.py
@@ -30,7 +30,7 @@
     chan = two_chan // 2
     pieces, rounds, rows, _ = arrived.shape
     per_bin = pieces // bins
-    step_bins = 4
+    step_bins = 2
     return pl.pallas_call(
         functools.partial(cross_kernel, scale),
         grid=(bins // step_bins,),

time: 102 us -> 103 us (level)
  no operation moved by 1% of the time
where the time goes in v10:
time: 103 us; the launch traced here: 102 us
  waiting for transfers between devices  55.8 us (54%)
  starting transfers between devices  22.7 us (22%)
  local copies, waits for them, and re-layouts  15.8 us (15%)
  Pallas kernels  4.7 us (5%)
  other arithmetic  2.57 us (2%)
    all_to_all x1, waiting for transfers between devices, on_device(): lax.all_to_all(outgoing, 'chan', split_axis=0, concat_axis=0, tiled=True)  23.3 us
    all_to_all x1, waiting for transfers between devices, on_device(): lax.all_to_all(send, ('chan', 'seg'), split_axis=0, concat_axis=0, tiled=...  18.9 us
    all_to_all x1, starting transfers between devices, on_device(): lax.all_to_all(send, ('chan', 'seg'), split_axis=0, concat_axis=0, tiled=...  14.7 us
    ppermute x3, waiting for transfers between devices, on_device(): by_shift.append(lax.ppermute(part, 'seg', pairs))  13.5 us
    all_to_all x1, starting transfers between devices, on_device(): lax.all_to_all(outgoing, 'chan', split_axis=0, concat_axis=0, tiled=True)  7.05 us
    pallas_call x1, Pallas kernels, cross_spectra(): pl.pallas_call(functools.partial(cross_kernel, scale), grid=(bins // step...  4.7 us
    another operation x1, local copies, waits for them, and re-layouts, on_device(): jnp.stack([own, imag_rows], axis=1)  2.82 us
    gather x2, local copies, waits for them, and re-layouts, on_device(): own = jnp.take(by_shift, order, axis=0)  2.54 us
  transfers between devices with their start and end apart: 5, of which 4 were waited for; matrix products, arithmetic and copies ran while one was open for 13% of the time, Pallas kernels for 0%

profile of v10, /device:TPU:2, one launch (start us, length us, event | category | flops | bytes accessed | tf_op | source)
XLA Modules:
  0.0 102.1 jit_solution(14047975680289467242)
XLA Ops:
  0.0 0.0 copy-start
  0.0 0.7 broadcast_subtract_fusion
  0.7 0.3 copy-done
  1.1 0.3 fusion
  1.4 0.0 copy-start.1
  1.4 0.5 copy.10
  1.9 0.3 reshape.78
  2.3 1.2 %copy.11 = bf16[8,8,4,4,256]{4,3,2,1,0:T(4,128)(2,1)} copy(bf16[8,8,4,4,256]{4,0,2,3,1:T(8,128)(2,1)S(1)} %bitcast.36) | data formatting | bytes 1048576 | tf_op jit(solution)/shard_map/transpose | solution.py:67
  3.5 14.7 %all-to-all-start = ((bf16[256,4,256]{2,1,0:T(4,128)(2,1)}), bf16[256,4,256]{2,1,0:T(4,128)(2,1)S(1)}, u32[]{:S(2)}, u32[]{:S(2)}) async-start(bf16[256,4,256]{2,1,0:T(4,128)(2,1)} %bitcast.15), calls=%async_computation | async-start | bytes 1048576 | tf_op jit(solution)/shard_map/all_to_all | solution.py:68
  18.2 0.0 copy-done.1
  18.2 0.1 copy.12
  18.3 0.1 reshape.91
  18.4 18.9 %all-to-all-done = bf16[256,4,256]{2,1,0:T(4,128)(2,1)S(1)} async-done(((bf16[256,4,256]{2,1,0:T(4,128)(2,1)}), bf16[256,4,256]{2,1,0:T(4,128)(2,1)S(1)}, u32[]{:S(2)}, u32[]{:S(2)}) %all-to-all-start) | async-done | bytes 524320 | tf_op jit(solution)/shard_map/all_to_all | solution.py:68
  37.3 0.1 reshape.80
  37.5 2.1 %gather_fusion.1 = bf16[256,16,256]{2,1,0:T(8,128)(2,1)} fusion(bf16[64,16,256]{2,1,0:T(8,128)(2,1)S(1)} %reshape.80, s32[1024]{0:T(1024)S(1)} %pad_clamp_fusion), kind=kCustom, calls=%fused_computation.1 | custom fusion | bytes 4195328 | tf_op jit(solution)/shard_map/gather | solution.py:70
  39.5 7.1 %all-to-all-start.1 = ((bf16[64,4,16,256]{3,2,1,0:T(8,128)(2,1)}), bf16[64,4,16,256]{3,2,1,0:T(8,128)(2,1)S(1)}, u32[]{:S(2)}, u32[]{:S(2)}) async-start(bf16[64,4,16,256]{3,2,1,0:T(8,128)(2,1)} %bitcast.33), calls=%async_computation.1 | async-start | bytes 4194304 | tf_op jit(solution)/shard_map/all_to_all | solution.py:71
  46.6 1.3 %copy.6 = bf16[32,32,2,128]{3,2,1,0:T(2,128)(2,1)} copy(bf16[32,32,2,128]{3,1,2,0:T(8,128)(2,1)S(1)} %fusion) | data formatting | bytes 1048576 | tf_op jit(solution)/shard_map/convert_element_type | solution.py:63
  48.0 1.4 %reshape.75 = bf16[4,8,32,256]{3,2,1,0:T(8,128)(2,1)S(1)} reshape(bf16[32,32,2,128]{3,2,1,0:T(2,128)(2,1)} %copy.6) | data formatting | bytes 1048576 | tf_op jit(solution)/shard_map/reshape | solution.py:72
  49.4 0.1 collective-permute-start.2
  49.5 0.8 collective-permute-start.1
  50.3 0.1 collective-permute-start
  50.5 6.3 %collective-permute-done.2 = bf16[8,32,256]{2,1,0:T(8,128)(2,1)S(1)} collective-permute-done((bf16[8,32,256]{2,1,0:T(8,128)(2,1)S(1)}, bf16[8,32,256]{2,1,0:T(8,128)(2,1)S(1)}, u32[]{:S(2)}, u32[]{:S(2)}) %collective-permute-start.2) | collective-permute-done | bytes 131104 | tf_op jit(solution)/shard_map/ppermute | solution.py:77
  56.7 7.2 %collective-permute-done.1 = bf16[8,32,256]{2,1,0:T(8,128)(2,1)S(1)} collective-permute-done((bf16[8,32,256]{2,1,0:T(8,128)(2,1)S(1)}, bf16[8,32,256]{2,1,0:T(8,128)(2,1)S(1)}, u32[]{:S(2)}, u32[]{:S(2)}) %collective-permute-start.1) | collective-permute-done | bytes 131104 | tf_op jit(solution)/shard_map/ppermute | solution.py:77
  63.9 0.0 collective-permute-done
  63.9 0.1 pad_maximum_fusion.1
  64.0 1.4 %gather_fusion = bf16[4,8,32,256]{3,2,1,0:T(8,128)(2,1)} fusion(bf16[4,8,32,256]{3,2,1,0:T(8,128)(2,1)S(1)} %pad_maximum_fusion.1, s32[1024]{0:T(1024)S(1)} %pad_clamp_fusion.1), kind=kCustom, calls=%fused_computation | custom fusion | bytes 1048592 | tf_op jit(solution)/shard_map/jit(_take)/gather | solution.py:80
  65.4 1.2 %gather.10 = bf16[4,8,8,4,2,128]{5,4,3,2,1,0:T(2,128)(2,1)S(1)} reshape(bf16[4,8,32,256]{3,2,1,0:T(8,128)(2,1)} %gather_fusion) | data formatting | bytes 1048576 | tf_op jit(solution)/shard_map/jit(_take)/gather | solution.py:80
  66.6 0.5 fusion.2
  67.1 0.3 copy.7
  67.4 0.1 fusion.9
  67.5 0.1 maximum_bitcast_fusion
  67.6 1.1 %pad_maximum_fusion = bf16[8,2,128,2,128]{2,0,4,3,1:T(8,128)(2,1)} fusion(bf16[8,1,128,2,128]{2,0,4,3,1:T(8,128)(2,1)S(1)} %maximum_bitcast_fusion, bf16[8,1,128,2,128]{2,0,4,3,1:T(8,128)(2,1)S(1)} %bitcast.35), kind=kLoop, calls=%fused_computation.4 | loop fusion | flops 524288 | bytes 2097152 | tf_op jit(solution)/shard_map/stack | solution.py:84
  68.7 2.8 %copy.9 = bf16[8,2,128,2,128]{4,3,2,1,0:T(2,128)(2,1)} copy(bf16[8,2,128,2,128]{2,0,4,3,1:T(8,128)(2,1)} %pad_maximum_fusion) | data formatting | bytes 2097152 | tf_op jit(solution)/shard_map/stack | solution.py:84
  71.5 2.5 %reshape.77.lhs_ref = bf16[8,256,256]{2,1,0:T(8,128)(2,1)} reshape(bf16[8,2,128,2,128]{4,3,2,1,0:T(2,128)(2,1)} %copy.9) | data formatting | bytes 2097152 | tf_op jit(solution)/shard_map/reshape | solution.py:84
  74.0 23.3 %all-to-all-done.1.rhs_ref = bf16[64,4,16,256]{3,2,1,0:T(8,128)(2,1)S(1)} async-done(((bf16[64,4,16,256]{3,2,1,0:T(8,128)(2,1)}), bf16[64,4,16,256]{3,2,1,0:T(8,128)(2,1)S(1)}, u32[]{:S(2)}, u32[]{:S(2)}) %all-to-all-start.1) | async-done | bytes 2097184 | tf_op jit(solution)/shard_map/all_to_all | solution.py:71
  97.4 4.7 %shard_map.37 = f32[4,8,2,128,128]{4,3,2,1,0:T(8,128)} custom-call(bf16[8,256,256]{2,1,0:T(8,128)(2,1)} %reshape.77.lhs_ref, bf16[64,4,16,256]{3,2,1,0:T(8,128)(2,1)S(1)} %all-to-all-done.1.rhs_ref), custom_call_target="tpu_custom_call" | custom-call | flops 536870912 | bytes 7340032 | tf_op jit(solution)/shard_map/pallas_call | solution.py:34
  (6 shorter events, 0.1 us)
Async XLA Ops:
  0.0 1.1 %copy-start = (bf16[32,32,2,128]{3,2,1,0:T(2,128)(2,1)S(1)}, bf16[32,32,2,128]{3,2,1,0:T(2,128)(2,1)}, u32[]{:S(2)}) copy-start(bf16[32,32,2,128]{3,2,1,0:T(2,128)(2,1)} %param.3) | copy-start | bytes 1572868
  1.4 16.8 %copy-start.1 = (s32[4,64]{1,0:T(4,128)S(1)}, s32[4,64]{1,0:T(4,128)}, u32[]{:S(2)}) copy-start(s32[4,64]{1,0:T(4,128)} %param.4) | copy-start | bytes 3076
  3.5 33.9 %all-to-all-start = ((bf16[256,4,256]{2,1,0:T(4,128)(2,1)}), bf16[256,4,256]{2,1,0:T(4,128)(2,1)S(1)}, u32[]{:S(2)}, u32[]{:S(2)}) async-start(bf16[256,4,256]{2,1,0:T(4,128)(2,1)} %bitcast.15), calls=%async_computation | async-start | bytes 1048576 | tf_op jit(solution)/shard_map/all_to_all | solution.py:68
  39.5 57.8 %all-to-all-start.1 = ((bf16[64,4,16,256]{3,2,1,0:T(8,128)(2,1)}), bf16[64,4,16,256]{3,2,1,0:T(8,128)(2,1)S(1)}, u32[]{:S(2)}, u32[]{:S(2)}) async-start(bf16[64,4,16,256]{3,2,1,0:T(8,128)(2,1)} %bitcast.33), calls=%async_computation.1 | async-start | bytes 4194304 | tf_op jit(solution)/shard_map/all_to_all | solution.py:71
  49.4 7.3 %collective-permute-start.2 = (bf16[8,32,256]{2,1,0:T(8,128)(2,1)S(1)}, bf16[8,32,256]{2,1,0:T(8,128)(2,1)S(1)}, u32[]{:S(2)}, u32[]{:S(2)}) collective-permute-start(bf16[8,32,256]{2,1,0:T(8,128)(2,1)S(1)} %get-tuple-element.8), channel_id=1, source_target_pairs={{0,3},{1,0},{2,1},{3,2},{4,7},{5,4},{6,5},{7,6},{8,11},{9,8},{10,9... | collective-permute-start | bytes 393224 | tf_op jit(solution)/shard_map/ppermute | solution.py:77
  49.5 14.4 %collective-permute-start.1 = (bf16[8,32,256]{2,1,0:T(8,128)(2,1)S(1)}, bf16[8,32,256]{2,1,0:T(8,128)(2,1)S(1)}, u32[]{:S(2)}, u32[]{:S(2)}) collective-permute-start(bf16[8,32,256]{2,1,0:T(8,128)(2,1)S(1)} %get-tuple-element.9), channel_id=1, source_target_pairs={{0,2},{1,3},{2,0},{3,1},{4,6},{5,7},{6,4},{7,5},{8,10},{9,11},{10,... | collective-permute-start | bytes 393224 | tf_op jit(solution)/shard_map/ppermute | solution.py:77
  50.3 13.7 %collective-permute-start = (bf16[8,32,256]{2,1,0:T(8,128)(2,1)S(1)}, bf16[8,32,256]{2,1,0:T(8,128)(2,1)S(1)}, u32[]{:S(2)}, u32[]{:S(2)}) collective-permute-start(bf16[8,32,256]{2,1,0:T(8,128)(2,1)S(1)} %get-tuple-element.10), channel_id=1, source_target_pairs={{0,1},{1,2},{2,3},{3,0},{4,5},{5,6},{6,7},{7,4},{8,9},{9,10},{10,1... | collective-permute-start | bytes 393224 | tf_op jit(solution)/shard_map/ppermute | solution.py:77

commit v11 on v8

--- a/solution.py
+++ b/solution.py
@@ -58,17 +58,19 @@
     scale = 1.0 / math.sqrt(win_count)
     local_slots = assignment - lax.axis_index("chan") * chan_width
     onehot = (local_slots[None, :] == jnp.arange(chan_width, dtype=local_slots.dtype)[:, None])
-    ordered = jnp.einsum(
-        "fwkm,mc->fwkc", spectra, onehot.astype(spectra.dtype), preferred_element_type=jnp.float32
-    ).astype(spectra.dtype)
     per_bin = group_count // my_bins
     win_piece = win_local // per_bin
-    rows = ordered.reshape(seg_count, my_bins, per_bin, win_piece, 2 * chan_width)
-    send = rows.transpose(1, 2, 0, 3, 4).reshape(group_count * seg_count, win_piece, 2 * chan_width)
+    pieces = spectra.reshape(seg_count, my_bins, per_bin, win_piece, 2, chan_width).transpose(1, 2, 0, 3, 4, 5)
+    send = jnp.einsum(
+        "fqsrkm,mc->fqsrkc", pieces, onehot.astype(spectra.dtype), preferred_element_type=jnp.float32
+    ).astype(spectra.dtype).reshape(group_count * seg_count, win_piece, 2 * chan_width)
     held = lax.all_to_all(send, ("chan", "seg"), split_axis=0, concat_axis=0, tiled=True)
     held = held.reshape(group_count, seg_count * win_piece, 2 * chan_width)
     outgoing = held.at[plan.T].get(mode="promise_in_bounds")
     arrived = lax.all_to_all(outgoing, "chan", split_axis=0, concat_axis=0, tiled=True)
+    ordered = jnp.einsum(
+        "fwkm,mc->fwkc", spectra, onehot.astype(spectra.dtype), preferred_element_type=jnp.float32
+    ).astype(spectra.dtype)
     ranges = ordered.reshape(seg_count, my_bins, win_local, 2 * chan_width)
     by_shift = [lax.dynamic_index_in_dim(ranges, seg_index, 0, keepdims=False)]
     for shift in range(1, seg_count):

time: 102 us -> 102 us (level)
  local copies, waits for them, and re-layouts: 15.8 us -> 10 us
  waiting for transfers between devices: 55.8 us -> 61.3 us
  matrix products: 0.29 us -> 1.62 us
  other arithmetic: 2.57 us -> 1.5 us
    all_to_all x1, waiting for transfers between devices: 23.3 us -> 27.4 us  [on_device(): lax.all_to_all(outgoing, 'chan', split_axis=0, concat_axis=0, tiled=True)]
    gather x2, local copies, waits for them, and re-layouts: 2.54 us -> 0.71 us  [on_device(): own = jnp.take(by_shift, order, axis=0)]
    ppermute x3, waiting for transfers between devices: 13.5 us -> 15 us  [on_device(): by_shift.append(lax.ppermute(part, 'seg', pairs))]
    convert_element_type x2 -> x1, local copies, waits for them, and re-layouts: 1.86 us -> 0.51 us  [on_device(): ordered = jnp.einsum('fwkm,mc->fwkc', spectra, onehot.astype(spectra.dtyp...]
    dot_general x0 -> x1, matrix products: none -> 1.33 us  [on_device(): jnp.einsum('fqsrkm,mc->fqsrkc', pieces, onehot.astype(spectra.dtype), pre...]
    reshape x1 -> x2, local copies, waits for them, and re-layouts: 0.34 us -> 1.56 us  [on_device(): send = jnp.einsum('fqsrkm,mc->fqsrkc', pieces, onehot.astype(spectra.dtyp...]
    another operation x1, local copies, waits for them, and re-layouts: 2.82 us -> 1.61 us  [on_device(): jnp.stack([own, imag_rows], axis=1)]
    transpose x1 -> x0, local copies, waits for them, and re-layouts: 1.2 us -> none  [on_device(): rows.transpose(1, 2, 0, 3, 4)]
  transfers between devices with their start and end apart: 5 -> 5, of which waited for: 4 -> 4; matrix products, arithmetic and copies ran while one was open for 13% -> 7% of each run, Pallas kernels for 0% -> 0%
where the time goes in v11:
time: 102 us; the launch traced here: 101 us
  waiting for transfers between devices  61.3 us (60%)
  starting transfers between devices  22.9 us (22%)
  local copies, waits for them, and re-layouts  10 us (10%)
  Pallas kernels  3.76 us (4%)
  matrix products  1.62 us (2%)
  other arithmetic  1.5 us (1%)
    all_to_all x1, waiting for transfers between devices, on_device(): lax.all_to_all(outgoing, 'chan', split_axis=0, concat_axis=0, tiled=True)  27.4 us
    all_to_all x1, waiting for transfers between devices, on_device(): lax.all_to_all(send, ('chan', 'seg'), split_axis=0, concat_axis=0, tiled=...  18.9 us
    ppermute x3, waiting for transfers between devices, on_device(): by_shift.append(lax.ppermute(part, 'seg', pairs))  15 us
    all_to_all x1, starting transfers between devices, on_device(): lax.all_to_all(send, ('chan', 'seg'), split_axis=0, concat_axis=0, tiled=...  14.7 us
    all_to_all x1, starting transfers between devices, on_device(): lax.all_to_all(outgoing, 'chan', split_axis=0, concat_axis=0, tiled=True)  7.18 us
    pallas_call x1, Pallas kernels, cross_spectra(): pl.pallas_call(functools.partial(cross_kernel, scale), grid=(bins // step...  3.76 us
    reshape x1, local copies, waits for them, and re-layouts, on_device(): jnp.stack([own, imag_rows], axis=1)  2.52 us
    gather x1, local copies, waits for them, and re-layouts, on_device(): outgoing = held.at[plan.T].get(mode='promise_in_bounds')  2.07 us
  transfers between devices with their start and end apart: 5, of which 4 were waited for; matrix products, arithmetic and copies ran while one was open for 7% of the time, Pallas kernels for 0%

profile of v11, /device:TPU:2, one launch (start us, length us, event | category | flops | bytes accessed | tf_op | source)
XLA Modules:
  0.0 101.4 jit_solution(14492379089008686771)
XLA Ops:
  0.0 0.7 broadcast_subtract_fusion
  0.7 1.3 %fusion.1 = bf16[8,8,4,4,2,128]{5,1,4,3,2,0:T(8,128)(2,1)S(1)} fusion(bf16[4,8,8,4,2,128]{5,4,3,2,1,0:T(2,128)(2,1)} %bitcast.43, s32[128]{0:T(128)S(1)} %broadcast_subtract_fusion), kind=kOutput, calls=%fused_computation.5 | convolution fusion | flops 67387392 | bytes 1049088 | tf_op jit(solution)/shard_map/fqsrkm,mc->fqsrkc/dot_general | solution.py:64
  2.0 0.0 copy-start.1
  2.0 0.4 copy.34
  2.5 1.1 %reshape.101 = bf16[256,4,256]{2,1,0:T(4,128)(2,1)} reshape(bf16[8,8,4,4,2,128]{5,4,3,2,1,0:T(2,128)(2,1)S(1)} %copy.34) | data formatting | bytes 1048576 | tf_op jit(solution)/shard_map/reshape | solution.py:66
  3.6 14.7 %all-to-all-start = ((bf16[256,4,256]{2,1,0:T(4,128)(2,1)}), bf16[256,4,256]{2,1,0:T(4,128)(2,1)S(1)}, u32[]{:S(2)}, u32[]{:S(2)}) async-start(bf16[256,4,256]{2,1,0:T(4,128)(2,1)} %reshape.101), calls=%async_computation | async-start | bytes 1048576 | tf_op jit(solution)/shard_map/all_to_all | solution.py:67
  18.3 0.0 copy-done.1
  18.3 0.1 copy.31
  18.4 0.1 reshape.91
  18.5 18.9 %all-to-all-done = bf16[256,4,256]{2,1,0:T(4,128)(2,1)S(1)} async-done(((bf16[256,4,256]{2,1,0:T(4,128)(2,1)}), bf16[256,4,256]{2,1,0:T(4,128)(2,1)S(1)}, u32[]{:S(2)}, u32[]{:S(2)}) %all-to-all-start) | async-done | bytes 524320 | tf_op jit(solution)/shard_map/all_to_all | solution.py:67
  37.4 0.1 reshape.80
  37.6 2.1 %gather_fusion.1 = bf16[256,16,256]{2,1,0:T(8,128)(2,1)} fusion(bf16[64,16,256]{2,1,0:T(8,128)(2,1)S(1)} %reshape.80, s32[1024]{0:T(1024)S(1)} %pad_clamp_fusion), kind=kCustom, calls=%fused_computation.1 | custom fusion | bytes 4195328 | tf_op jit(solution)/shard_map/gather | solution.py:69
  39.7 0.0 copy-start
  39.7 7.2 %all-to-all-start.1 = ((bf16[64,4,16,256]{3,2,1,0:T(8,128)(2,1)}), bf16[64,4,16,256]{3,2,1,0:T(8,128)(2,1)S(1)}, u32[]{:S(2)}, u32[]{:S(2)}) async-start(bf16[64,4,16,256]{3,2,1,0:T(8,128)(2,1)} %bitcast.40), calls=%async_computation.1 | async-start | bytes 4194304 | tf_op jit(solution)/shard_map/all_to_all | solution.py:70
  46.9 0.0 copy-done
  46.9 0.3 fusion
  47.2 0.5 copy.24
  47.7 0.3 reshape.75
  48.1 0.1 collective-permute-start.2
  48.2 0.8 collective-permute-start.1
  49.0 0.1 collective-permute-start
  49.2 6.8 %collective-permute-done.2 = bf16[8,32,256]{2,1,0:T(8,128)(2,1)S(1)} collective-permute-done((bf16[8,32,256]{2,1,0:T(8,128)(2,1)S(1)}, bf16[8,32,256]{2,1,0:T(8,128)(2,1)S(1)}, u32[]{:S(2)}, u32[]{:S(2)}) %collective-permute-start.2) | collective-permute-done | bytes 131104 | tf_op jit(solution)/shard_map/ppermute | solution.py:79
  56.0 8.2 %collective-permute-done.1 = bf16[8,32,256]{2,1,0:T(8,128)(2,1)S(1)} collective-permute-done((bf16[8,32,256]{2,1,0:T(8,128)(2,1)S(1)}, bf16[8,32,256]{2,1,0:T(8,128)(2,1)S(1)}, u32[]{:S(2)}, u32[]{:S(2)}) %collective-permute-start.1) | collective-permute-done | bytes 131104 | tf_op jit(solution)/shard_map/ppermute | solution.py:79
  64.2 0.0 collective-permute-done
  64.2 0.1 pad_maximum_fusion.1
  64.3 0.6 gather_fusion
  64.9 0.1 gather.10
  65.0 0.5 fusion.5
  65.5 0.3 copy.25
  65.9 0.1 fusion.15
  65.9 0.1 maximum_bitcast_fusion
  66.0 0.1 pad_maximum_fusion
  66.1 1.6 %copy.27 = bf16[8,2,128,2,128]{4,3,2,1,0:T(2,128)(2,1)} copy(bf16[8,2,128,2,128]{2,0,4,3,1:T(8,128)(2,1)S(1)} %pad_maximum_fusion) | data formatting | bytes 2097152 | tf_op jit(solution)/shard_map/stack | solution.py:86
  67.7 2.5 %reshape.77.lhs_ref = bf16[8,256,256]{2,1,0:T(8,128)(2,1)} reshape(bf16[8,2,128,2,128]{4,3,2,1,0:T(2,128)(2,1)} %copy.27) | data formatting | bytes 2097152 | tf_op jit(solution)/shard_map/reshape | solution.py:86
  70.2 27.4 %all-to-all-done.1.rhs_ref = bf16[64,4,16,256]{3,2,1,0:T(8,128)(2,1)S(1)} async-done(((bf16[64,4,16,256]{3,2,1,0:T(8,128)(2,1)}), bf16[64,4,16,256]{3,2,1,0:T(8,128)(2,1)S(1)}, u32[]{:S(2)}, u32[]{:S(2)}) %all-to-all-start.1) | async-done | bytes 2097184 | tf_op jit(solution)/shard_map/all_to_all | solution.py:70
  97.6 3.8 %shard_map.37 = f32[4,8,2,128,128]{4,3,2,1,0:T(8,128)} custom-call(bf16[8,256,256]{2,1,0:T(8,128)(2,1)} %reshape.77.lhs_ref, bf16[64,4,16,256]{3,2,1,0:T(8,128)(2,1)S(1)} %all-to-all-done.1.rhs_ref), custom_call_target="tpu_custom_call" | custom-call | flops 536870912 | bytes 7340032 | tf_op jit(solution)/shard_map/pallas_call | solution.py:34
  (6 shorter events, 0.1 us)
Async XLA Ops:
  2.0 16.3 %copy-start.1 = (s32[4,64]{1,0:T(4,128)S(1)}, s32[4,64]{1,0:T(4,128)}, u32[]{:S(2)}) copy-start(s32[4,64]{1,0:T(4,128)} %param.4) | copy-start | bytes 3076
  3.6 33.9 %all-to-all-start = ((bf16[256,4,256]{2,1,0:T(4,128)(2,1)}), bf16[256,4,256]{2,1,0:T(4,128)(2,1)S(1)}, u32[]{:S(2)}, u32[]{:S(2)}) async-start(bf16[256,4,256]{2,1,0:T(4,128)(2,1)} %reshape.101), calls=%async_computation | async-start | bytes 1048576 | tf_op jit(solution)/shard_map/all_to_all | solution.py:67
  39.7 7.2 %copy-start = (bf16[32,32,2,128]{3,2,1,0:T(2,128)(2,1)S(1)}, bf16[32,32,2,128]{3,2,1,0:T(2,128)(2,1)}, u32[]{:S(2)}) copy-start(bf16[32,32,2,128]{3,2,1,0:T(2,128)(2,1)} %param.3) | copy-start | bytes 1572868
  39.7 58.0 %all-to-all-start.1 = ((bf16[64,4,16,256]{3,2,1,0:T(8,128)(2,1)}), bf16[64,4,16,256]{3,2,1,0:T(8,128)(2,1)S(1)}, u32[]{:S(2)}, u32[]{:S(2)}) async-start(bf16[64,4,16,256]{3,2,1,0:T(8,128)(2,1)} %bitcast.40), calls=%async_computation.1 | async-start | bytes 4194304 | tf_op jit(solution)/shard_map/all_to_all | solution.py:70
  48.1 7.9 %collective-permute-start.2 = (bf16[8,32,256]{2,1,0:T(8,128)(2,1)S(1)}, bf16[8,32,256]{2,1,0:T(8,128)(2,1)S(1)}, u32[]{:S(2)}, u32[]{:S(2)}) collective-permute-start(bf16[8,32,256]{2,1,0:T(8,128)(2,1)S(1)} %get-tuple-element.8), channel_id=1, source_target_pairs={{0,3},{1,0},{2,1},{3,2},{4,7},{5,4},{6,5},{7,6},{8,11},{9,8},{10,9... | collective-permute-start | bytes 393224 | tf_op jit(solution)/shard_map/ppermute | solution.py:79
  48.2 16.0 %collective-permute-start.1 = (bf16[8,32,256]{2,1,0:T(8,128)(2,1)S(1)}, bf16[8,32,256]{2,1,0:T(8,128)(2,1)S(1)}, u32[]{:S(2)}, u32[]{:S(2)}) collective-permute-start(bf16[8,32,256]{2,1,0:T(8,128)(2,1)S(1)} %get-tuple-element.9), channel_id=1, source_target_pairs={{0,2},{1,3},{2,0},{3,1},{4,6},{5,7},{6,4},{7,5},{8,10},{9,11},{10,... | collective-permute-start | bytes 393224 | tf_op jit(solution)/shard_map/ppermute | solution.py:79
  49.0 15.2 %collective-permute-start = (bf16[8,32,256]{2,1,0:T(8,128)(2,1)S(1)}, bf16[8,32,256]{2,1,0:T(8,128)(2,1)S(1)}, u32[]{:S(2)}, u32[]{:S(2)}) collective-permute-start(bf16[8,32,256]{2,1,0:T(8,128)(2,1)S(1)} %get-tuple-element.10), channel_id=1, source_target_pairs={{0,1},{1,2},{2,3},{3,0},{4,5},{5,6},{6,7},{7,4},{8,9},{9,10},{10,1... | collective-permute-start | bytes 393224 | tf_op jit(solution)/shard_map/ppermute | solution.py:79

commit v12 on v8

--- a/solution.py
+++ b/solution.py
@@ -11,16 +11,14 @@
 
 def cross_kernel(scale, lhs_ref, rhs_ref, out_ref):
     step_bins = lhs_ref.shape[0]
-    pieces, rounds, rows, two_chan = rhs_ref.shape
+    pieces, rounds, rows, chan = rhs_ref.shape
     per_bin = pieces // (step_bins * pl.num_programs(0))
-    chan = two_chan // 2
     first = pl.program_id(0) * step_bins
     for b in range(step_bins):
         lhs = lhs_ref[b]
         for r in range(rounds):
             block = rhs_ref[pl.ds((first + b) * per_bin, per_bin), r]
-            block = block.reshape(per_bin * rows, two_chan)
-            block = jnp.concatenate([block[:, :chan], block[:, chan:]], axis=0)
+            block = block.reshape(per_bin * rows, chan)
             acc = jnp.dot(lhs, block, preferred_element_type=jnp.float32)
             out_ref[r, b] = (acc * scale).reshape(2, chan, chan)
 
@@ -64,9 +62,9 @@
     per_bin = group_count // my_bins
     win_piece = win_local // per_bin
     rows = ordered.reshape(seg_count, my_bins, per_bin, win_piece, 2 * chan_width)
-    send = rows.transpose(1, 2, 0, 3, 4).reshape(group_count * seg_count, win_piece, 2 * chan_width)
+    send = rows.transpose(1, 2, 0, 3, 4).reshape(group_count * seg_count, win_piece * 2, chan_width)
     held = lax.all_to_all(send, ("chan", "seg"), split_axis=0, concat_axis=0, tiled=True)
-    held = held.reshape(group_count, seg_count * win_piece, 2 * chan_width)
+    held = held.reshape(group_count, seg_count * win_piece * 2, chan_width)
     outgoing = held.at[plan.T].get(mode="promise_in_bounds")
     arrived = lax.all_to_all(outgoing, "chan", split_axis=0, concat_axis=0, tiled=True)
     ranges = ordered.reshape(seg_count, my_bins, win_local, 2 * chan_width)
@@ -79,9 +77,9 @@
     order = (seg_index - jnp.arange(seg_count)) % seg_count
     own = jnp.take(by_shift, order, axis=0)
     own = own.reshape(seg_count, my_bins, per_bin, win_piece, 2, chan_width)
-    own = own.transpose(1, 5, 4, 2, 0, 3).reshape(my_bins, chan_width, 2, win_count)
-    imag_rows = jnp.stack([own[:, :, 1], -own[:, :, 0]], axis=2)
-    lhs = jnp.stack([own, imag_rows], axis=1).reshape(my_bins, 2 * chan_width, 2 * win_count)
+    imag_rows = jnp.stack([own[:, :, :, :, 1], -own[:, :, :, :, 0]], axis=4)
+    lhs = jnp.stack([own, imag_rows], axis=0).transpose(2, 0, 6, 3, 1, 4, 5)
+    lhs = lhs.reshape(my_bins, 2 * chan_width, 2 * win_count)
     return cross_spectra(lhs, arrived, scale)
 
 

time: 102 us -> 102 us (level)
  waiting for transfers between devices: 55.8 us -> 48.4 us
  other arithmetic: 2.57 us -> 7.32 us
  local copies, waits for them, and re-layouts: 15.8 us -> 18.6 us
    all_to_all x1, waiting for transfers between devices: 23.3 us -> 16 us  [on_device(): lax.all_to_all(outgoing, 'chan', split_axis=0, concat_axis=0, tiled=True)]
    reshape x2 -> x3, local copies, waits for them, and re-layouts: 2.64 us -> 5.75 us  [the longest x2 4.76 us: on_device(): lhs = lhs.reshape(my_bins, 2 * chan_width, 2 * win_count)]
    another operation x1 -> x0, local copies, waits for them, and re-layouts: 2.82 us -> none  [on_device(): jnp.stack([own, imag_rows], axis=1)]
    transpose x1, local copies, waits for them, and re-layouts: 0.34 us -> 2.62 us  [on_device(): lhs = jnp.stack([own, imag_rows], axis=0).transpose(2, 0, 6, 3, 1, 4, 5)]
    select_n x1 -> x3, other arithmetic: 0.01 us -> 2.1 us  [on_device(): own = jnp.take(by_shift, order, axis=0)]
    gather x2 -> x3, local copies, waits for them, and re-layouts: 2.54 us -> 3.44 us  [on_device(): own = jnp.take(by_shift, order, axis=0)]
  transfers between devices with their start and end apart: 5 -> 5, of which waited for: 4 -> 4; matrix products, arithmetic and copies ran while one was open for 13% -> 20% of each run, Pallas kernels for 0% -> 0%
where the time goes in v12:
time: 102 us; the launch traced here: 101 us
  waiting for transfers between devices  48.4 us (47%)
  starting transfers between devices  22.7 us (22%)
  local copies, waits for them, and re-layouts  18.6 us (18%)
  other arithmetic  7.32 us (7%)
  Pallas kernels  3.76 us (4%)
    all_to_all x1, waiting for transfers between devices, on_device(): lax.all_to_all(send, ('chan', 'seg'), split_axis=0, concat_axis=0, tiled=...  18.9 us
    all_to_all x1, waiting for transfers between devices, on_device(): lax.all_to_all(outgoing, 'chan', split_axis=0, concat_axis=0, tiled=True)  16 us
    all_to_all x1, starting transfers between devices, on_device(): lax.all_to_all(send, ('chan', 'seg'), split_axis=0, concat_axis=0, tiled=...  14.7 us
    ppermute x3, waiting for transfers between devices, on_device(): by_shift.append(lax.ppermute(part, 'seg', pairs))  13.5 us
    all_to_all x1, starting transfers between devices, on_device(): lax.all_to_all(outgoing, 'chan', split_axis=0, concat_axis=0, tiled=True)  7.05 us
    reshape x2, local copies, waits for them, and re-layouts, on_device(): lhs = lhs.reshape(my_bins, 2 * chan_width, 2 * win_count)  4.76 us
    pallas_call x1, Pallas kernels, cross_spectra(): pl.pallas_call(functools.partial(cross_kernel, scale), grid=(bins // step...  3.76 us
    gather x3, local copies, waits for them, and re-layouts, on_device(): own = jnp.take(by_shift, order, axis=0)  3.44 us
  transfers between devices with their start and end apart: 5, of which 4 were waited for; matrix products, arithmetic and copies ran while one was open for 20% of the time, Pallas kernels for 0%

profile of v12, /device:TPU:2, one launch (start us, length us, event | category | flops | bytes accessed | tf_op | source)
XLA Modules:
  0.0 101.3 jit_solution(10696610014031114327)
XLA Ops:
  0.0 0.0 copy-start
  0.0 0.7 broadcast_subtract_fusion
  0.7 0.3 copy-done
  1.1 0.3 fusion
  1.4 0.5 copy.8
  1.9 0.0 copy-start.2
  1.9 0.3 reshape.84
  2.3 0.4 copy.9
  2.7 1.0 reshape.85
  3.7 14.7 %all-to-all-start = ((bf16[256,8,128]{2,1,0:T(8,128)(2,1)}), bf16[256,8,128]{2,1,0:T(8,128)(2,1)S(1)}, u32[]{:S(2)}, u32[]{:S(2)}) async-start(bf16[256,8,128]{2,1,0:T(8,128)(2,1)} %reshape.85), calls=%async_computation | async-start | bytes 1048576 | tf_op jit(solution)/shard_map/all_to_all | solution.py:66
  18.4 0.0 copy-done.2
  18.4 0.1 copy.10
  18.5 0.1 reshape.97
  18.6 18.9 %all-to-all-done = bf16[256,8,128]{2,1,0:T(8,128)(2,1)S(1)} async-done(((bf16[256,8,128]{2,1,0:T(8,128)(2,1)}), bf16[256,8,128]{2,1,0:T(8,128)(2,1)S(1)}, u32[]{:S(2)}, u32[]{:S(2)}) %all-to-all-start) | async-done | bytes 524320 | tf_op jit(solution)/shard_map/all_to_all | solution.py:66
  37.5 2.2 %gather_fusion.1 = bf16[256,32,128]{2,1,0:T(8,128)(2,1)} fusion(bf16[64,32,128]{2,1,0:T(8,128)(2,1)S(1)} %bitcast.35, s32[1024]{0:T(1024)S(1)} %pad_clamp_fusion), kind=kCustom, calls=%fused_computation.1 | custom fusion | bytes 4195328 | tf_op jit(solution)/shard_map/gather | solution.py:68
  39.7 7.1 %all-to-all-start.1 = ((bf16[64,4,32,128]{3,2,1,0:T(8,128)(2,1)}), bf16[64,4,32,128]{3,2,1,0:T(8,128)(2,1)S(1)}, u32[]{:S(2)}, u32[]{:S(2)}) async-start(bf16[64,4,32,128]{3,2,1,0:T(8,128)(2,1)} %bitcast.36), calls=%async_computation.1 | async-start | bytes 4194304 | tf_op jit(solution)/shard_map/all_to_all | solution.py:69
  46.8 1.3 %copy.6 = bf16[32,32,2,128]{3,2,1,0:T(2,128)(2,1)} copy(bf16[32,32,2,128]{3,1,2,0:T(8,128)(2,1)S(1)} %fusion) | data formatting | bytes 1048576 | tf_op jit(solution)/shard_map/convert_element_type | solution.py:61
  48.1 1.4 %reshape.82 = bf16[4,8,32,256]{3,2,1,0:T(8,128)(2,1)S(1)} reshape(bf16[32,32,2,128]{3,2,1,0:T(2,128)(2,1)} %copy.6) | data formatting | bytes 1048576 | tf_op jit(solution)/shard_map/reshape | solution.py:70
  49.6 0.1 collective-permute-start.2
  49.7 0.8 collective-permute-start.1
  50.4 0.1 collective-permute-start
  50.6 6.3 %collective-permute-done.2 = bf16[8,32,256]{2,1,0:T(8,128)(2,1)S(1)} collective-permute-done((bf16[8,32,256]{2,1,0:T(8,128)(2,1)S(1)}, bf16[8,32,256]{2,1,0:T(8,128)(2,1)S(1)}, u32[]{:S(2)}, u32[]{:S(2)}) %collective-permute-start.2) | collective-permute-done | bytes 131104 | tf_op jit(solution)/shard_map/ppermute | solution.py:75
  56.9 7.2 %collective-permute-done.1 = bf16[8,32,256]{2,1,0:T(8,128)(2,1)S(1)} collective-permute-done((bf16[8,32,256]{2,1,0:T(8,128)(2,1)S(1)}, bf16[8,32,256]{2,1,0:T(8,128)(2,1)S(1)}, u32[]{:S(2)}, u32[]{:S(2)}) %collective-permute-start.1) | collective-permute-done | bytes 131104 | tf_op jit(solution)/shard_map/ppermute | solution.py:75
  64.1 0.0 collective-permute-done
  64.1 0.9 pad_maximum_fusion
  65.0 1.6 %gather_fusion = bf16[4,8,32,256]{3,2,1,0:T(8,128)(2,1)S(1)} fusion(bf16[4,8,32,256]{3,2,1,0:T(8,128)(2,1)} %pad_maximum_fusion, s32[1024]{0:T(1024)S(1)} %pad_clamp_fusion.1), kind=kCustom, calls=%fused_computation | custom fusion | bytes 1048592 | tf_op jit(solution)/shard_map/jit(_take)/gather | solution.py:78
  66.6 0.9 gather.12
  67.5 0.9 gather.13
  68.4 1.6 %broadcast_select_fusion = bf16[4,8,8,4,2,128]{5,4,3,2,1,0:T(2,128)(2,1)S(1)} fusion(bf16[4,8,8,4,2,128]{5,4,3,2,1,0:T(2,128)(2,1)} %gather.13, pred[4]{0:T(512)(128)(4,1)S(1)} %compare_and_fusion), kind=kLoop, calls=%fused_computation.5 | loop fusion | flops 262144 | bytes 1048580 | tf_op jit(solution)/shard_map/jit(_take)/select_n | solution.py:78
  70.0 0.0 copy-start.1
  70.0 0.9 fusion.8
  71.0 1.2 %maximum_bitcast_fusion.1 = bf16[1,4,8,8,4,2,128]{6,5,4,3,2,1,0:T(2,128)(2,1)S(1)} fusion(bf16[4,8,8,4,1,128]{5,4,3,2,1,0:T(2,128)(2,1)S(1)} %get-tuple-element.6, bf16[4,8,8,4,1,128]{5,4,3,2,1,0:T(2,128)(2,1)S(1)} %get-tuple-element.5), kind=kLoop, calls=%fused_computation.9 | loop fusion | flops 1048576 | bytes 1048576 | tf_op jit(solution)/shard_map/stack | solution.py:81
  72.2 0.0 copy-done.1
  72.2 0.5 broadcast_select_fusion.1
  72.7 1.5 %maximum_bitcast_fusion = bf16[8,2,128,8,4,4,2]{2,6,5,3,0,4,1:T(2,128)(2,1)S(1)} fusion(bf16[1,4,8,8,4,2,128]{6,5,4,3,2,1,0:T(2,128)(2,1)S(1)} %maximum_bitcast_fusion.1, bf16[1,4,8,8,4,2,128]{6,5,4,3,2,1,0:T(2,128)(2,1)S(1)} %broadcast_select_fusion.1), kind=kLoop, calls=%fused_computation.4 | loop fusion | flops 524288 | bytes 2097152 | tf_op jit(solution)/shard_map/transpose | solution.py:81
  74.2 2.6 %copy.7 = bf16[8,2,128,8,4,4,2]{2,1,6,5,4,3,0:T(2,128)(2,1)} copy(bf16[8,2,128,8,4,4,2]{2,6,5,3,0,4,1:T(2,128)(2,1)S(1)} %maximum_bitcast_fusion) | data formatting | bytes 2097152 | tf_op jit(solution)/shard_map/transpose | solution.py:81
  76.8 2.5 %reshape.83 = bf16[8,256,256]{1,2,0:T(8,128)(2,1)} reshape(bf16[8,2,128,8,4,4,2]{2,1,6,5,4,3,0:T(2,128)(2,1)} %copy.7) | data formatting | bytes 2097152 | tf_op jit(solution)/shard_map/reshape | solution.py:82
  79.3 2.3 %copy.11.lhs_ref = bf16[8,256,256]{2,1,0:T(8,128)(2,1)} copy(bf16[8,256,256]{1,2,0:T(8,128)(2,1)} %reshape.83) | data formatting | bytes 2097152 | tf_op jit(solution)/shard_map/reshape | solution.py:82
  81.6 16.0 %all-to-all-done.1.rhs_ref = bf16[64,4,32,128]{3,2,1,0:T(8,128)(2,1)S(1)} async-done(((bf16[64,4,32,128]{3,2,1,0:T(8,128)(2,1)}), bf16[64,4,32,128]{3,2,1,0:T(8,128)(2,1)S(1)}, u32[]{:S(2)}, u32[]{:S(2)}) %all-to-all-start.1) | async-done | bytes 2097184 | tf_op jit(solution)/shard_map/all_to_all | solution.py:69
  97.5 3.8 %shard_map.37 = f32[4,8,2,128,128]{4,3,2,1,0:T(8,128)} custom-call(bf16[8,256,256]{2,1,0:T(8,128)(2,1)} %copy.11.lhs_ref, bf16[64,4,32,128]{3,2,1,0:T(8,128)(2,1)S(1)} %all-to-all-done.1.rhs_ref), custom_call_target="tpu_custom_call" | custom-call | flops 536870912 | bytes 7340032 | tf_op jit(solution)/shard_map/pallas_call | solution.py:32
  (6 shorter events, 0.1 us)
Async XLA Ops:
  0.0 1.1 %copy-start = (bf16[32,32,2,128]{3,2,1,0:T(2,128)(2,1)S(1)}, bf16[32,32,2,128]{3,2,1,0:T(2,128)(2,1)}, u32[]{:S(2)}) copy-start(bf16[32,32,2,128]{3,2,1,0:T(2,128)(2,1)} %param.3) | copy-start | bytes 1572868
  1.9 16.5 %copy-start.2 = (s32[4,64]{1,0:T(4,128)S(1)}, s32[4,64]{1,0:T(4,128)}, u32[]{:S(2)}) copy-start(s32[4,64]{1,0:T(4,128)} %param.4) | copy-start | bytes 3076
  3.7 33.9 %all-to-all-start = ((bf16[256,8,128]{2,1,0:T(8,128)(2,1)}), bf16[256,8,128]{2,1,0:T(8,128)(2,1)S(1)}, u32[]{:S(2)}, u32[]{:S(2)}) async-start(bf16[256,8,128]{2,1,0:T(8,128)(2,1)} %reshape.85), calls=%async_computation | async-start | bytes 1048576 | tf_op jit(solution)/shard_map/all_to_all | solution.py:66
  39.7 57.8 %all-to-all-start.1 = ((bf16[64,4,32,128]{3,2,1,0:T(8,128)(2,1)}), bf16[64,4,32,128]{3,2,1,0:T(8,128)(2,1)S(1)}, u32[]{:S(2)}, u32[]{:S(2)}) async-start(bf16[64,4,32,128]{3,2,1,0:T(8,128)(2,1)} %bitcast.36), calls=%async_computation.1 | async-start | bytes 4194304 | tf_op jit(solution)/shard_map/all_to_all | solution.py:69
  49.6 7.3 %collective-permute-start.2 = (bf16[8,32,256]{2,1,0:T(8,128)(2,1)S(1)}, bf16[8,32,256]{2,1,0:T(8,128)(2,1)S(1)}, u32[]{:S(2)}, u32[]{:S(2)}) collective-permute-start(bf16[8,32,256]{2,1,0:T(8,128)(2,1)S(1)} %get-tuple-element.8), channel_id=1, source_target_pairs={{0,3},{1,0},{2,1},{3,2},{4,7},{5,4},{6,5},{7,6},{8,11},{9,8},{10,9... | collective-permute-start | bytes 393224 | tf_op jit(solution)/shard_map/ppermute | solution.py:75
  49.7 14.4 %collective-permute-start.1 = (bf16[8,32,256]{2,1,0:T(8,128)(2,1)S(1)}, bf16[8,32,256]{2,1,0:T(8,128)(2,1)S(1)}, u32[]{:S(2)}, u32[]{:S(2)}) collective-permute-start(bf16[8,32,256]{2,1,0:T(8,128)(2,1)S(1)} %get-tuple-element.9), channel_id=1, source_target_pairs={{0,2},{1,3},{2,0},{3,1},{4,6},{5,7},{6,4},{7,5},{8,10},{9,11},{10,... | collective-permute-start | bytes 393224 | tf_op jit(solution)/shard_map/ppermute | solution.py:75
  50.4 13.7 %collective-permute-start = (bf16[8,32,256]{2,1,0:T(8,128)(2,1)S(1)}, bf16[8,32,256]{2,1,0:T(8,128)(2,1)S(1)}, u32[]{:S(2)}, u32[]{:S(2)}) collective-permute-start(bf16[8,32,256]{2,1,0:T(8,128)(2,1)S(1)} %get-tuple-element.10), channel_id=1, source_target_pairs={{0,1},{1,2},{2,3},{3,0},{4,5},{5,6},{6,7},{7,4},{8,9},{9,10},{10,1... | collective-permute-start | bytes 393224 | tf_op jit(solution)/shard_map/ppermute | solution.py:75
  70.0 2.2 %copy-start.1 = (bf16[1,4,8,8,4,2,128]{6,5,4,3,2,1,0:T(2,128)(2,1)S(1)}, bf16[1,4,8,8,4,2,128]{6,5,4,3,2,1,0:T(2,128)(2,1)}, u32[]{:S(2)}) copy-start(bf16[1,4,8,8,4,2,128]{6,5,4,3,2,1,0:T(2,128)(2,1)} %gather.12) | copy-start | bytes 1572868

commit v13 on v8

--- a/solution.py
+++ b/solution.py
@@ -48,6 +48,33 @@
     )(lhs, pltpu.with_memory_space_constraint(arrived, pltpu.VMEM))
 
 
+def pick_kernel(plan_ref, held_ref, out_ref):
+    step_dests, rounds = out_ref.shape[0], out_ref.shape[1]
+    first = pl.program_id(0) * step_dests
+    for d in range(step_dests):
+        for r in range(rounds):
+            out_ref[d, r] = held_ref[plan_ref[r, first + d]]
+
+
+def pick_partners(plan, held):
+    rounds, dests = plan.shape
+    _, rows, width = held.shape
+    step_dests = 16
+    return pl.pallas_call(
+        pick_kernel,
+        grid_spec=pltpu.PrefetchScalarGridSpec(
+            num_scalar_prefetch=1,
+            grid=(dests // step_dests,),
+            in_specs=[pl.BlockSpec(memory_space=pltpu.VMEM)],
+            out_specs=pl.BlockSpec((step_dests, rounds, rows, width), lambda g, plan_ref: (g, 0, 0, 0)),
+        ),
+        out_shape=jax.ShapeDtypeStruct((dests, rounds, rows, width), held.dtype),
+        cost_estimate=pl.CostEstimate(
+            flops=0, bytes_accessed=held.size * 2 + dests * rounds * rows * width * 4, transcendentals=0
+        ),
+    )(plan, pltpu.with_memory_space_constraint(held, pltpu.VMEM))
+
+
 def on_device(spectra, plan, assignment):
     bin_count, win_local, _, chan_width = spectra.shape
     seg_count = lax.axis_size("seg")
@@ -67,7 +94,7 @@
     send = rows.transpose(1, 2, 0, 3, 4).reshape(group_count * seg_count, win_piece, 2 * chan_width)
     held = lax.all_to_all(send, ("chan", "seg"), split_axis=0, concat_axis=0, tiled=True)
     held = held.reshape(group_count, seg_count * win_piece, 2 * chan_width)
-    outgoing = held.at[plan.T].get(mode="promise_in_bounds")
+    outgoing = pick_partners(plan, held)
     arrived = lax.all_to_all(outgoing, "chan", split_axis=0, concat_axis=0, tiled=True)
     ranges = ordered.reshape(seg_count, my_bins, win_local, 2 * chan_width)
     by_shift = [lax.dynamic_index_in_dim(ranges, seg_index, 0, keepdims=False)]

time: 102 us -> 101 us (level)
  blocking collectives: 0 us -> 33.7 us
  waiting for transfers between devices: 55.8 us -> 36.8 us
  starting transfers between devices: 22.7 us -> 8.06 us
  local copies, waits for them, and re-layouts: 15.8 us -> 12.7 us
  Pallas kernels: 3.77 us -> 6.42 us
    all_to_all x0 -> x1, blocking collectives: none -> 33.7 us  [on_device(): lax.all_to_all(send, ('chan', 'seg'), split_axis=0, concat_axis=0, tiled=...]
    all_to_all x1 -> x0, waiting for transfers between devices: 18.9 us -> none  [on_device(): lax.all_to_all(send, ('chan', 'seg'), split_axis=0, concat_axis=0, tiled=...]
    all_to_all x1 -> x0, starting transfers between devices: 14.7 us -> none  [on_device(): lax.all_to_all(send, ('chan', 'seg'), split_axis=0, concat_axis=0, tiled=...]
    pallas_call x0 -> x1, Pallas kernels: none -> 2.65 us  [pick_partners(): pl.pallas_call(pick_kernel, grid_spec=pltpu.PrefetchScalarGridSpec(num_sc...]
    gather x1 -> x0, local copies, waits for them, and re-layouts: 2.07 us -> none  [on_device(): outgoing = held.at[plan.T].get(mode='promise_in_bounds')]
  transfers between devices with their start and end apart: 5 -> 4, of which waited for: 4 -> 3; matrix products, arithmetic and copies ran while one was open for 13% -> 13% of each run, Pallas kernels for 0% -> 0%
where the time goes in v13:
time: 101 us
  waiting for transfers between devices  36.8 us (36%)
  blocking collectives  33.7 us (33%)
  local copies, waits for them, and re-layouts  12.7 us (13%)
  starting transfers between devices  8.06 us (8%)
  Pallas kernels  6.42 us (6%)
  other arithmetic  2.57 us (3%)
    all_to_all x1, blocking collectives, on_device(): lax.all_to_all(send, ('chan', 'seg'), split_axis=0, concat_axis=0, tiled=...  33.7 us
    all_to_all x1, waiting for transfers between devices, on_device(): lax.all_to_all(outgoing, 'chan', split_axis=0, concat_axis=0, tiled=True)  23.3 us
    ppermute x3, waiting for transfers between devices, on_device(): by_shift.append(lax.ppermute(part, 'seg', pairs))  13.5 us
    all_to_all x1, starting transfers between devices, on_device(): lax.all_to_all(outgoing, 'chan', split_axis=0, concat_axis=0, tiled=True)  7.05 us
    pallas_call x1, Pallas kernels, cross_spectra(): pl.pallas_call(functools.partial(cross_kernel, scale), grid=(bins // step...  3.77 us
    another operation x1, local copies, waits for them, and re-layouts, on_device(): jnp.stack([own, imag_rows], axis=1)  2.85 us
    pallas_call x1, Pallas kernels, pick_partners(): pl.pallas_call(pick_kernel, grid_spec=pltpu.PrefetchScalarGridSpec(num_sc...  2.65 us
    gather x2, local copies, waits for them, and re-layouts, on_device(): own = jnp.take(by_shift, order, axis=0)  2.53 us
  transfers between devices with their start and end apart: 4, of which 3 were waited for; matrix products, arithmetic and copies ran while one was open for 13% of the time, Pallas kernels for 0%

profile of v13, /device:TPU:2, one launch (start us, length us, event | category | flops | bytes accessed | tf_op | source)
XLA Modules:
  0.0 100.7 jit_solution(13135591028054487576)
XLA Ops:
  0.0 0.0 copy-start
  0.0 0.7 broadcast_subtract_fusion
  0.7 0.3 copy-done
  1.1 0.3 fusion
  1.4 0.5 copy.16
  1.9 0.3 reshape.78
  2.3 0.4 copy.17
  2.7 33.7 %all_to_all.10 = bf16[256,4,256]{2,1,0:T(4,128)(2,1)S(1)} all-to-all(bf16[256,4,256]{2,1,0:T(4,128)(2,1)S(1)} %bitcast.33), channel_id=1, replica_groups=mesh['chan'=64,'seg'=4] {'chan','seg'}, dimensions={0} | all-to-all | bytes 1048576 | tf_op jit(solution)/shard_map/all_to_all | solution.py:95
  36.3 0.1 reshape.80.held_ref
  36.5 2.6 %shard_map.37 = bf16[64,4,16,256]{3,2,1,0:T(8,128)(2,1)} custom-call(s32[4,64]{1,0:T(4,128)} %plan_ref.1, bf16[64,16,256]{2,1,0:T(8,128)(2,1)S(1)} %reshape.80.held_ref), custom_call_target="tpu_custom_call" | custom-call | bytes 4718592 | tf_op jit(solution)/shard_map/pallas_call | solution.py:63
  39.1 7.1 %all-to-all-start.1 = ((bf16[64,4,16,256]{3,2,1,0:T(8,128)(2,1)}), bf16[64,4,16,256]{3,2,1,0:T(8,128)(2,1)S(1)}, u32[]{:S(2)}, u32[]{:S(2)}) async-start(bf16[64,4,16,256]{3,2,1,0:T(8,128)(2,1)} %shard_map.37), calls=%async_computation.1 | async-start | bytes 4194304 | tf_op jit(solution)/shard_map/all_to_all | solution.py:98
  46.2 1.3 %copy.12 = bf16[32,32,2,128]{3,2,1,0:T(2,128)(2,1)} copy(bf16[32,32,2,128]{3,1,2,0:T(8,128)(2,1)S(1)} %fusion) | data formatting | bytes 1048576 | tf_op jit(solution)/shard_map/convert_element_type | solution.py:90
  47.5 1.4 %reshape.75 = bf16[4,8,32,256]{3,2,1,0:T(8,128)(2,1)S(1)} reshape(bf16[32,32,2,128]{3,2,1,0:T(2,128)(2,1)} %copy.12) | data formatting | bytes 1048576 | tf_op jit(solution)/shard_map/reshape | solution.py:99
  49.0 0.1 collective-permute-start.2
  49.1 0.8 collective-permute-start.1
  49.8 0.1 collective-permute-start
  50.0 6.3 %collective-permute-done.2 = bf16[8,32,256]{2,1,0:T(8,128)(2,1)S(1)} collective-permute-done((bf16[8,32,256]{2,1,0:T(8,128)(2,1)S(1)}, bf16[8,32,256]{2,1,0:T(8,128)(2,1)S(1)}, u32[]{:S(2)}, u32[]{:S(2)}) %collective-permute-start.2) | collective-permute-done | bytes 131104 | tf_op jit(solution)/shard_map/ppermute | solution.py:104
  56.3 7.2 %collective-permute-done.1 = bf16[8,32,256]{2,1,0:T(8,128)(2,1)S(1)} collective-permute-done((bf16[8,32,256]{2,1,0:T(8,128)(2,1)S(1)}, bf16[8,32,256]{2,1,0:T(8,128)(2,1)S(1)}, u32[]{:S(2)}, u32[]{:S(2)}) %collective-permute-start.1) | collective-permute-done | bytes 131104 | tf_op jit(solution)/shard_map/ppermute | solution.py:104
  63.5 0.0 collective-permute-done
  63.5 0.1 pad_maximum_fusion.1
  63.6 1.4 %gather_fusion = bf16[4,8,32,256]{3,2,1,0:T(8,128)(2,1)} fusion(bf16[4,8,32,256]{3,2,1,0:T(8,128)(2,1)S(1)} %pad_maximum_fusion.1, s32[1024]{0:T(1024)S(1)} %pad_clamp_fusion), kind=kCustom, calls=%fused_computation | custom fusion | bytes 1048592 | tf_op jit(solution)/shard_map/jit(_take)/gather | solution.py:107
  65.0 1.2 %gather.7 = bf16[4,8,8,4,2,128]{5,4,3,2,1,0:T(2,128)(2,1)S(1)} reshape(bf16[4,8,32,256]{3,2,1,0:T(8,128)(2,1)} %gather_fusion) | data formatting | bytes 1048576 | tf_op jit(solution)/shard_map/jit(_take)/gather | solution.py:107
  66.1 0.5 fusion.2
  66.7 0.3 copy.13
  67.0 0.1 fusion.9
  67.1 0.1 maximum_bitcast_fusion
  67.1 1.1 %pad_maximum_fusion = bf16[8,2,128,2,128]{2,0,4,3,1:T(8,128)(2,1)} fusion(bf16[8,1,128,2,128]{2,0,4,3,1:T(8,128)(2,1)S(1)} %maximum_bitcast_fusion, bf16[8,1,128,2,128]{2,0,4,3,1:T(8,128)(2,1)S(1)} %bitcast.31), kind=kLoop, calls=%fused_computation.3 | loop fusion | flops 524288 | bytes 2097152 | tf_op jit(solution)/shard_map/stack | solution.py:111
  68.3 2.8 %copy.15 = bf16[8,2,128,2,128]{4,3,2,1,0:T(2,128)(2,1)} copy(bf16[8,2,128,2,128]{2,0,4,3,1:T(8,128)(2,1)} %pad_maximum_fusion) | data formatting | bytes 2097152 | tf_op jit(solution)/shard_map/stack | solution.py:111
  71.1 2.5 %reshape.77.lhs_ref = bf16[8,256,256]{2,1,0:T(8,128)(2,1)} reshape(bf16[8,2,128,2,128]{4,3,2,1,0:T(2,128)(2,1)} %copy.15) | data formatting | bytes 2097152 | tf_op jit(solution)/shard_map/reshape | solution.py:111
  73.6 23.3 %all-to-all-done.1.rhs_ref = bf16[64,4,16,256]{3,2,1,0:T(8,128)(2,1)S(1)} async-done(((bf16[64,4,16,256]{3,2,1,0:T(8,128)(2,1)}), bf16[64,4,16,256]{3,2,1,0:T(8,128)(2,1)S(1)}, u32[]{:S(2)}, u32[]{:S(2)}) %all-to-all-start.1) | async-done | bytes 2097184 | tf_op jit(solution)/shard_map/all_to_all | solution.py:98
  96.9 3.8 %shard_map.38 = f32[4,8,2,128,128]{4,3,2,1,0:T(8,128)} custom-call(bf16[8,256,256]{2,1,0:T(8,128)(2,1)} %reshape.77.lhs_ref, bf16[64,4,16,256]{3,2,1,0:T(8,128)(2,1)S(1)} %all-to-all-done.1.rhs_ref), custom_call_target="tpu_custom_call" | custom-call | flops 536870912 | bytes 7340032 | tf_op jit(solution)/shard_map/pallas_call | solution.py:34
  (4 shorter events, 0.1 us)
Async XLA Ops:
  0.0 1.1 %copy-start = (bf16[32,32,2,128]{3,2,1,0:T(2,128)(2,1)S(1)}, bf16[32,32,2,128]{3,2,1,0:T(2,128)(2,1)}, u32[]{:S(2)}) copy-start(bf16[32,32,2,128]{3,2,1,0:T(2,128)(2,1)} %param.3) | copy-start | bytes 1572868
  39.1 57.8 %all-to-all-start.1 = ((bf16[64,4,16,256]{3,2,1,0:T(8,128)(2,1)}), bf16[64,4,16,256]{3,2,1,0:T(8,128)(2,1)S(1)}, u32[]{:S(2)}, u32[]{:S(2)}) async-start(bf16[64,4,16,256]{3,2,1,0:T(8,128)(2,1)} %shard_map.37), calls=%async_computation.1 | async-start | bytes 4194304 | tf_op jit(solution)/shard_map/all_to_all | solution.py:98
  49.0 7.3 %collective-permute-start.2 = (bf16[8,32,256]{2,1,0:T(8,128)(2,1)S(1)}, bf16[8,32,256]{2,1,0:T(8,128)(2,1)S(1)}, u32[]{:S(2)}, u32[]{:S(2)}) collective-permute-start(bf16[8,32,256]{2,1,0:T(8,128)(2,1)S(1)} %get-tuple-element.8), channel_id=1, source_target_pairs={{0,3},{1,0},{2,1},{3,2},{4,7},{5,4},{6,5},{7,6},{8,11},{9,8},{10,9... | collective-permute-start | bytes 393224 | tf_op jit(solution)/shard_map/ppermute | solution.py:104
  49.1 14.4 %collective-permute-start.1 = (bf16[8,32,256]{2,1,0:T(8,128)(2,1)S(1)}, bf16[8,32,256]{2,1,0:T(8,128)(2,1)S(1)}, u32[]{:S(2)}, u32[]{:S(2)}) collective-permute-start(bf16[8,32,256]{2,1,0:T(8,128)(2,1)S(1)} %get-tuple-element.9), channel_id=1, source_target_pairs={{0,2},{1,3},{2,0},{3,1},{4,6},{5,7},{6,4},{7,5},{8,10},{9,11},{10,... | collective-permute-start | bytes 393224 | tf_op jit(solution)/shard_map/ppermute | solution.py:104
  49.8 13.7 %collective-permute-start = (bf16[8,32,256]{2,1,0:T(8,128)(2,1)S(1)}, bf16[8,32,256]{2,1,0:T(8,128)(2,1)S(1)}, u32[]{:S(2)}, u32[]{:S(2)}) collective-permute-start(bf16[8,32,256]{2,1,0:T(8,128)(2,1)S(1)} %get-tuple-element.10), channel_id=1, source_target_pairs={{0,1},{1,2},{2,3},{3,0},{4,5},{5,6},{6,7},{7,4},{8,9},{9,10},{10,1... | collective-permute-start | bytes 393224 | tf_op jit(solution)/shard_map/ppermute | solution.py:104

commit v14 on v13

--- a/solution.py
+++ b/solution.py
@@ -49,25 +49,19 @@
 
 
 def pick_kernel(plan_ref, held_ref, out_ref):
-    step_dests, rounds = out_ref.shape[0], out_ref.shape[1]
-    first = pl.program_id(0) * step_dests
-    for d in range(step_dests):
+    dests, rounds = out_ref.shape[0], out_ref.shape[1]
+    for d in range(dests):
         for r in range(rounds):
-            out_ref[d, r] = held_ref[plan_ref[r, first + d]]
+            out_ref[d, r] = held_ref[plan_ref[r, d]]
 
 
 def pick_partners(plan, held):
     rounds, dests = plan.shape
     _, rows, width = held.shape
-    step_dests = 16
     return pl.pallas_call(
         pick_kernel,
-        grid_spec=pltpu.PrefetchScalarGridSpec(
-            num_scalar_prefetch=1,
-            grid=(dests // step_dests,),
-            in_specs=[pl.BlockSpec(memory_space=pltpu.VMEM)],
-            out_specs=pl.BlockSpec((step_dests, rounds, rows, width), lambda g, plan_ref: (g, 0, 0, 0)),
-        ),
+        in_specs=[pl.BlockSpec(memory_space=pltpu.SMEM), pl.BlockSpec(memory_space=pltpu.VMEM)],
+        out_specs=pl.BlockSpec(memory_space=pltpu.VMEM),
         out_shape=jax.ShapeDtypeStruct((dests, rounds, rows, width), held.dtype),
         cost_estimate=pl.CostEstimate(
             flops=0, bytes_accessed=held.size * 2 + dests * rounds * rows * width * 4, transcendentals=0

time: 101 us -> 101 us (level)
  no operation moved by 1% of the time
where the time goes in v14:
time: 101 us; the launch traced here: 100 us
  waiting for transfers between devices  36.8 us (36%)
  blocking collectives  33.7 us (33%)
  local copies, waits for them, and re-layouts  12.7 us (13%)
  starting transfers between devices  8.06 us (8%)
  Pallas kernels  5.98 us (6%)
  other arithmetic  2.57 us (3%)
    all_to_all x1, blocking collectives, on_device(): lax.all_to_all(send, ('chan', 'seg'), split_axis=0, concat_axis=0, tiled=...  33.7 us
    all_to_all x1, waiting for transfers between devices, on_device(): lax.all_to_all(outgoing, 'chan', split_axis=0, concat_axis=0, tiled=True)  23.3 us
    ppermute x3, waiting for transfers between devices, on_device(): by_shift.append(lax.ppermute(part, 'seg', pairs))  13.5 us
    all_to_all x1, starting transfers between devices, on_device(): lax.all_to_all(outgoing, 'chan', split_axis=0, concat_axis=0, tiled=True)  7.05 us
    pallas_call x1, Pallas kernels, cross_spectra(): pl.pallas_call(functools.partial(cross_kernel, scale), grid=(bins // step...  3.76 us
    another operation x1, local copies, waits for them, and re-layouts, on_device(): jnp.stack([own, imag_rows], axis=1)  2.85 us
    gather x2, local copies, waits for them, and re-layouts, on_device(): own = jnp.take(by_shift, order, axis=0)  2.53 us
    reshape x1, local copies, waits for them, and re-layouts, on_device(): jnp.stack([own, imag_rows], axis=1)  2.51 us
  transfers between devices with their start and end apart: 4, of which 3 were waited for; matrix products, arithmetic and copies ran while one was open for 13% of the time, Pallas kernels for 0%

profile of v14, /device:TPU:2, one launch (start us, length us, event | category | flops | bytes accessed | tf_op | source)
XLA Modules:
  0.0 100.3 jit_solution(545900232667940834)
XLA Ops:
  0.0 0.0 copy-start
  0.0 0.7 broadcast_subtract_fusion
  0.7 0.3 copy-done
  1.1 0.3 fusion
  1.4 0.5 copy.16
  1.9 0.3 reshape.78
  2.3 0.4 copy.17
  2.7 33.7 %all_to_all.10 = bf16[256,4,256]{2,1,0:T(4,128)(2,1)S(1)} all-to-all(bf16[256,4,256]{2,1,0:T(4,128)(2,1)S(1)} %bitcast.33), channel_id=1, replica_groups=mesh['chan'=64,'seg'=4] {'chan','seg'}, dimensions={0} | all-to-all | bytes 1048576 | tf_op jit(solution)/shard_map/all_to_all | solution.py:89
  36.3 0.1 reshape.80.held_ref
  36.5 2.2 %shard_map.37 = bf16[64,4,16,256]{3,2,1,0:T(8,128)(2,1)} custom-call(s32[4,64]{1,0:T(4,128)} %plan_ref.1, bf16[64,16,256]{2,1,0:T(8,128)(2,1)S(1)} %reshape.80.held_ref), custom_call_target="tpu_custom_call" | custom-call | bytes 4718592 | tf_op jit(solution)/shard_map/pallas_call | solution.py:61
  38.7 7.1 %all-to-all-start.1 = ((bf16[64,4,16,256]{3,2,1,0:T(8,128)(2,1)}), bf16[64,4,16,256]{3,2,1,0:T(8,128)(2,1)S(1)}, u32[]{:S(2)}, u32[]{:S(2)}) async-start(bf16[64,4,16,256]{3,2,1,0:T(8,128)(2,1)} %shard_map.37), calls=%async_computation.1 | async-start | bytes 4194304 | tf_op jit(solution)/shard_map/all_to_all | solution.py:92
  45.8 1.3 %copy.12 = bf16[32,32,2,128]{3,2,1,0:T(2,128)(2,1)} copy(bf16[32,32,2,128]{3,1,2,0:T(8,128)(2,1)S(1)} %fusion) | data formatting | bytes 1048576 | tf_op jit(solution)/shard_map/convert_element_type | solution.py:84
  47.1 1.4 %reshape.75 = bf16[4,8,32,256]{3,2,1,0:T(8,128)(2,1)S(1)} reshape(bf16[32,32,2,128]{3,2,1,0:T(2,128)(2,1)} %copy.12) | data formatting | bytes 1048576 | tf_op jit(solution)/shard_map/reshape | solution.py:93
  48.5 0.1 collective-permute-start.2
  48.6 0.8 collective-permute-start.1
  49.4 0.1 collective-permute-start
  49.6 6.3 %collective-permute-done.2 = bf16[8,32,256]{2,1,0:T(8,128)(2,1)S(1)} collective-permute-done((bf16[8,32,256]{2,1,0:T(8,128)(2,1)S(1)}, bf16[8,32,256]{2,1,0:T(8,128)(2,1)S(1)}, u32[]{:S(2)}, u32[]{:S(2)}) %collective-permute-start.2) | collective-permute-done | bytes 131104 | tf_op jit(solution)/shard_map/ppermute | solution.py:98
  55.9 7.2 %collective-permute-done.1 = bf16[8,32,256]{2,1,0:T(8,128)(2,1)S(1)} collective-permute-done((bf16[8,32,256]{2,1,0:T(8,128)(2,1)S(1)}, bf16[8,32,256]{2,1,0:T(8,128)(2,1)S(1)}, u32[]{:S(2)}, u32[]{:S(2)}) %collective-permute-start.1) | collective-permute-done | bytes 131104 | tf_op jit(solution)/shard_map/ppermute | solution.py:98
  63.1 0.0 collective-permute-done
  63.1 0.1 pad_maximum_fusion.1
  63.2 1.4 %gather_fusion = bf16[4,8,32,256]{3,2,1,0:T(8,128)(2,1)} fusion(bf16[4,8,32,256]{3,2,1,0:T(8,128)(2,1)S(1)} %pad_maximum_fusion.1, s32[1024]{0:T(1024)S(1)} %pad_clamp_fusion), kind=kCustom, calls=%fused_computation | custom fusion | bytes 1048592 | tf_op jit(solution)/shard_map/jit(_take)/gather | solution.py:101
  64.5 1.2 %gather.7 = bf16[4,8,8,4,2,128]{5,4,3,2,1,0:T(2,128)(2,1)S(1)} reshape(bf16[4,8,32,256]{3,2,1,0:T(8,128)(2,1)} %gather_fusion) | data formatting | bytes 1048576 | tf_op jit(solution)/shard_map/jit(_take)/gather | solution.py:101
  65.7 0.5 fusion.2
  66.2 0.3 copy.13
  66.6 0.1 fusion.9
  66.6 0.1 maximum_bitcast_fusion
  66.7 1.1 %pad_maximum_fusion = bf16[8,2,128,2,128]{2,0,4,3,1:T(8,128)(2,1)} fusion(bf16[8,1,128,2,128]{2,0,4,3,1:T(8,128)(2,1)S(1)} %maximum_bitcast_fusion, bf16[8,1,128,2,128]{2,0,4,3,1:T(8,128)(2,1)S(1)} %bitcast.31), kind=kLoop, calls=%fused_computation.3 | loop fusion | flops 524288 | bytes 2097152 | tf_op jit(solution)/shard_map/stack | solution.py:105
  67.8 2.8 %copy.15 = bf16[8,2,128,2,128]{4,3,2,1,0:T(2,128)(2,1)} copy(bf16[8,2,128,2,128]{2,0,4,3,1:T(8,128)(2,1)} %pad_maximum_fusion) | data formatting | bytes 2097152 | tf_op jit(solution)/shard_map/stack | solution.py:105
  70.7 2.5 %reshape.77.lhs_ref = bf16[8,256,256]{2,1,0:T(8,128)(2,1)} reshape(bf16[8,2,128,2,128]{4,3,2,1,0:T(2,128)(2,1)} %copy.15) | data formatting | bytes 2097152 | tf_op jit(solution)/shard_map/reshape | solution.py:105
  73.2 23.3 %all-to-all-done.1.rhs_ref = bf16[64,4,16,256]{3,2,1,0:T(8,128)(2,1)S(1)} async-done(((bf16[64,4,16,256]{3,2,1,0:T(8,128)(2,1)}), bf16[64,4,16,256]{3,2,1,0:T(8,128)(2,1)S(1)}, u32[]{:S(2)}, u32[]{:S(2)}) %all-to-all-start.1) | async-done | bytes 2097184 | tf_op jit(solution)/shard_map/all_to_all | solution.py:92
  96.5 3.8 %shard_map.38 = f32[4,8,2,128,128]{4,3,2,1,0:T(8,128)} custom-call(bf16[8,256,256]{2,1,0:T(8,128)(2,1)} %reshape.77.lhs_ref, bf16[64,4,16,256]{3,2,1,0:T(8,128)(2,1)S(1)} %all-to-all-done.1.rhs_ref), custom_call_target="tpu_custom_call" | custom-call | flops 536870912 | bytes 7340032 | tf_op jit(solution)/shard_map/pallas_call | solution.py:34
  (4 shorter events, 0.1 us)
Async XLA Ops:
  0.0 1.1 %copy-start = (bf16[32,32,2,128]{3,2,1,0:T(2,128)(2,1)S(1)}, bf16[32,32,2,128]{3,2,1,0:T(2,128)(2,1)}, u32[]{:S(2)}) copy-start(bf16[32,32,2,128]{3,2,1,0:T(2,128)(2,1)} %param.3) | copy-start | bytes 1572868
  38.7 57.8 %all-to-all-start.1 = ((bf16[64,4,16,256]{3,2,1,0:T(8,128)(2,1)}), bf16[64,4,16,256]{3,2,1,0:T(8,128)(2,1)S(1)}, u32[]{:S(2)}, u32[]{:S(2)}) async-start(bf16[64,4,16,256]{3,2,1,0:T(8,128)(2,1)} %shard_map.37), calls=%async_computation.1 | async-start | bytes 4194304 | tf_op jit(solution)/shard_map/all_to_all | solution.py:92
  48.5 7.3 %collective-permute-start.2 = (bf16[8,32,256]{2,1,0:T(8,128)(2,1)S(1)}, bf16[8,32,256]{2,1,0:T(8,128)(2,1)S(1)}, u32[]{:S(2)}, u32[]{:S(2)}) collective-permute-start(bf16[8,32,256]{2,1,0:T(8,128)(2,1)S(1)} %get-tuple-element.8), channel_id=1, source_target_pairs={{0,3},{1,0},{2,1},{3,2},{4,7},{5,4},{6,5},{7,6},{8,11},{9,8},{10,9... | collective-permute-start | bytes 393224 | tf_op jit(solution)/shard_map/ppermute | solution.py:98
  48.6 14.4 %collective-permute-start.1 = (bf16[8,32,256]{2,1,0:T(8,128)(2,1)S(1)}, bf16[8,32,256]{2,1,0:T(8,128)(2,1)S(1)}, u32[]{:S(2)}, u32[]{:S(2)}) collective-permute-start(bf16[8,32,256]{2,1,0:T(8,128)(2,1)S(1)} %get-tuple-element.9), channel_id=1, source_target_pairs={{0,2},{1,3},{2,0},{3,1},{4,6},{5,7},{6,4},{7,5},{8,10},{9,11},{10,... | collective-permute-start | bytes 393224 | tf_op jit(solution)/shard_map/ppermute | solution.py:98
  49.4 13.7 %collective-permute-start = (bf16[8,32,256]{2,1,0:T(8,128)(2,1)S(1)}, bf16[8,32,256]{2,1,0:T(8,128)(2,1)S(1)}, u32[]{:S(2)}, u32[]{:S(2)}) collective-permute-start(bf16[8,32,256]{2,1,0:T(8,128)(2,1)S(1)} %get-tuple-element.10), channel_id=1, source_target_pairs={{0,1},{1,2},{2,3},{3,0},{4,5},{5,6},{6,7},{7,4},{8,9},{9,10},{10,1... | collective-permute-start | bytes 393224 | tf_op jit(solution)/shard_map/ppermute | solution.py:98

commit v15 on v14

--- a/solution.py
+++ b/solution.py
@@ -48,11 +48,16 @@
     )(lhs, pltpu.with_memory_space_constraint(arrived, pltpu.VMEM))
 
 
-def pick_kernel(plan_ref, held_ref, out_ref):
-    dests, rounds = out_ref.shape[0], out_ref.shape[1]
+def pick_kernel(plan_ref, held_ref, out_hbm, sems):
+    dests, rounds = out_hbm.shape[0], out_hbm.shape[1]
+    copies = []
     for d in range(dests):
         for r in range(rounds):
-            out_ref[d, r] = held_ref[plan_ref[r, d]]
+            copy = pltpu.make_async_copy(held_ref.at[plan_ref[r, d]], out_hbm.at[d, r], sems.at[r, d])
+            copy.start()
+            copies.append(copy)
+    for copy in copies:
+        copy.wait()
 
 
 def pick_partners(plan, held):
@@ -61,8 +66,9 @@
     return pl.pallas_call(
         pick_kernel,
         in_specs=[pl.BlockSpec(memory_space=pltpu.SMEM), pl.BlockSpec(memory_space=pltpu.VMEM)],
-        out_specs=pl.BlockSpec(memory_space=pltpu.VMEM),
+        out_specs=pl.BlockSpec(memory_space=pl.ANY),
         out_shape=jax.ShapeDtypeStruct((dests, rounds, rows, width), held.dtype),
+        scratch_shapes=[pltpu.SemaphoreType.DMA((rounds, dests))],
         cost_estimate=pl.CostEstimate(
             flops=0, bytes_accessed=held.size * 2 + dests * rounds * rows * width * 4, transcendentals=0
         ),

time: 101 us -> 103 us (1.020)
  Pallas kernels: 5.98 us -> 8.29 us
    pallas_call x1, Pallas kernels: 2.21 us -> 4.52 us  [pick_partners(): pl.pallas_call(pick_kernel, in_specs=[pl.BlockSpec(memory_space=pltpu.SME...]
  transfers between devices with their start and end apart: 4 -> 4, of which waited for: 3 -> 3; matrix products, arithmetic and copies ran while one was open for 13% -> 12% of each run, Pallas kernels for 0% -> 0%
where the time goes in v15:
time: 103 us
  waiting for transfers between devices  36.8 us (36%)
  blocking collectives  33.7 us (33%)
  local copies, waits for them, and re-layouts  12.7 us (12%)
  Pallas kernels  8.29 us (8%)
  starting transfers between devices  8.07 us (8%)
  other arithmetic  2.57 us (2%)
    all_to_all x1, blocking collectives, on_device(): lax.all_to_all(send, ('chan', 'seg'), split_axis=0, concat_axis=0, tiled=...  33.7 us
    all_to_all x1, waiting for transfers between devices, on_device(): lax.all_to_all(outgoing, 'chan', split_axis=0, concat_axis=0, tiled=True)  23.3 us
    ppermute x3, waiting for transfers between devices, on_device(): by_shift.append(lax.ppermute(part, 'seg', pairs))  13.5 us
    all_to_all x1, starting transfers between devices, on_device(): lax.all_to_all(outgoing, 'chan', split_axis=0, concat_axis=0, tiled=True)  7.06 us
    pallas_call x1, Pallas kernels, pick_partners(): pl.pallas_call(pick_kernel, in_specs=[pl.BlockSpec(memory_space=pltpu.SME...  4.52 us
    pallas_call x1, Pallas kernels, cross_spectra(): pl.pallas_call(functools.partial(cross_kernel, scale), grid=(bins // step...  3.76 us
    another operation x1, local copies, waits for them, and re-layouts, on_device(): jnp.stack([own, imag_rows], axis=1)  2.85 us
    gather x2, local copies, waits for them, and re-layouts, on_device(): own = jnp.take(by_shift, order, axis=0)  2.53 us
  transfers between devices with their start and end apart: 4, of which 3 were waited for; matrix products, arithmetic and copies ran while one was open for 12% of the time, Pallas kernels for 0%

profile of v15, /device:TPU:2, one launch (start us, length us, event | category | flops | bytes accessed | tf_op | source)
XLA Modules:
  0.0 102.6 jit_solution(16519718074761125579)
XLA Ops:
  0.0 0.0 copy-start
  0.0 0.7 broadcast_subtract_fusion
  0.7 0.3 copy-done
  1.1 0.3 fusion
  1.4 0.5 copy.16
  1.9 0.3 reshape.78
  2.3 0.4 copy.17
  2.7 33.7 %all_to_all.10 = bf16[256,4,256]{2,1,0:T(4,128)(2,1)S(1)} all-to-all(bf16[256,4,256]{2,1,0:T(4,128)(2,1)S(1)} %bitcast.33), channel_id=1, replica_groups=mesh['chan'=64,'seg'=4] {'chan','seg'}, dimensions={0} | all-to-all | bytes 1048576 | tf_op jit(solution)/shard_map/all_to_all | solution.py:95
  36.3 0.1 reshape.80.held_ref
  36.5 4.5 %shard_map.37 = bf16[64,4,16,256]{3,2,1,0:T(8,128)(2,1)} custom-call(s32[4,64]{1,0:T(4,128)} %plan_ref.1, bf16[64,16,256]{2,1,0:T(8,128)(2,1)S(1)} %reshape.80.held_ref), custom_call_target="tpu_custom_call" | custom-call | bytes 4718592 | tf_op jit(solution)/shard_map/pallas_call | solution.py:66
  41.0 7.1 %all-to-all-start.1 = ((bf16[64,4,16,256]{3,2,1,0:T(8,128)(2,1)}), bf16[64,4,16,256]{3,2,1,0:T(8,128)(2,1)S(1)}, u32[]{:S(2)}, u32[]{:S(2)}) async-start(bf16[64,4,16,256]{3,2,1,0:T(8,128)(2,1)} %shard_map.37), calls=%async_computation.1 | async-start | bytes 4194304 | tf_op jit(solution)/shard_map/all_to_all | solution.py:98
  48.1 1.3 %copy.12 = bf16[32,32,2,128]{3,2,1,0:T(2,128)(2,1)} copy(bf16[32,32,2,128]{3,1,2,0:T(8,128)(2,1)S(1)} %fusion) | data formatting | bytes 1048576 | tf_op jit(solution)/shard_map/convert_element_type | solution.py:90
  49.4 1.4 %reshape.75 = bf16[4,8,32,256]{3,2,1,0:T(8,128)(2,1)S(1)} reshape(bf16[32,32,2,128]{3,2,1,0:T(2,128)(2,1)} %copy.12) | data formatting | bytes 1048576 | tf_op jit(solution)/shard_map/reshape | solution.py:99
  50.9 0.1 collective-permute-start.2
  51.0 0.8 collective-permute-start.1
  51.7 0.1 collective-permute-start
  51.9 6.3 %collective-permute-done.2 = bf16[8,32,256]{2,1,0:T(8,128)(2,1)S(1)} collective-permute-done((bf16[8,32,256]{2,1,0:T(8,128)(2,1)S(1)}, bf16[8,32,256]{2,1,0:T(8,128)(2,1)S(1)}, u32[]{:S(2)}, u32[]{:S(2)}) %collective-permute-start.2) | collective-permute-done | bytes 131104 | tf_op jit(solution)/shard_map/ppermute | solution.py:104
  58.2 7.2 %collective-permute-done.1 = bf16[8,32,256]{2,1,0:T(8,128)(2,1)S(1)} collective-permute-done((bf16[8,32,256]{2,1,0:T(8,128)(2,1)S(1)}, bf16[8,32,256]{2,1,0:T(8,128)(2,1)S(1)}, u32[]{:S(2)}, u32[]{:S(2)}) %collective-permute-start.1) | collective-permute-done | bytes 131104 | tf_op jit(solution)/shard_map/ppermute | solution.py:104
  65.4 0.0 collective-permute-done
  65.4 0.1 pad_maximum_fusion.1
  65.5 1.4 %gather_fusion = bf16[4,8,32,256]{3,2,1,0:T(8,128)(2,1)} fusion(bf16[4,8,32,256]{3,2,1,0:T(8,128)(2,1)S(1)} %pad_maximum_fusion.1, s32[1024]{0:T(1024)S(1)} %pad_clamp_fusion), kind=kCustom, calls=%fused_computation | custom fusion | bytes 1048592 | tf_op jit(solution)/shard_map/jit(_take)/gather | solution.py:107
  66.9 1.2 %gather.7 = bf16[4,8,8,4,2,128]{5,4,3,2,1,0:T(2,128)(2,1)S(1)} reshape(bf16[4,8,32,256]{3,2,1,0:T(8,128)(2,1)} %gather_fusion) | data formatting | bytes 1048576 | tf_op jit(solution)/shard_map/jit(_take)/gather | solution.py:107
  68.0 0.5 fusion.2
  68.6 0.3 copy.13
  68.9 0.1 fusion.9
  69.0 0.1 maximum_bitcast_fusion
  69.0 1.1 %pad_maximum_fusion = bf16[8,2,128,2,128]{2,0,4,3,1:T(8,128)(2,1)} fusion(bf16[8,1,128,2,128]{2,0,4,3,1:T(8,128)(2,1)S(1)} %maximum_bitcast_fusion, bf16[8,1,128,2,128]{2,0,4,3,1:T(8,128)(2,1)S(1)} %bitcast.31), kind=kLoop, calls=%fused_computation.3 | loop fusion | flops 524288 | bytes 2097152 | tf_op jit(solution)/shard_map/stack | solution.py:111
  70.2 2.8 %copy.15 = bf16[8,2,128,2,128]{4,3,2,1,0:T(2,128)(2,1)} copy(bf16[8,2,128,2,128]{2,0,4,3,1:T(8,128)(2,1)} %pad_maximum_fusion) | data formatting | bytes 2097152 | tf_op jit(solution)/shard_map/stack | solution.py:111
  73.0 2.5 %reshape.77.lhs_ref = bf16[8,256,256]{2,1,0:T(8,128)(2,1)} reshape(bf16[8,2,128,2,128]{4,3,2,1,0:T(2,128)(2,1)} %copy.15) | data formatting | bytes 2097152 | tf_op jit(solution)/shard_map/reshape | solution.py:111
  75.5 23.3 %all-to-all-done.1.rhs_ref = bf16[64,4,16,256]{3,2,1,0:T(8,128)(2,1)S(1)} async-done(((bf16[64,4,16,256]{3,2,1,0:T(8,128)(2,1)}), bf16[64,4,16,256]{3,2,1,0:T(8,128)(2,1)S(1)}, u32[]{:S(2)}, u32[]{:S(2)}) %all-to-all-start.1) | async-done | bytes 2097184 | tf_op jit(solution)/shard_map/all_to_all | solution.py:98
  98.8 3.8 %shard_map.38 = f32[4,8,2,128,128]{4,3,2,1,0:T(8,128)} custom-call(bf16[8,256,256]{2,1,0:T(8,128)(2,1)} %reshape.77.lhs_ref, bf16[64,4,16,256]{3,2,1,0:T(8,128)(2,1)S(1)} %all-to-all-done.1.rhs_ref), custom_call_target="tpu_custom_call" | custom-call | flops 536870912 | bytes 7340032 | tf_op jit(solution)/shard_map/pallas_call | solution.py:34
  (4 shorter events, 0.1 us)
Async XLA Ops:
  0.0 1.1 %copy-start = (bf16[32,32,2,128]{3,2,1,0:T(2,128)(2,1)S(1)}, bf16[32,32,2,128]{3,2,1,0:T(2,128)(2,1)}, u32[]{:S(2)}) copy-start(bf16[32,32,2,128]{3,2,1,0:T(2,128)(2,1)} %param.3) | copy-start | bytes 1572868
  41.0 57.8 %all-to-all-start.1 = ((bf16[64,4,16,256]{3,2,1,0:T(8,128)(2,1)}), bf16[64,4,16,256]{3,2,1,0:T(8,128)(2,1)S(1)}, u32[]{:S(2)}, u32[]{:S(2)}) async-start(bf16[64,4,16,256]{3,2,1,0:T(8,128)(2,1)} %shard_map.37), calls=%async_computation.1 | async-start | bytes 4194304 | tf_op jit(solution)/shard_map/all_to_all | solution.py:98
  50.9 7.3 %collective-permute-start.2 = (bf16[8,32,256]{2,1,0:T(8,128)(2,1)S(1)}, bf16[8,32,256]{2,1,0:T(8,128)(2,1)S(1)}, u32[]{:S(2)}, u32[]{:S(2)}) collective-permute-start(bf16[8,32,256]{2,1,0:T(8,128)(2,1)S(1)} %get-tuple-element.8), channel_id=1, source_target_pairs={{0,3},{1,0},{2,1},{3,2},{4,7},{5,4},{6,5},{7,6},{8,11},{9,8},{10,9... | collective-permute-start | bytes 393224 | tf_op jit(solution)/shard_map/ppermute | solution.py:104
  51.0 14.4 %collective-permute-start.1 = (bf16[8,32,256]{2,1,0:T(8,128)(2,1)S(1)}, bf16[8,32,256]{2,1,0:T(8,128)(2,1)S(1)}, u32[]{:S(2)}, u32[]{:S(2)}) collective-permute-start(bf16[8,32,256]{2,1,0:T(8,128)(2,1)S(1)} %get-tuple-element.9), channel_id=1, source_target_pairs={{0,2},{1,3},{2,0},{3,1},{4,6},{5,7},{6,4},{7,5},{8,10},{9,11},{10,... | collective-permute-start | bytes 393224 | tf_op jit(solution)/shard_map/ppermute | solution.py:104
  51.7 13.7 %collective-permute-start = (bf16[8,32,256]{2,1,0:T(8,128)(2,1)S(1)}, bf16[8,32,256]{2,1,0:T(8,128)(2,1)S(1)}, u32[]{:S(2)}, u32[]{:S(2)}) collective-permute-start(bf16[8,32,256]{2,1,0:T(8,128)(2,1)S(1)} %get-tuple-element.10), channel_id=1, source_target_pairs={{0,1},{1,2},{2,3},{3,0},{4,5},{5,6},{6,7},{7,4},{8,9},{9,10},{10,1... | collective-permute-start | bytes 393224 | tf_op jit(solution)/shard_map/ppermute | solution.py:104

commit v16 on v14

--- a/solution.py
+++ b/solution.py
@@ -17,12 +17,16 @@
     first = pl.program_id(0) * step_bins
     for b in range(step_bins):
         lhs = lhs_ref[b]
-        for r in range(rounds):
-            block = rhs_ref[pl.ds((first + b) * per_bin, per_bin), r]
-            block = block.reshape(per_bin * rows, two_chan)
-            block = jnp.concatenate([block[:, :chan], block[:, chan:]], axis=0)
-            acc = jnp.dot(lhs, block, preferred_element_type=jnp.float32)
-            out_ref[r, b] = (acc * scale).reshape(2, chan, chan)
+        for r0 in range(0, rounds, 2):
+            columns = []
+            for r in (r0, r0 + 1):
+                block = rhs_ref[pl.ds((first + b) * per_bin, per_bin), r]
+                block = block.reshape(per_bin * rows, two_chan)
+                columns.append(jnp.concatenate([block[:, :chan], block[:, chan:]], axis=0))
+            acc = jnp.dot(lhs, jnp.concatenate(columns, axis=1), preferred_element_type=jnp.float32)
+            acc = acc * scale
+            out_ref[r0, b] = acc[:, :chan].reshape(2, chan, chan)
+            out_ref[r0 + 1, b] = acc[:, chan:].reshape(2, chan, chan)
 
 
 def cross_spectra(lhs, arrived, scale):

time: 101 us -> 100 us (0.990)
  no operation moved by 1% of the time
where the time goes in v16:
time: 100 us
  waiting for transfers between devices  36.8 us (37%)
  blocking collectives  33.7 us (34%)
  local copies, waits for them, and re-layouts  12.7 us (13%)
  starting transfers between devices  8.06 us (8%)
  Pallas kernels  5.71 us (6%)
  other arithmetic  2.57 us (3%)
    all_to_all x1, blocking collectives, on_device(): lax.all_to_all(send, ('chan', 'seg'), split_axis=0, concat_axis=0, tiled=...  33.7 us
    all_to_all x1, waiting for transfers between devices, on_device(): lax.all_to_all(outgoing, 'chan', split_axis=0, concat_axis=0, tiled=True)  23.3 us
    ppermute x3, waiting for transfers between devices, on_device(): by_shift.append(lax.ppermute(part, 'seg', pairs))  13.5 us
    all_to_all x1, starting transfers between devices, on_device(): lax.all_to_all(outgoing, 'chan', split_axis=0, concat_axis=0, tiled=True)  7.05 us
    pallas_call x1, Pallas kernels, cross_spectra(): pl.pallas_call(functools.partial(cross_kernel, scale), grid=(bins // step...  3.49 us
    another operation x1, local copies, waits for them, and re-layouts, on_device(): jnp.stack([own, imag_rows], axis=1)  2.85 us
    gather x2, local copies, waits for them, and re-layouts, on_device(): own = jnp.take(by_shift, order, axis=0)  2.53 us
    reshape x1, local copies, waits for them, and re-layouts, on_device(): jnp.stack([own, imag_rows], axis=1)  2.51 us
  transfers between devices with their start and end apart: 4, of which 3 were waited for; matrix products, arithmetic and copies ran while one was open for 13% of the time, Pallas kernels for 0%

profile of v16, /device:TPU:2, one launch (start us, length us, event | category | flops | bytes accessed | tf_op | source)
XLA Modules:
  0.0 100.0 jit_solution(17221231155595368338)
XLA Ops:
  0.0 0.0 copy-start
  0.0 0.7 broadcast_subtract_fusion
  0.7 0.3 copy-done
  1.1 0.3 fusion
  1.4 0.5 copy.16
  1.9 0.3 reshape.78
  2.3 0.4 copy.17
  2.7 33.7 %all_to_all.10 = bf16[256,4,256]{2,1,0:T(4,128)(2,1)S(1)} all-to-all(bf16[256,4,256]{2,1,0:T(4,128)(2,1)S(1)} %bitcast.33), channel_id=1, replica_groups=mesh['chan'=64,'seg'=4] {'chan','seg'}, dimensions={0} | all-to-all | bytes 1048576 | tf_op jit(solution)/shard_map/all_to_all | solution.py:93
  36.3 0.1 reshape.80.held_ref
  36.5 2.2 %shard_map.37 = bf16[64,4,16,256]{3,2,1,0:T(8,128)(2,1)} custom-call(s32[4,64]{1,0:T(4,128)} %plan_ref.1, bf16[64,16,256]{2,1,0:T(8,128)(2,1)S(1)} %reshape.80.held_ref), custom_call_target="tpu_custom_call" | custom-call | bytes 4718592 | tf_op jit(solution)/shard_map/pallas_call | solution.py:65
  38.7 7.1 %all-to-all-start.1 = ((bf16[64,4,16,256]{3,2,1,0:T(8,128)(2,1)}), bf16[64,4,16,256]{3,2,1,0:T(8,128)(2,1)S(1)}, u32[]{:S(2)}, u32[]{:S(2)}) async-start(bf16[64,4,16,256]{3,2,1,0:T(8,128)(2,1)} %shard_map.37), calls=%async_computation.1 | async-start | bytes 4194304 | tf_op jit(solution)/shard_map/all_to_all | solution.py:96
  45.8 1.3 %copy.12 = bf16[32,32,2,128]{3,2,1,0:T(2,128)(2,1)} copy(bf16[32,32,2,128]{3,1,2,0:T(8,128)(2,1)S(1)} %fusion) | data formatting | bytes 1048576 | tf_op jit(solution)/shard_map/convert_element_type | solution.py:88
  47.1 1.4 %reshape.75 = bf16[4,8,32,256]{3,2,1,0:T(8,128)(2,1)S(1)} reshape(bf16[32,32,2,128]{3,2,1,0:T(2,128)(2,1)} %copy.12) | data formatting | bytes 1048576 | tf_op jit(solution)/shard_map/reshape | solution.py:97
  48.5 0.1 collective-permute-start.2
  48.6 0.8 collective-permute-start.1
  49.4 0.1 collective-permute-start
  49.6 6.3 %collective-permute-done.2 = bf16[8,32,256]{2,1,0:T(8,128)(2,1)S(1)} collective-permute-done((bf16[8,32,256]{2,1,0:T(8,128)(2,1)S(1)}, bf16[8,32,256]{2,1,0:T(8,128)(2,1)S(1)}, u32[]{:S(2)}, u32[]{:S(2)}) %collective-permute-start.2) | collective-permute-done | bytes 131104 | tf_op jit(solution)/shard_map/ppermute | solution.py:102
  55.9 7.2 %collective-permute-done.1 = bf16[8,32,256]{2,1,0:T(8,128)(2,1)S(1)} collective-permute-done((bf16[8,32,256]{2,1,0:T(8,128)(2,1)S(1)}, bf16[8,32,256]{2,1,0:T(8,128)(2,1)S(1)}, u32[]{:S(2)}, u32[]{:S(2)}) %collective-permute-start.1) | collective-permute-done | bytes 131104 | tf_op jit(solution)/shard_map/ppermute | solution.py:102
  63.1 0.0 collective-permute-done
  63.1 0.1 pad_maximum_fusion.1
  63.2 1.4 %gather_fusion = bf16[4,8,32,256]{3,2,1,0:T(8,128)(2,1)} fusion(bf16[4,8,32,256]{3,2,1,0:T(8,128)(2,1)S(1)} %pad_maximum_fusion.1, s32[1024]{0:T(1024)S(1)} %pad_clamp_fusion), kind=kCustom, calls=%fused_computation | custom fusion | bytes 1048592 | tf_op jit(solution)/shard_map/jit(_take)/gather | solution.py:105
  64.5 1.2 %gather.7 = bf16[4,8,8,4,2,128]{5,4,3,2,1,0:T(2,128)(2,1)S(1)} reshape(bf16[4,8,32,256]{3,2,1,0:T(8,128)(2,1)} %gather_fusion) | data formatting | bytes 1048576 | tf_op jit(solution)/shard_map/jit(_take)/gather | solution.py:105
  65.7 0.5 fusion.2
  66.2 0.3 copy.13
  66.6 0.1 fusion.9
  66.6 0.1 maximum_bitcast_fusion
  66.7 1.1 %pad_maximum_fusion = bf16[8,2,128,2,128]{2,0,4,3,1:T(8,128)(2,1)} fusion(bf16[8,1,128,2,128]{2,0,4,3,1:T(8,128)(2,1)S(1)} %maximum_bitcast_fusion, bf16[8,1,128,2,128]{2,0,4,3,1:T(8,128)(2,1)S(1)} %bitcast.31), kind=kLoop, calls=%fused_computation.3 | loop fusion | flops 524288 | bytes 2097152 | tf_op jit(solution)/shard_map/stack | solution.py:109
  67.8 2.8 %copy.15 = bf16[8,2,128,2,128]{4,3,2,1,0:T(2,128)(2,1)} copy(bf16[8,2,128,2,128]{2,0,4,3,1:T(8,128)(2,1)} %pad_maximum_fusion) | data formatting | bytes 2097152 | tf_op jit(solution)/shard_map/stack | solution.py:109
  70.7 2.5 %reshape.77.lhs_ref = bf16[8,256,256]{2,1,0:T(8,128)(2,1)} reshape(bf16[8,2,128,2,128]{4,3,2,1,0:T(2,128)(2,1)} %copy.15) | data formatting | bytes 2097152 | tf_op jit(solution)/shard_map/reshape | solution.py:109
  73.2 23.3 %all-to-all-done.1.rhs_ref = bf16[64,4,16,256]{3,2,1,0:T(8,128)(2,1)S(1)} async-done(((bf16[64,4,16,256]{3,2,1,0:T(8,128)(2,1)}), bf16[64,4,16,256]{3,2,1,0:T(8,128)(2,1)S(1)}, u32[]{:S(2)}, u32[]{:S(2)}) %all-to-all-start.1) | async-done | bytes 2097184 | tf_op jit(solution)/shard_map/all_to_all | solution.py:96
  96.5 3.5 %shard_map.38 = f32[4,8,2,128,128]{4,3,2,1,0:T(8,128)} custom-call(bf16[8,256,256]{2,1,0:T(8,128)(2,1)} %reshape.77.lhs_ref, bf16[64,4,16,256]{3,2,1,0:T(8,128)(2,1)S(1)} %all-to-all-done.1.rhs_ref), custom_call_target="tpu_custom_call" | custom-call | flops 536870912 | bytes 7340032 | tf_op jit(solution)/shard_map/pallas_call | solution.py:38
  (4 shorter events, 0.1 us)
Async XLA Ops:
  0.0 1.1 %copy-start = (bf16[32,32,2,128]{3,2,1,0:T(2,128)(2,1)S(1)}, bf16[32,32,2,128]{3,2,1,0:T(2,128)(2,1)}, u32[]{:S(2)}) copy-start(bf16[32,32,2,128]{3,2,1,0:T(2,128)(2,1)} %param.3) | copy-start | bytes 1572868
  38.7 57.8 %all-to-all-start.1 = ((bf16[64,4,16,256]{3,2,1,0:T(8,128)(2,1)}), bf16[64,4,16,256]{3,2,1,0:T(8,128)(2,1)S(1)}, u32[]{:S(2)}, u32[]{:S(2)}) async-start(bf16[64,4,16,256]{3,2,1,0:T(8,128)(2,1)} %shard_map.37), calls=%async_computation.1 | async-start | bytes 4194304 | tf_op jit(solution)/shard_map/all_to_all | solution.py:96
  48.5 7.3 %collective-permute-start.2 = (bf16[8,32,256]{2,1,0:T(8,128)(2,1)S(1)}, bf16[8,32,256]{2,1,0:T(8,128)(2,1)S(1)}, u32[]{:S(2)}, u32[]{:S(2)}) collective-permute-start(bf16[8,32,256]{2,1,0:T(8,128)(2,1)S(1)} %get-tuple-element.8), channel_id=1, source_target_pairs={{0,3},{1,0},{2,1},{3,2},{4,7},{5,4},{6,5},{7,6},{8,11},{9,8},{10,9... | collective-permute-start | bytes 393224 | tf_op jit(solution)/shard_map/ppermute | solution.py:102
  48.6 14.4 %collective-permute-start.1 = (bf16[8,32,256]{2,1,0:T(8,128)(2,1)S(1)}, bf16[8,32,256]{2,1,0:T(8,128)(2,1)S(1)}, u32[]{:S(2)}, u32[]{:S(2)}) collective-permute-start(bf16[8,32,256]{2,1,0:T(8,128)(2,1)S(1)} %get-tuple-element.9), channel_id=1, source_target_pairs={{0,2},{1,3},{2,0},{3,1},{4,6},{5,7},{6,4},{7,5},{8,10},{9,11},{10,... | collective-permute-start | bytes 393224 | tf_op jit(solution)/shard_map/ppermute | solution.py:102
  49.4 13.7 %collective-permute-start = (bf16[8,32,256]{2,1,0:T(8,128)(2,1)S(1)}, bf16[8,32,256]{2,1,0:T(8,128)(2,1)S(1)}, u32[]{:S(2)}, u32[]{:S(2)}) collective-permute-start(bf16[8,32,256]{2,1,0:T(8,128)(2,1)S(1)} %get-tuple-element.10), channel_id=1, source_target_pairs={{0,1},{1,2},{2,3},{3,0},{4,5},{5,6},{6,7},{7,4},{8,9},{9,10},{10,1... | collective-permute-start | bytes 393224 | tf_op jit(solution)/shard_map/ppermute | solution.py:102

commit v17 on v16

--- a/solution.py
+++ b/solution.py
@@ -52,21 +52,33 @@
     )(lhs, pltpu.with_memory_space_constraint(arrived, pltpu.VMEM))
 
 
-def pick_kernel(plan_ref, held_ref, out_ref):
-    dests, rounds = out_ref.shape[0], out_ref.shape[1]
-    for d in range(dests):
-        for r in range(rounds):
-            out_ref[d, r] = held_ref[plan_ref[r, d]]
+def pick_kernel(plan_ref, held_ref, out_hbm, staged, sems):
+    groups, per_group, rounds = staged.shape[0], staged.shape[1], staged.shape[2]
+    copies = []
+    for g in range(groups):
+        for d in range(per_group):
+            for r in range(rounds):
+                staged[g, d, r] = held_ref[plan_ref[r, g * per_group + d]]
+        copy = pltpu.make_async_copy(staged.at[g], out_hbm.at[pl.ds(g * per_group, per_group)], sems.at[g])
+        copy.start()
+        copies.append(copy)
+    for copy in copies:
+        copy.wait()
 
 
 def pick_partners(plan, held):
     rounds, dests = plan.shape
     _, rows, width = held.shape
+    groups = 4
     return pl.pallas_call(
         pick_kernel,
         in_specs=[pl.BlockSpec(memory_space=pltpu.SMEM), pl.BlockSpec(memory_space=pltpu.VMEM)],
-        out_specs=pl.BlockSpec(memory_space=pltpu.VMEM),
+        out_specs=pl.BlockSpec(memory_space=pl.ANY),
         out_shape=jax.ShapeDtypeStruct((dests, rounds, rows, width), held.dtype),
+        scratch_shapes=[
+            pltpu.VMEM((groups, dests // groups, rounds, rows, width), held.dtype),
+            pltpu.SemaphoreType.DMA((groups,)),
+        ],
         cost_estimate=pl.CostEstimate(
             flops=0, bytes_accessed=held.size * 2 + dests * rounds * rows * width * 4, transcendentals=0
         ),

time: 100 us -> 100 us (level)
  no operation moved by 1% of the time
where the time goes in v17:
time: 100 us; the launch traced here: 99.9 us
  waiting for transfers between devices  36.8 us (37%)
  blocking collectives  33.7 us (34%)
  local copies, waits for them, and re-layouts  12.7 us (13%)
  starting transfers between devices  8.07 us (8%)
  Pallas kernels  5.58 us (6%)
  other arithmetic  2.57 us (3%)
    all_to_all x1, blocking collectives, on_device(): lax.all_to_all(send, ('chan', 'seg'), split_axis=0, concat_axis=0, tiled=...  33.7 us
    all_to_all x1, waiting for transfers between devices, on_device(): lax.all_to_all(outgoing, 'chan', split_axis=0, concat_axis=0, tiled=True)  23.3 us
    ppermute x3, waiting for transfers between devices, on_device(): by_shift.append(lax.ppermute(part, 'seg', pairs))  13.5 us
    all_to_all x1, starting transfers between devices, on_device(): lax.all_to_all(outgoing, 'chan', split_axis=0, concat_axis=0, tiled=True)  7.06 us
    pallas_call x1, Pallas kernels, cross_spectra(): pl.pallas_call(functools.partial(cross_kernel, scale), grid=(bins // step...  3.49 us
    another operation x1, local copies, waits for them, and re-layouts, on_device(): jnp.stack([own, imag_rows], axis=1)  2.85 us
    gather x2, local copies, waits for them, and re-layouts, on_device(): own = jnp.take(by_shift, order, axis=0)  2.53 us
    reshape x1, local copies, waits for them, and re-layouts, on_device(): jnp.stack([own, imag_rows], axis=1)  2.51 us
  transfers between devices with their start and end apart: 4, of which 3 were waited for; matrix products, arithmetic and copies ran while one was open for 13% of the time, Pallas kernels for 0%

profile of v17, /device:TPU:2, one launch (start us, length us, event | category | flops | bytes accessed | tf_op | source)
XLA Modules:
  0.0 99.9 jit_solution(2317180383691326229)
XLA Ops:
  0.0 0.0 copy-start
  0.0 0.7 broadcast_subtract_fusion
  0.7 0.3 copy-done
  1.1 0.3 fusion
  1.4 0.5 copy.16
  1.9 0.3 reshape.78
  2.3 0.4 copy.17
  2.7 33.7 %all_to_all.10 = bf16[256,4,256]{2,1,0:T(4,128)(2,1)S(1)} all-to-all(bf16[256,4,256]{2,1,0:T(4,128)(2,1)S(1)} %bitcast.33), channel_id=1, replica_groups=mesh['chan'=64,'seg'=4] {'chan','seg'}, dimensions={0} | all-to-all | bytes 1048576 | tf_op jit(solution)/shard_map/all_to_all | solution.py:105
  36.3 0.1 reshape.80.held_ref
  36.5 2.1 %shard_map.37 = bf16[64,4,16,256]{3,2,1,0:T(8,128)(2,1)} custom-call(s32[4,64]{1,0:T(4,128)} %plan_ref.1, bf16[64,16,256]{2,1,0:T(8,128)(2,1)S(1)} %reshape.80.held_ref), custom_call_target="tpu_custom_call" | custom-call | bytes 4718592 | tf_op jit(solution)/shard_map/pallas_call | solution.py:73
  38.6 7.1 %all-to-all-start.1 = ((bf16[64,4,16,256]{3,2,1,0:T(8,128)(2,1)}), bf16[64,4,16,256]{3,2,1,0:T(8,128)(2,1)S(1)}, u32[]{:S(2)}, u32[]{:S(2)}) async-start(bf16[64,4,16,256]{3,2,1,0:T(8,128)(2,1)} %shard_map.37), calls=%async_computation.1 | async-start | bytes 4194304 | tf_op jit(solution)/shard_map/all_to_all | solution.py:108
  45.7 1.3 %copy.12 = bf16[32,32,2,128]{3,2,1,0:T(2,128)(2,1)} copy(bf16[32,32,2,128]{3,1,2,0:T(8,128)(2,1)S(1)} %fusion) | data formatting | bytes 1048576 | tf_op jit(solution)/shard_map/convert_element_type | solution.py:100
  47.0 1.4 %reshape.75 = bf16[4,8,32,256]{3,2,1,0:T(8,128)(2,1)S(1)} reshape(bf16[32,32,2,128]{3,2,1,0:T(2,128)(2,1)} %copy.12) | data formatting | bytes 1048576 | tf_op jit(solution)/shard_map/reshape | solution.py:109
  48.4 0.1 collective-permute-start.2
  48.5 0.8 collective-permute-start.1
  49.3 0.1 collective-permute-start
  49.5 6.3 %collective-permute-done.2 = bf16[8,32,256]{2,1,0:T(8,128)(2,1)S(1)} collective-permute-done((bf16[8,32,256]{2,1,0:T(8,128)(2,1)S(1)}, bf16[8,32,256]{2,1,0:T(8,128)(2,1)S(1)}, u32[]{:S(2)}, u32[]{:S(2)}) %collective-permute-start.2) | collective-permute-done | bytes 131104 | tf_op jit(solution)/shard_map/ppermute | solution.py:114
  55.8 7.2 %collective-permute-done.1 = bf16[8,32,256]{2,1,0:T(8,128)(2,1)S(1)} collective-permute-done((bf16[8,32,256]{2,1,0:T(8,128)(2,1)S(1)}, bf16[8,32,256]{2,1,0:T(8,128)(2,1)S(1)}, u32[]{:S(2)}, u32[]{:S(2)}) %collective-permute-start.1) | collective-permute-done | bytes 131104 | tf_op jit(solution)/shard_map/ppermute | solution.py:114
  63.0 0.0 collective-permute-done
  63.0 0.1 pad_maximum_fusion.1
  63.1 1.4 %gather_fusion = bf16[4,8,32,256]{3,2,1,0:T(8,128)(2,1)} fusion(bf16[4,8,32,256]{3,2,1,0:T(8,128)(2,1)S(1)} %pad_maximum_fusion.1, s32[1024]{0:T(1024)S(1)} %pad_clamp_fusion), kind=kCustom, calls=%fused_computation | custom fusion | bytes 1048592 | tf_op jit(solution)/shard_map/jit(_take)/gather | solution.py:117
  64.4 1.2 %gather.7 = bf16[4,8,8,4,2,128]{5,4,3,2,1,0:T(2,128)(2,1)S(1)} reshape(bf16[4,8,32,256]{3,2,1,0:T(8,128)(2,1)} %gather_fusion) | data formatting | bytes 1048576 | tf_op jit(solution)/shard_map/jit(_take)/gather | solution.py:117
  65.6 0.5 fusion.2
  66.1 0.3 copy.13
  66.5 0.1 fusion.9
  66.5 0.1 maximum_bitcast_fusion
  66.6 1.1 %pad_maximum_fusion = bf16[8,2,128,2,128]{2,0,4,3,1:T(8,128)(2,1)} fusion(bf16[8,1,128,2,128]{2,0,4,3,1:T(8,128)(2,1)S(1)} %maximum_bitcast_fusion, bf16[8,1,128,2,128]{2,0,4,3,1:T(8,128)(2,1)S(1)} %bitcast.31), kind=kLoop, calls=%fused_computation.3 | loop fusion | flops 524288 | bytes 2097152 | tf_op jit(solution)/shard_map/stack | solution.py:121
  67.7 2.8 %copy.15 = bf16[8,2,128,2,128]{4,3,2,1,0:T(2,128)(2,1)} copy(bf16[8,2,128,2,128]{2,0,4,3,1:T(8,128)(2,1)} %pad_maximum_fusion) | data formatting | bytes 2097152 | tf_op jit(solution)/shard_map/stack | solution.py:121
  70.6 2.5 %reshape.77.lhs_ref = bf16[8,256,256]{2,1,0:T(8,128)(2,1)} reshape(bf16[8,2,128,2,128]{4,3,2,1,0:T(2,128)(2,1)} %copy.15) | data formatting | bytes 2097152 | tf_op jit(solution)/shard_map/reshape | solution.py:121
  73.1 23.3 %all-to-all-done.1.rhs_ref = bf16[64,4,16,256]{3,2,1,0:T(8,128)(2,1)S(1)} async-done(((bf16[64,4,16,256]{3,2,1,0:T(8,128)(2,1)}), bf16[64,4,16,256]{3,2,1,0:T(8,128)(2,1)S(1)}, u32[]{:S(2)}, u32[]{:S(2)}) %all-to-all-start.1) | async-done | bytes 2097184 | tf_op jit(solution)/shard_map/all_to_all | solution.py:108
  96.4 3.5 %shard_map.38 = f32[4,8,2,128,128]{4,3,2,1,0:T(8,128)} custom-call(bf16[8,256,256]{2,1,0:T(8,128)(2,1)} %reshape.77.lhs_ref, bf16[64,4,16,256]{3,2,1,0:T(8,128)(2,1)S(1)} %all-to-all-done.1.rhs_ref), custom_call_target="tpu_custom_call" | custom-call | flops 536870912 | bytes 7340032 | tf_op jit(solution)/shard_map/pallas_call | solution.py:38
  (4 shorter events, 0.1 us)
Async XLA Ops:
  0.0 1.1 %copy-start = (bf16[32,32,2,128]{3,2,1,0:T(2,128)(2,1)S(1)}, bf16[32,32,2,128]{3,2,1,0:T(2,128)(2,1)}, u32[]{:S(2)}) copy-start(bf16[32,32,2,128]{3,2,1,0:T(2,128)(2,1)} %param.3) | copy-start | bytes 1572868
  38.6 57.8 %all-to-all-start.1 = ((bf16[64,4,16,256]{3,2,1,0:T(8,128)(2,1)}), bf16[64,4,16,256]{3,2,1,0:T(8,128)(2,1)S(1)}, u32[]{:S(2)}, u32[]{:S(2)}) async-start(bf16[64,4,16,256]{3,2,1,0:T(8,128)(2,1)} %shard_map.37), calls=%async_computation.1 | async-start | bytes 4194304 | tf_op jit(solution)/shard_map/all_to_all | solution.py:108
  48.4 7.3 %collective-permute-start.2 = (bf16[8,32,256]{2,1,0:T(8,128)(2,1)S(1)}, bf16[8,32,256]{2,1,0:T(8,128)(2,1)S(1)}, u32[]{:S(2)}, u32[]{:S(2)}) collective-permute-start(bf16[8,32,256]{2,1,0:T(8,128)(2,1)S(1)} %get-tuple-element.8), channel_id=1, source_target_pairs={{0,3},{1,0},{2,1},{3,2},{4,7},{5,4},{6,5},{7,6},{8,11},{9,8},{10,9... | collective-permute-start | bytes 393224 | tf_op jit(solution)/shard_map/ppermute | solution.py:114
  48.5 14.4 %collective-permute-start.1 = (bf16[8,32,256]{2,1,0:T(8,128)(2,1)S(1)}, bf16[8,32,256]{2,1,0:T(8,128)(2,1)S(1)}, u32[]{:S(2)}, u32[]{:S(2)}) collective-permute-start(bf16[8,32,256]{2,1,0:T(8,128)(2,1)S(1)} %get-tuple-element.9), channel_id=1, source_target_pairs={{0,2},{1,3},{2,0},{3,1},{4,6},{5,7},{6,4},{7,5},{8,10},{9,11},{10,... | collective-permute-start | bytes 393224 | tf_op jit(solution)/shard_map/ppermute | solution.py:114
  49.3 13.7 %collective-permute-start = (bf16[8,32,256]{2,1,0:T(8,128)(2,1)S(1)}, bf16[8,32,256]{2,1,0:T(8,128)(2,1)S(1)}, u32[]{:S(2)}, u32[]{:S(2)}) collective-permute-start(bf16[8,32,256]{2,1,0:T(8,128)(2,1)S(1)} %get-tuple-element.10), channel_id=1, source_target_pairs={{0,1},{1,2},{2,3},{3,0},{4,5},{5,6},{6,7},{7,4},{8,9},{9,10},{10,1... | collective-permute-start | bytes 393224 | tf_op jit(solution)/shard_map/ppermute | solution.py:114

commit v18 on v17

--- a/solution.py
+++ b/solution.py
@@ -69,7 +69,7 @@
 def pick_partners(plan, held):
     rounds, dests = plan.shape
     _, rows, width = held.shape
-    groups = 4
+    groups = 8
     return pl.pallas_call(
         pick_kernel,
         in_specs=[pl.BlockSpec(memory_space=pltpu.SMEM), pl.BlockSpec(memory_space=pltpu.VMEM)],

time: 100 us -> 100 us (level)
  no operation moved by 1% of the time
where the time goes in v18:
time: 100 us; the launch traced here: 99.9 us
  waiting for transfers between devices  36.8 us (37%)
  blocking collectives  33.7 us (34%)
  local copies, waits for them, and re-layouts  12.7 us (13%)
  starting transfers between devices  8.07 us (8%)
  Pallas kernels  5.59 us (6%)
  other arithmetic  2.57 us (3%)
    all_to_all x1, blocking collectives, on_device(): lax.all_to_all(send, ('chan', 'seg'), split_axis=0, concat_axis=0, tiled=...  33.7 us
    all_to_all x1, waiting for transfers between devices, on_device(): lax.all_to_all(outgoing, 'chan', split_axis=0, concat_axis=0, tiled=True)  23.3 us
    ppermute x3, waiting for transfers between devices, on_device(): by_shift.append(lax.ppermute(part, 'seg', pairs))  13.5 us
    all_to_all x1, starting transfers between devices, on_device(): lax.all_to_all(outgoing, 'chan', split_axis=0, concat_axis=0, tiled=True)  7.06 us
    pallas_call x1, Pallas kernels, cross_spectra(): pl.pallas_call(functools.partial(cross_kernel, scale), grid=(bins // step...  3.49 us
    another operation x1, local copies, waits for them, and re-layouts, on_device(): jnp.stack([own, imag_rows], axis=1)  2.85 us
    gather x2, local copies, waits for them, and re-layouts, on_device(): own = jnp.take(by_shift, order, axis=0)  2.53 us
    reshape x1, local copies, waits for them, and re-layouts, on_device(): jnp.stack([own, imag_rows], axis=1)  2.51 us
  transfers between devices with their start and end apart: 4, of which 3 were waited for; matrix products, arithmetic and copies ran while one was open for 13% of the time, Pallas kernels for 0%

profile of v18, /device:TPU:2, one launch (start us, length us, event | category | flops | bytes accessed | tf_op | source)
XLA Modules:
  0.0 99.9 jit_solution(1240837553848701921)
XLA Ops:
  0.0 0.0 copy-start
  0.0 0.7 broadcast_subtract_fusion
  0.7 0.3 copy-done
  1.1 0.3 fusion
  1.4 0.5 copy.16
  1.9 0.3 reshape.78
  2.3 0.4 copy.17
  2.7 33.7 %all_to_all.10 = bf16[256,4,256]{2,1,0:T(4,128)(2,1)S(1)} all-to-all(bf16[256,4,256]{2,1,0:T(4,128)(2,1)S(1)} %bitcast.33), channel_id=1, replica_groups=mesh['chan'=64,'seg'=4] {'chan','seg'}, dimensions={0} | all-to-all | bytes 1048576 | tf_op jit(solution)/shard_map/all_to_all | solution.py:105
  36.3 0.1 reshape.80.held_ref
  36.5 2.1 %shard_map.37 = bf16[64,4,16,256]{3,2,1,0:T(8,128)(2,1)} custom-call(s32[4,64]{1,0:T(4,128)} %plan_ref.1, bf16[64,16,256]{2,1,0:T(8,128)(2,1)S(1)} %reshape.80.held_ref), custom_call_target="tpu_custom_call" | custom-call | bytes 4718592 | tf_op jit(solution)/shard_map/pallas_call | solution.py:73
  38.6 7.1 %all-to-all-start.1 = ((bf16[64,4,16,256]{3,2,1,0:T(8,128)(2,1)}), bf16[64,4,16,256]{3,2,1,0:T(8,128)(2,1)S(1)}, u32[]{:S(2)}, u32[]{:S(2)}) async-start(bf16[64,4,16,256]{3,2,1,0:T(8,128)(2,1)} %shard_map.37), calls=%async_computation.1 | async-start | bytes 4194304 | tf_op jit(solution)/shard_map/all_to_all | solution.py:108
  45.7 1.3 %copy.12 = bf16[32,32,2,128]{3,2,1,0:T(2,128)(2,1)} copy(bf16[32,32,2,128]{3,1,2,0:T(8,128)(2,1)S(1)} %fusion) | data formatting | bytes 1048576 | tf_op jit(solution)/shard_map/convert_element_type | solution.py:100
  47.0 1.4 %reshape.75 = bf16[4,8,32,256]{3,2,1,0:T(8,128)(2,1)S(1)} reshape(bf16[32,32,2,128]{3,2,1,0:T(2,128)(2,1)} %copy.12) | data formatting | bytes 1048576 | tf_op jit(solution)/shard_map/reshape | solution.py:109
  48.4 0.1 collective-permute-start.2
  48.5 0.8 collective-permute-start.1
  49.3 0.1 collective-permute-start
  49.5 6.3 %collective-permute-done.2 = bf16[8,32,256]{2,1,0:T(8,128)(2,1)S(1)} collective-permute-done((bf16[8,32,256]{2,1,0:T(8,128)(2,1)S(1)}, bf16[8,32,256]{2,1,0:T(8,128)(2,1)S(1)}, u32[]{:S(2)}, u32[]{:S(2)}) %collective-permute-start.2) | collective-permute-done | bytes 131104 | tf_op jit(solution)/shard_map/ppermute | solution.py:114
  55.8 7.2 %collective-permute-done.1 = bf16[8,32,256]{2,1,0:T(8,128)(2,1)S(1)} collective-permute-done((bf16[8,32,256]{2,1,0:T(8,128)(2,1)S(1)}, bf16[8,32,256]{2,1,0:T(8,128)(2,1)S(1)}, u32[]{:S(2)}, u32[]{:S(2)}) %collective-permute-start.1) | collective-permute-done | bytes 131104 | tf_op jit(solution)/shard_map/ppermute | solution.py:114
  63.0 0.0 collective-permute-done
  63.0 0.1 pad_maximum_fusion.1
  63.1 1.4 %gather_fusion = bf16[4,8,32,256]{3,2,1,0:T(8,128)(2,1)} fusion(bf16[4,8,32,256]{3,2,1,0:T(8,128)(2,1)S(1)} %pad_maximum_fusion.1, s32[1024]{0:T(1024)S(1)} %pad_clamp_fusion), kind=kCustom, calls=%fused_computation | custom fusion | bytes 1048592 | tf_op jit(solution)/shard_map/jit(_take)/gather | solution.py:117
  64.4 1.2 %gather.7 = bf16[4,8,8,4,2,128]{5,4,3,2,1,0:T(2,128)(2,1)S(1)} reshape(bf16[4,8,32,256]{3,2,1,0:T(8,128)(2,1)} %gather_fusion) | data formatting | bytes 1048576 | tf_op jit(solution)/shard_map/jit(_take)/gather | solution.py:117
  65.6 0.5 fusion.2
  66.1 0.3 copy.13
  66.5 0.1 fusion.9
  66.5 0.1 maximum_bitcast_fusion
  66.6 1.1 %pad_maximum_fusion = bf16[8,2,128,2,128]{2,0,4,3,1:T(8,128)(2,1)} fusion(bf16[8,1,128,2,128]{2,0,4,3,1:T(8,128)(2,1)S(1)} %maximum_bitcast_fusion, bf16[8,1,128,2,128]{2,0,4,3,1:T(8,128)(2,1)S(1)} %bitcast.31), kind=kLoop, calls=%fused_computation.3 | loop fusion | flops 524288 | bytes 2097152 | tf_op jit(solution)/shard_map/stack | solution.py:121
  67.7 2.8 %copy.15 = bf16[8,2,128,2,128]{4,3,2,1,0:T(2,128)(2,1)} copy(bf16[8,2,128,2,128]{2,0,4,3,1:T(8,128)(2,1)} %pad_maximum_fusion) | data formatting | bytes 2097152 | tf_op jit(solution)/shard_map/stack | solution.py:121
  70.6 2.5 %reshape.77.lhs_ref = bf16[8,256,256]{2,1,0:T(8,128)(2,1)} reshape(bf16[8,2,128,2,128]{4,3,2,1,0:T(2,128)(2,1)} %copy.15) | data formatting | bytes 2097152 | tf_op jit(solution)/shard_map/reshape | solution.py:121
  73.1 23.3 %all-to-all-done.1.rhs_ref = bf16[64,4,16,256]{3,2,1,0:T(8,128)(2,1)S(1)} async-done(((bf16[64,4,16,256]{3,2,1,0:T(8,128)(2,1)}), bf16[64,4,16,256]{3,2,1,0:T(8,128)(2,1)S(1)}, u32[]{:S(2)}, u32[]{:S(2)}) %all-to-all-start.1) | async-done | bytes 2097184 | tf_op jit(solution)/shard_map/all_to_all | solution.py:108
  96.4 3.5 %shard_map.38 = f32[4,8,2,128,128]{4,3,2,1,0:T(8,128)} custom-call(bf16[8,256,256]{2,1,0:T(8,128)(2,1)} %reshape.77.lhs_ref, bf16[64,4,16,256]{3,2,1,0:T(8,128)(2,1)S(1)} %all-to-all-done.1.rhs_ref), custom_call_target="tpu_custom_call" | custom-call | flops 536870912 | bytes 7340032 | tf_op jit(solution)/shard_map/pallas_call | solution.py:38
  (4 shorter events, 0.1 us)
Async XLA Ops:
  0.0 1.1 %copy-start = (bf16[32,32,2,128]{3,2,1,0:T(2,128)(2,1)S(1)}, bf16[32,32,2,128]{3,2,1,0:T(2,128)(2,1)}, u32[]{:S(2)}) copy-start(bf16[32,32,2,128]{3,2,1,0:T(2,128)(2,1)} %param.3) | copy-start | bytes 1572868
  38.6 57.8 %all-to-all-start.1 = ((bf16[64,4,16,256]{3,2,1,0:T(8,128)(2,1)}), bf16[64,4,16,256]{3,2,1,0:T(8,128)(2,1)S(1)}, u32[]{:S(2)}, u32[]{:S(2)}) async-start(bf16[64,4,16,256]{3,2,1,0:T(8,128)(2,1)} %shard_map.37), calls=%async_computation.1 | async-start | bytes 4194304 | tf_op jit(solution)/shard_map/all_to_all | solution.py:108
  48.4 7.3 %collective-permute-start.2 = (bf16[8,32,256]{2,1,0:T(8,128)(2,1)S(1)}, bf16[8,32,256]{2,1,0:T(8,128)(2,1)S(1)}, u32[]{:S(2)}, u32[]{:S(2)}) collective-permute-start(bf16[8,32,256]{2,1,0:T(8,128)(2,1)S(1)} %get-tuple-element.8), channel_id=1, source_target_pairs={{0,3},{1,0},{2,1},{3,2},{4,7},{5,4},{6,5},{7,6},{8,11},{9,8},{10,9... | collective-permute-start | bytes 393224 | tf_op jit(solution)/shard_map/ppermute | solution.py:114
  48.5 14.4 %collective-permute-start.1 = (bf16[8,32,256]{2,1,0:T(8,128)(2,1)S(1)}, bf16[8,32,256]{2,1,0:T(8,128)(2,1)S(1)}, u32[]{:S(2)}, u32[]{:S(2)}) collective-permute-start(bf16[8,32,256]{2,1,0:T(8,128)(2,1)S(1)} %get-tuple-element.9), channel_id=1, source_target_pairs={{0,2},{1,3},{2,0},{3,1},{4,6},{5,7},{6,4},{7,5},{8,10},{9,11},{10,... | collective-permute-start | bytes 393224 | tf_op jit(solution)/shard_map/ppermute | solution.py:114
  49.3 13.7 %collective-permute-start = (bf16[8,32,256]{2,1,0:T(8,128)(2,1)S(1)}, bf16[8,32,256]{2,1,0:T(8,128)(2,1)S(1)}, u32[]{:S(2)}, u32[]{:S(2)}) collective-permute-start(bf16[8,32,256]{2,1,0:T(8,128)(2,1)S(1)} %get-tuple-element.10), channel_id=1, source_target_pairs={{0,1},{1,2},{2,3},{3,0},{4,5},{5,6},{6,7},{7,4},{8,9},{9,10},{10,1... | collective-permute-start | bytes 393224 | tf_op jit(solution)/shard_map/ppermute | solution.py:114

commit v19 on v17

--- a/solution.py
+++ b/solution.py
@@ -16,7 +16,10 @@
     chan = two_chan // 2
     first = pl.program_id(0) * step_bins
     for b in range(step_bins):
-        lhs = lhs_ref[b]
+        real_rows = lhs_ref[b]
+        half = real_rows.shape[1] // 2
+        imag_rows = jnp.concatenate([real_rows[:, half:], -real_rows[:, :half]], axis=1)
+        lhs = jnp.concatenate([real_rows, imag_rows], axis=0)
         for r0 in range(0, rounds, 2):
             columns = []
             for r in (r0, r0 + 1):
@@ -30,8 +33,8 @@
 
 
 def cross_spectra(lhs, arrived, scale):
-    bins, two_chan, two_win = lhs.shape
-    chan = two_chan // 2
+    bins, chan, two_win = lhs.shape
+    two_chan = 2 * chan
     pieces, rounds, rows, _ = arrived.shape
     per_bin = pieces // bins
     step_bins = 4
@@ -39,7 +42,7 @@
         functools.partial(cross_kernel, scale),
         grid=(bins // step_bins,),
         in_specs=[
-            pl.BlockSpec((step_bins, two_chan, two_win), lambda g: (g, 0, 0)),
+            pl.BlockSpec((step_bins, chan, two_win), lambda g: (g, 0, 0)),
             pl.BlockSpec(memory_space=pltpu.VMEM),
         ],
         out_specs=pl.BlockSpec((rounds, step_bins, 2, chan, chan), lambda g: (0, g, 0, 0, 0)),
@@ -117,9 +120,7 @@
     own = jnp.take(by_shift, order, axis=0)
     own = own.reshape(seg_count, my_bins, per_bin, win_piece, 2, chan_width)
     own = own.transpose(1, 5, 4, 2, 0, 3).reshape(my_bins, chan_width, 2, win_count)
-    imag_rows = jnp.stack([own[:, :, 1], -own[:, :, 0]], axis=2)
-    lhs = jnp.stack([own, imag_rows], axis=1).reshape(my_bins, 2 * chan_width, 2 * win_count)
-    return cross_spectra(lhs, arrived, scale)
+    return cross_spectra(own.reshape(my_bins, chan_width, 2 * win_count), arrived, scale)
 
 
 def solution(mesh):

time: 100 us -> 100 us (level)
  waiting for transfers between devices: 36.8 us -> 42.3 us
  local copies, waits for them, and re-layouts: 12.7 us -> 8.5 us
  other arithmetic: 2.57 us -> 1.34 us
    all_to_all x1, waiting for transfers between devices: 23.3 us -> 28.8 us  [on_device(): lax.all_to_all(outgoing, 'chan', split_axis=0, concat_axis=0, tiled=True)]
    reshape x1 -> x0, local copies, waits for them, and re-layouts: 2.51 us -> none  [on_device(): jnp.stack([own, imag_rows], axis=1)]
    another operation x1, local copies, waits for them, and re-layouts: 2.85 us -> 1.13 us  [on_device(): own.reshape(my_bins, chan_width, 2 * win_count)]
    another operation x2 -> x0, other arithmetic: 1.18 us -> none  [on_device(): jnp.stack([own, imag_rows], axis=1)]
  transfers between devices with their start and end apart: 4 -> 4, of which waited for: 3 -> 3; matrix products, arithmetic and copies ran while one was open for 13% -> 7% of each run, Pallas kernels for 0% -> 0%
where the time goes in v19:
time: 100 us; the launch traced here: 99.8 us
  waiting for transfers between devices  42.3 us (42%)
  blocking collectives  33.7 us (34%)
  local copies, waits for them, and re-layouts  8.5 us (8%)
  starting transfers between devices  8.07 us (8%)
  Pallas kernels  5.49 us (5%)
  other arithmetic  1.34 us (1%)
    all_to_all x1, blocking collectives, on_device(): lax.all_to_all(send, ('chan', 'seg'), split_axis=0, concat_axis=0, tiled=...  33.7 us
    all_to_all x1, waiting for transfers between devices, on_device(): lax.all_to_all(outgoing, 'chan', split_axis=0, concat_axis=0, tiled=True)  28.8 us
    ppermute x3, waiting for transfers between devices, on_device(): by_shift.append(lax.ppermute(part, 'seg', pairs))  13.5 us
    all_to_all x1, starting transfers between devices, on_device(): lax.all_to_all(outgoing, 'chan', split_axis=0, concat_axis=0, tiled=True)  7.06 us
    pallas_call x1, Pallas kernels, cross_spectra(): pl.pallas_call(functools.partial(cross_kernel, scale), grid=(bins // step...  3.4 us
    gather x2, local copies, waits for them, and re-layouts, on_device(): own = jnp.take(by_shift, order, axis=0)  2.54 us
    pallas_call x1, Pallas kernels, pick_partners(): pl.pallas_call(pick_kernel, in_specs=[pl.BlockSpec(memory_space=pltpu.SME...  2.09 us
  transfers between devices with their start and end apart: 4, of which 3 were waited for; matrix products, arithmetic and copies ran while one was open for 7% of the time, Pallas kernels for 0%

profile of v19, /device:TPU:2, one launch (start us, length us, event | category | flops | bytes accessed | tf_op | source)
XLA Modules:
  0.0 99.8 jit_solution(15291976914147564784)
XLA Ops:
  0.0 0.0 copy-start
  0.0 0.7 broadcast_subtract_fusion
  0.7 0.3 copy-done
  1.1 0.3 fusion
  1.4 0.5 copy.13
  1.9 0.3 reshape.70
  2.3 0.4 copy.14
  2.7 33.7 %all_to_all.10 = bf16[256,4,256]{2,1,0:T(4,128)(2,1)S(1)} all-to-all(bf16[256,4,256]{2,1,0:T(4,128)(2,1)S(1)} %bitcast.28), channel_id=1, replica_groups=mesh['chan'=64,'seg'=4] {'chan','seg'}, dimensions={0} | all-to-all | bytes 1048576 | tf_op jit(solution)/shard_map/all_to_all | solution.py:108
  36.3 0.1 reshape.72.held_ref
  36.5 2.1 %shard_map.37 = bf16[64,4,16,256]{3,2,1,0:T(8,128)(2,1)} custom-call(s32[4,64]{1,0:T(4,128)} %plan_ref.1, bf16[64,16,256]{2,1,0:T(8,128)(2,1)S(1)} %reshape.72.held_ref), custom_call_target="tpu_custom_call" | custom-call | bytes 4718592 | tf_op jit(solution)/shard_map/pallas_call | solution.py:76
  38.6 7.1 %all-to-all-start.1 = ((bf16[64,4,16,256]{3,2,1,0:T(8,128)(2,1)}), bf16[64,4,16,256]{3,2,1,0:T(8,128)(2,1)S(1)}, u32[]{:S(2)}, u32[]{:S(2)}) async-start(bf16[64,4,16,256]{3,2,1,0:T(8,128)(2,1)} %shard_map.37), calls=%async_computation.1 | async-start | bytes 4194304 | tf_op jit(solution)/shard_map/all_to_all | solution.py:111
  45.7 1.3 %copy.11 = bf16[32,32,2,128]{3,2,1,0:T(2,128)(2,1)} copy(bf16[32,32,2,128]{3,1,2,0:T(8,128)(2,1)S(1)} %fusion) | data formatting | bytes 1048576 | tf_op jit(solution)/shard_map/convert_element_type | solution.py:103
  47.0 1.4 %reshape.69 = bf16[4,8,32,256]{3,2,1,0:T(8,128)(2,1)S(1)} reshape(bf16[32,32,2,128]{3,2,1,0:T(2,128)(2,1)} %copy.11) | data formatting | bytes 1048576 | tf_op jit(solution)/shard_map/reshape | solution.py:112
  48.4 0.1 collective-permute-start.2
  48.5 0.8 collective-permute-start.1
  49.3 0.1 collective-permute-start
  49.5 6.3 %collective-permute-done.2 = bf16[8,32,256]{2,1,0:T(8,128)(2,1)S(1)} collective-permute-done((bf16[8,32,256]{2,1,0:T(8,128)(2,1)S(1)}, bf16[8,32,256]{2,1,0:T(8,128)(2,1)S(1)}, u32[]{:S(2)}, u32[]{:S(2)}) %collective-permute-start.2) | collective-permute-done | bytes 131104 | tf_op jit(solution)/shard_map/ppermute | solution.py:117
  55.8 7.2 %collective-permute-done.1 = bf16[8,32,256]{2,1,0:T(8,128)(2,1)S(1)} collective-permute-done((bf16[8,32,256]{2,1,0:T(8,128)(2,1)S(1)}, bf16[8,32,256]{2,1,0:T(8,128)(2,1)S(1)}, u32[]{:S(2)}, u32[]{:S(2)}) %collective-permute-start.1) | collective-permute-done | bytes 131104 | tf_op jit(solution)/shard_map/ppermute | solution.py:117
  63.0 0.0 collective-permute-done
  63.0 0.1 pad_maximum_fusion
  63.1 1.4 %gather_fusion = bf16[4,8,32,256]{3,2,1,0:T(8,128)(2,1)} fusion(bf16[4,8,32,256]{3,2,1,0:T(8,128)(2,1)S(1)} %pad_maximum_fusion, s32[1024]{0:T(1024)S(1)} %pad_clamp_fusion), kind=kCustom, calls=%fused_computation | custom fusion | bytes 1048592 | tf_op jit(solution)/shard_map/jit(_take)/gather | solution.py:120
  64.4 1.2 %gather.7 = bf16[4,8,8,4,2,128]{5,4,3,2,1,0:T(2,128)(2,1)S(1)} reshape(bf16[4,8,32,256]{3,2,1,0:T(8,128)(2,1)} %gather_fusion) | data formatting | bytes 1048576 | tf_op jit(solution)/shard_map/jit(_take)/gather | solution.py:120
  65.6 0.5 fusion.2
  66.1 0.3 copy.12
  66.5 1.1 %copy.15.lhs_ref = bf16[8,128,256]{2,1,0:T(8,128)(2,1)} copy(bf16[8,128,256]{1,0,2:T(8,128)(2,1)S(1)} %bitcast.29) | data formatting | bytes 1048576 | tf_op jit(solution)/shard_map/reshape;reshape | solution.py:123
  67.6 28.8 %all-to-all-done.1.rhs_ref = bf16[64,4,16,256]{3,2,1,0:T(8,128)(2,1)S(1)} async-done(((bf16[64,4,16,256]{3,2,1,0:T(8,128)(2,1)}), bf16[64,4,16,256]{3,2,1,0:T(8,128)(2,1)S(1)}, u32[]{:S(2)}, u32[]{:S(2)}) %all-to-all-start.1) | async-done | bytes 2097184 | tf_op jit(solution)/shard_map/all_to_all | solution.py:111
  96.4 3.4 %shard_map.38 = f32[4,8,2,128,128]{4,3,2,1,0:T(8,128)} custom-call(bf16[8,128,256]{2,1,0:T(8,128)(2,1)} %copy.15.lhs_ref, bf16[64,4,16,256]{3,2,1,0:T(8,128)(2,1)S(1)} %all-to-all-done.1.rhs_ref), custom_call_target="tpu_custom_call" | custom-call | flops 536870912 | bytes 6815744 | tf_op jit(solution)/shard_map/pallas_call | solution.py:41
  (4 shorter events, 0.1 us)
Async XLA Ops:
  0.0 1.1 %copy-start = (bf16[32,32,2,128]{3,2,1,0:T(2,128)(2,1)S(1)}, bf16[32,32,2,128]{3,2,1,0:T(2,128)(2,1)}, u32[]{:S(2)}) copy-start(bf16[32,32,2,128]{3,2,1,0:T(2,128)(2,1)} %param.3) | copy-start | bytes 1572868
  38.6 57.8 %all-to-all-start.1 = ((bf16[64,4,16,256]{3,2,1,0:T(8,128)(2,1)}), bf16[64,4,16,256]{3,2,1,0:T(8,128)(2,1)S(1)}, u32[]{:S(2)}, u32[]{:S(2)}) async-start(bf16[64,4,16,256]{3,2,1,0:T(8,128)(2,1)} %shard_map.37), calls=%async_computation.1 | async-start | bytes 4194304 | tf_op jit(solution)/shard_map/all_to_all | solution.py:111
  48.4 7.3 %collective-permute-start.2 = (bf16[8,32,256]{2,1,0:T(8,128)(2,1)S(1)}, bf16[8,32,256]{2,1,0:T(8,128)(2,1)S(1)}, u32[]{:S(2)}, u32[]{:S(2)}) collective-permute-start(bf16[8,32,256]{2,1,0:T(8,128)(2,1)S(1)} %get-tuple-element.6), channel_id=1, source_target_pairs={{0,3},{1,0},{2,1},{3,2},{4,7},{5,4},{6,5},{7,6},{8,11},{9,8},{10,9... | collective-permute-start | bytes 393224 | tf_op jit(solution)/shard_map/ppermute | solution.py:117
  48.5 14.4 %collective-permute-start.1 = (bf16[8,32,256]{2,1,0:T(8,128)(2,1)S(1)}, bf16[8,32,256]{2,1,0:T(8,128)(2,1)S(1)}, u32[]{:S(2)}, u32[]{:S(2)}) collective-permute-start(bf16[8,32,256]{2,1,0:T(8,128)(2,1)S(1)} %get-tuple-element.7), channel_id=1, source_target_pairs={{0,2},{1,3},{2,0},{3,1},{4,6},{5,7},{6,4},{7,5},{8,10},{9,11},{10,... | collective-permute-start | bytes 393224 | tf_op jit(solution)/shard_map/ppermute | solution.py:117
  49.3 13.7 %collective-permute-start = (bf16[8,32,256]{2,1,0:T(8,128)(2,1)S(1)}, bf16[8,32,256]{2,1,0:T(8,128)(2,1)S(1)}, u32[]{:S(2)}, u32[]{:S(2)}) collective-permute-start(bf16[8,32,256]{2,1,0:T(8,128)(2,1)S(1)} %get-tuple-element.8), channel_id=1, source_target_pairs={{0,1},{1,2},{2,3},{3,0},{4,5},{5,6},{6,7},{7,4},{8,9},{9,10},{10,1... | collective-permute-start | bytes 393224 | tf_op jit(solution)/shard_map/ppermute | solution.py:117

commit v20 on v19

--- a/solution.py
+++ b/solution.py
@@ -37,7 +37,7 @@
     two_chan = 2 * chan
     pieces, rounds, rows, _ = arrived.shape
     per_bin = pieces // bins
-    step_bins = 4
+    step_bins = 2
     return pl.pallas_call(
         functools.partial(cross_kernel, scale),
         grid=(bins // step_bins,),

time: 100 us -> 101 us (1.010)
  no operation moved by 1% of the time
where the time goes in v20:
time: 101 us
  waiting for transfers between devices  42.3 us (42%)
  blocking collectives  33.7 us (33%)
  local copies, waits for them, and re-layouts  8.5 us (8%)
  starting transfers between devices  8.07 us (8%)
  Pallas kernels  6.46 us (6%)
  other arithmetic  1.34 us (1%)
    all_to_all x1, blocking collectives, on_device(): lax.all_to_all(send, ('chan', 'seg'), split_axis=0, concat_axis=0, tiled=...  33.7 us
    all_to_all x1, waiting for transfers between devices, on_device(): lax.all_to_all(outgoing, 'chan', split_axis=0, concat_axis=0, tiled=True)  28.8 us
    ppermute x3, waiting for transfers between devices, on_device(): by_shift.append(lax.ppermute(part, 'seg', pairs))  13.5 us
    all_to_all x1, starting transfers between devices, on_device(): lax.all_to_all(outgoing, 'chan', split_axis=0, concat_axis=0, tiled=True)  7.06 us
    pallas_call x1, Pallas kernels, cross_spectra(): pl.pallas_call(functools.partial(cross_kernel, scale), grid=(bins // step...  4.37 us
    gather x2, local copies, waits for them, and re-layouts, on_device(): own = jnp.take(by_shift, order, axis=0)  2.54 us
    pallas_call x1, Pallas kernels, pick_partners(): pl.pallas_call(pick_kernel, in_specs=[pl.BlockSpec(memory_space=pltpu.SME...  2.09 us
  transfers between devices with their start and end apart: 4, of which 3 were waited for; matrix products, arithmetic and copies ran while one was open for 7% of the time, Pallas kernels for 0%

profile of v20, /device:TPU:2, one launch (start us, length us, event | category | flops | bytes accessed | tf_op | source)
XLA Modules:
  0.0 100.8 jit_solution(4415898410861388783)
XLA Ops:
  0.0 0.0 copy-start
  0.0 0.7 broadcast_subtract_fusion
  0.7 0.3 copy-done
  1.1 0.3 fusion
  1.4 0.5 copy.13
  1.9 0.3 reshape.70
  2.3 0.4 copy.14
  2.7 33.7 %all_to_all.10 = bf16[256,4,256]{2,1,0:T(4,128)(2,1)S(1)} all-to-all(bf16[256,4,256]{2,1,0:T(4,128)(2,1)S(1)} %bitcast.28), channel_id=1, replica_groups=mesh['chan'=64,'seg'=4] {'chan','seg'}, dimensions={0} | all-to-all | bytes 1048576 | tf_op jit(solution)/shard_map/all_to_all | solution.py:108
  36.3 0.1 reshape.72.held_ref
  36.5 2.1 %shard_map.37 = bf16[64,4,16,256]{3,2,1,0:T(8,128)(2,1)} custom-call(s32[4,64]{1,0:T(4,128)} %plan_ref.1, bf16[64,16,256]{2,1,0:T(8,128)(2,1)S(1)} %reshape.72.held_ref), custom_call_target="tpu_custom_call" | custom-call | bytes 4718592 | tf_op jit(solution)/shard_map/pallas_call | solution.py:76
  38.6 7.1 %all-to-all-start.1 = ((bf16[64,4,16,256]{3,2,1,0:T(8,128)(2,1)}), bf16[64,4,16,256]{3,2,1,0:T(8,128)(2,1)S(1)}, u32[]{:S(2)}, u32[]{:S(2)}) async-start(bf16[64,4,16,256]{3,2,1,0:T(8,128)(2,1)} %shard_map.37), calls=%async_computation.1 | async-start | bytes 4194304 | tf_op jit(solution)/shard_map/all_to_all | solution.py:111
  45.7 1.3 %copy.11 = bf16[32,32,2,128]{3,2,1,0:T(2,128)(2,1)} copy(bf16[32,32,2,128]{3,1,2,0:T(8,128)(2,1)S(1)} %fusion) | data formatting | bytes 1048576 | tf_op jit(solution)/shard_map/convert_element_type | solution.py:103
  47.0 1.4 %reshape.69 = bf16[4,8,32,256]{3,2,1,0:T(8,128)(2,1)S(1)} reshape(bf16[32,32,2,128]{3,2,1,0:T(2,128)(2,1)} %copy.11) | data formatting | bytes 1048576 | tf_op jit(solution)/shard_map/reshape | solution.py:112
  48.4 0.1 collective-permute-start.2
  48.5 0.8 collective-permute-start.1
  49.3 0.1 collective-permute-start
  49.5 6.3 %collective-permute-done.2 = bf16[8,32,256]{2,1,0:T(8,128)(2,1)S(1)} collective-permute-done((bf16[8,32,256]{2,1,0:T(8,128)(2,1)S(1)}, bf16[8,32,256]{2,1,0:T(8,128)(2,1)S(1)}, u32[]{:S(2)}, u32[]{:S(2)}) %collective-permute-start.2) | collective-permute-done | bytes 131104 | tf_op jit(solution)/shard_map/ppermute | solution.py:117
  55.8 7.2 %collective-permute-done.1 = bf16[8,32,256]{2,1,0:T(8,128)(2,1)S(1)} collective-permute-done((bf16[8,32,256]{2,1,0:T(8,128)(2,1)S(1)}, bf16[8,32,256]{2,1,0:T(8,128)(2,1)S(1)}, u32[]{:S(2)}, u32[]{:S(2)}) %collective-permute-start.1) | collective-permute-done | bytes 131104 | tf_op jit(solution)/shard_map/ppermute | solution.py:117
  63.0 0.0 collective-permute-done
  63.0 0.1 pad_maximum_fusion
  63.1 1.4 %gather_fusion = bf16[4,8,32,256]{3,2,1,0:T(8,128)(2,1)} fusion(bf16[4,8,32,256]{3,2,1,0:T(8,128)(2,1)S(1)} %pad_maximum_fusion, s32[1024]{0:T(1024)S(1)} %pad_clamp_fusion), kind=kCustom, calls=%fused_computation | custom fusion | bytes 1048592 | tf_op jit(solution)/shard_map/jit(_take)/gather | solution.py:120
  64.4 1.2 %gather.7 = bf16[4,8,8,4,2,128]{5,4,3,2,1,0:T(2,128)(2,1)S(1)} reshape(bf16[4,8,32,256]{3,2,1,0:T(8,128)(2,1)} %gather_fusion) | data formatting | bytes 1048576 | tf_op jit(solution)/shard_map/jit(_take)/gather | solution.py:120
  65.6 0.5 fusion.2
  66.1 0.3 copy.12
  66.5 1.1 %copy.15.lhs_ref = bf16[8,128,256]{2,1,0:T(8,128)(2,1)} copy(bf16[8,128,256]{1,0,2:T(8,128)(2,1)S(1)} %bitcast.29) | data formatting | bytes 1048576 | tf_op jit(solution)/shard_map/reshape;reshape | solution.py:123
  67.6 28.8 %all-to-all-done.1.rhs_ref = bf16[64,4,16,256]{3,2,1,0:T(8,128)(2,1)S(1)} async-done(((bf16[64,4,16,256]{3,2,1,0:T(8,128)(2,1)}), bf16[64,4,16,256]{3,2,1,0:T(8,128)(2,1)S(1)}, u32[]{:S(2)}, u32[]{:S(2)}) %all-to-all-start.1) | async-done | bytes 2097184 | tf_op jit(solution)/shard_map/all_to_all | solution.py:111
  96.4 4.4 %shard_map.38 = f32[4,8,2,128,128]{4,3,2,1,0:T(8,128)} custom-call(bf16[8,128,256]{2,1,0:T(8,128)(2,1)} %copy.15.lhs_ref, bf16[64,4,16,256]{3,2,1,0:T(8,128)(2,1)S(1)} %all-to-all-done.1.rhs_ref), custom_call_target="tpu_custom_call" | custom-call | flops 536870912 | bytes 6815744 | tf_op jit(solution)/shard_map/pallas_call | solution.py:41
  (4 shorter events, 0.1 us)
Async XLA Ops:
  0.0 1.1 %copy-start = (bf16[32,32,2,128]{3,2,1,0:T(2,128)(2,1)S(1)}, bf16[32,32,2,128]{3,2,1,0:T(2,128)(2,1)}, u32[]{:S(2)}) copy-start(bf16[32,32,2,128]{3,2,1,0:T(2,128)(2,1)} %param.3) | copy-start | bytes 1572868
  38.6 57.8 %all-to-all-start.1 = ((bf16[64,4,16,256]{3,2,1,0:T(8,128)(2,1)}), bf16[64,4,16,256]{3,2,1,0:T(8,128)(2,1)S(1)}, u32[]{:S(2)}, u32[]{:S(2)}) async-start(bf16[64,4,16,256]{3,2,1,0:T(8,128)(2,1)} %shard_map.37), calls=%async_computation.1 | async-start | bytes 4194304 | tf_op jit(solution)/shard_map/all_to_all | solution.py:111
  48.4 7.3 %collective-permute-start.2 = (bf16[8,32,256]{2,1,0:T(8,128)(2,1)S(1)}, bf16[8,32,256]{2,1,0:T(8,128)(2,1)S(1)}, u32[]{:S(2)}, u32[]{:S(2)}) collective-permute-start(bf16[8,32,256]{2,1,0:T(8,128)(2,1)S(1)} %get-tuple-element.6), channel_id=1, source_target_pairs={{0,3},{1,0},{2,1},{3,2},{4,7},{5,4},{6,5},{7,6},{8,11},{9,8},{10,9... | collective-permute-start | bytes 393224 | tf_op jit(solution)/shard_map/ppermute | solution.py:117
  48.5 14.4 %collective-permute-start.1 = (bf16[8,32,256]{2,1,0:T(8,128)(2,1)S(1)}, bf16[8,32,256]{2,1,0:T(8,128)(2,1)S(1)}, u32[]{:S(2)}, u32[]{:S(2)}) collective-permute-start(bf16[8,32,256]{2,1,0:T(8,128)(2,1)S(1)} %get-tuple-element.7), channel_id=1, source_target_pairs={{0,2},{1,3},{2,0},{3,1},{4,6},{5,7},{6,4},{7,5},{8,10},{9,11},{10,... | collective-permute-start | bytes 393224 | tf_op jit(solution)/shard_map/ppermute | solution.py:117
  49.3 13.7 %collective-permute-start = (bf16[8,32,256]{2,1,0:T(8,128)(2,1)S(1)}, bf16[8,32,256]{2,1,0:T(8,128)(2,1)S(1)}, u32[]{:S(2)}, u32[]{:S(2)}) collective-permute-start(bf16[8,32,256]{2,1,0:T(8,128)(2,1)S(1)} %get-tuple-element.8), channel_id=1, source_target_pairs={{0,1},{1,2},{2,3},{3,0},{4,5},{5,6},{6,7},{7,4},{8,9},{9,10},{10,1... | collective-permute-start | bytes 393224 | tf_op jit(solution)/shard_map/ppermute | solution.py:117
